TPU v7x, 512 devices: a whole 4x8x8 slice. The times are simulated.
512 devices in a mesh: seq: 16 (over y, core), exp: 32 (over z, x).
Axes of the slice: x: 4, y: 8, z: 8, core: 2. Of those that a mesh axis runs over, the one named last changes fastest.
Arguments:
- x_act: bfloat16 [32, 2048, 4096], P('exp', 'seq'), may hold values from -6 to 6
- dt_low: bfloat16 [32, 2048, 256], P('exp', 'seq'), may hold values from -6 to 6
- b_c: float32 [32, 2048, 32], P('exp', 'seq'), may hold values from -6 to 6
- w_dt: bfloat16 [256, 4096], replicated, may hold values from -0.375 to 0.375
- dt_bias: float32 [4096], replicated, may hold values from -6 to -1
- a_log: float32 [16, 4096], replicated, may hold values from -1 to 2
- d_skip: float32 [4096], replicated, may hold values from 0.5 to 1.5
- w_router: bfloat16 [16, 4096], replicated, may hold values from -0.09375 to 0.09375
- expert_ids: int32 [32, 2048, 2], P('exp', 'seq'), may hold values from 0 to 15, all different within a row; in each aligned block of 128 rows (0 to 127, 128 to 255, ..., all dimensions but the last counted through in order) at most 20 rows name the same one
- w_up: bfloat16 [32, 4096, 640], P('exp', 'seq'), may hold values from -0.09375 to 0.09375
- w_down: bfloat16 [32, 640, 4096], P('exp', None, 'seq'), may hold values from -0.15625 to 0.15625
Outputs:
- layer_out: bfloat16 [32, 2048, 4096], P('exp', 'seq')
Inputs may be any that keep to these rules, and one draw needn't show every extreme that they name: `expert_ids`: within the 128 tokens of one device (an aligned block), no expert is chosen by more than 20 tokens, and in some blocks one expert is chosen by exactly 20; a token's two experts differ.
All inputs are finite; a program needn't handle non-finite values.
Results may differ from a plain program's by a relative error of at most 0.011.
Values may be sent and summed in bfloat16 or wider, within the bound.
No kernel may reach another device: no remote copies, remote signals or barrier semaphores. Data moves between devices by JAX's collectives and lax.ppermute only.
A program may use at most 128 MiB of HBM per device.

v0:
```python
import jax
import jax.numpy as jnp
from jax import lax
from jax.sharding import PartitionSpec as P


def from_behind(value, axis, by):
    count = lax.axis_size(axis)
    pairs = [(i, i + by) for i in range(count) if 0 <= i + by < count]
    return lax.ppermute(value, axis, pairs)


def carry_in(decay_total, end_state):

    def relay(index, incoming):
        return from_behind(decay_total * incoming + end_state, "seq", 1)

    return lax.fori_loop(0, lax.axis_size("seq") - 1, relay, jnp.zeros_like(end_state))


def sweep(start_state, a_neg, delta, driven, b_in, c_out):
    tokens_here, channels = delta.shape
    nstate = b_in.shape[1]
    group = 8
    turns = tokens_here // group

    def advance(state, inputs):
        rate, drive, b_rows, c_rows = inputs
        results = []
        for inner in range(group):
            state = (
                jnp.exp(a_neg * rate[inner][None, :]) * state
                + drive[inner][None, :] * b_rows[inner][:, None]
            )
            results.append(jnp.sum(c_rows[inner][:, None] * state, axis=0))
        return (state, jnp.stack(results))

    inputs = (
        delta.reshape(turns, group, channels),
        driven.reshape(turns, group, channels),
        b_in.reshape(turns, group, nstate),
        c_out.reshape(turns, group, nstate),
    )
    final, results = lax.scan(advance, start_state, inputs)
    return (final, results.reshape(tokens_here, channels))


def per_device(
    x_act, dt_low, b_c, w_dt, dt_bias, a_log, d_skip, w_router, expert_ids, w_up, w_down
):
    tokens_here = x_act.shape[1]
    channels = x_act.shape[2]
    nstate = a_log.shape[0]
    xfloat = x_act[0].astype(jnp.float32)
    pre = jnp.dot(dt_low[0], w_dt, preferred_element_type=jnp.float32)
    delta = jax.nn.softplus(pre + dt_bias)
    a_neg = -jnp.exp(a_log)
    driven = delta * xfloat
    b_in = b_c[0, :, :nstate]
    c_out = b_c[0, :, nstate:]
    cumulated = jnp.cumsum(delta, axis=0)
    decay_total = jnp.exp(a_neg * cumulated[-1][None, :])
    pieces = max(1, channels // 512)
    span = channels // pieces
    ends = []
    for lower in range(0, channels, span):
        exponent = a_neg[None, :, lower : lower + span] * (
            cumulated[-1, lower : lower + span][None, None, :]
            - cumulated[:, None, lower : lower + span]
        )
        ends.append(
            jnp.sum(
                jnp.exp(exponent) * driven[:, None, lower : lower + span] * b_in[:, :, None], axis=0
            )
        )
    start = carry_in(decay_total, jnp.concatenate(ends, axis=1))
    _, scanned = sweep(start, a_neg, delta, driven, b_in, c_out)
    mixer = (scanned + d_skip * xfloat).astype(jnp.bfloat16)
    experts_count = w_router.shape[0]
    owners = lax.axis_size("exp")
    capacity = 5 * tokens_here // owners
    picks = expert_ids[0]
    logits = jnp.dot(mixer, w_router.T, preferred_element_type=jnp.float32)
    chosen = jnp.take_along_axis(logits, picks, axis=1)
    first = jax.nn.sigmoid(chosen[:, 0] - chosen[:, 1])
    second = 1.0 - first
    flat_ids = picks.reshape(-1)
    onehot = (flat_ids[:, None] == jnp.arange(experts_count, dtype=jnp.int32)[None, :]).astype(
        jnp.int32
    )
    position = jnp.sum(onehot * jnp.cumsum(onehot, axis=0), axis=1) - 1
    token_index = jnp.arange(2 * tokens_here, dtype=jnp.int32) // 2
    buffer = (
        jnp.zeros((experts_count, capacity, channels), jnp.bfloat16)
        .at[flat_ids, position]
        .set(mixer[token_index])
    )
    outgoing = jnp.repeat(buffer, 2, axis=0)
    incoming = lax.all_to_all(outgoing, "exp", split_axis=0, concat_axis=0, tiled=True)
    rows = incoming.reshape(-1, channels)
    pre_hidden = jnp.dot(
        rows, lax.all_gather(w_up, "seq", axis=1, tiled=True)[0], preferred_element_type=jnp.float32
    )
    hidden = jax.nn.silu(pre_hidden).astype(jnp.bfloat16)
    partial_out = lax.optimization_barrier(
        jnp.dot(
            hidden,
            lax.all_gather(w_down, "seq", axis=2, tiled=True)[0],
            preferred_element_type=jnp.float32,
        ).astype(jnp.bfloat16)
    )
    partial_out = partial_out.reshape(owners, capacity, channels)
    returned = lax.all_to_all(partial_out, "exp", split_axis=0, concat_axis=0, tiled=True)
    paired = returned.reshape(experts_count, 2, capacity, channels)
    combined = (paired[:, 0].astype(jnp.float32) + paired[:, 1].astype(jnp.float32)).astype(
        jnp.bfloat16
    )
    picked = combined[flat_ids, position].reshape(tokens_here, 2, channels).astype(jnp.float32)
    routed = first[:, None] * picked[:, 0] + second[:, None] * picked[:, 1]
    return (mixer.astype(jnp.float32) + routed).astype(jnp.bfloat16)[None]


def solution(mesh):
    in_specs = (
        P("exp", "seq", None),
        P("exp", "seq", None),
        P("exp", "seq", None),
        P(),
        P(),
        P(),
        P(),
        P(),
        P("exp", "seq", None),
        P("exp", "seq", None),
        P("exp", None, "seq"),
    )
    out_specs = P("exp", "seq", None)
    return jax.shard_map(
        per_device, mesh=mesh, in_specs=in_specs, out_specs=out_specs, check_vma=False
    )
```

profile of v0, /device:TPU:223, one launch (start us, length us, event | category | flops | bytes accessed | tf_op | source)
XLA Modules:
  0.0 714.3 jit_solution(18300772989486584227)
XLA Ops:
  8.1 4.8 fusion.4
  12.9 3.5 reduce_window_sum.26
  26.7 6.6 multiply_reduce_fusion.8
  33.4 139.8 %while.22 = (s32[]{:T(128)}, f32[16,4096]{1,0:T(8,128)S(1)}, f32[16,4096]{1,0:T(8,128)S(1)}, f32[16,4096]{1,0:T(8,128)S(1)}, s32[]{:T(128)}) while((s32[]{:T(128)}, f32[16,4096]{1,0:T(8,128)S(1)}, f32[16,4096]{1,0:T(8,128)S(1)}, f32[16,4096]{1,0:T(8,128)S(1)}, s32[]{:T(128)}) %tuple.132), condition=%wide.region_10.11_spmd, body=%wide.region_9.10_spmd.sunk | while | flops 131074 | bytes 2097253 | solution.py:18
  33.5 5.0 collective-permute-start
  38.5 8.8 %collective-permute-done = f32[16,4096]{1,0:T(8,128)S(1)} collective-permute-done((f32[16,4096]{1,0:T(8,128)S(1)}, f32[16,4096]{1,0:T(8,128)S(1)}, u32[]{:S(2)}, u32[]{:S(2)}) %collective-permute-start) | collective-permute-done | bytes 262176 | tf_op jit(solution)/shard_map/while/body/eval_jaxpr/ppermute | solution.py:10
  47.3 5.6 collective-permute-start
  52.9 4.0 collective-permute-done
  56.9 5.6 collective-permute-start
  62.6 3.3 collective-permute-done
  65.9 5.6 collective-permute-start
  71.5 3.3 collective-permute-done
  74.8 5.6 collective-permute-start
  80.4 3.3 collective-permute-done
  83.8 5.6 collective-permute-start
  89.4 3.3 collective-permute-done
  92.7 5.6 collective-permute-start
  98.3 3.3 collective-permute-done
  101.7 5.6 collective-permute-start
  107.3 3.3 collective-permute-done
  110.6 5.6 collective-permute-start
  119.6 5.6 collective-permute-start
  125.2 3.3 collective-permute-done
  128.5 5.6 collective-permute-start
  137.4 5.6 collective-permute-start
  143.1 3.3 collective-permute-done
  146.4 5.6 collective-permute-start
  152.0 3.3 collective-permute-done
  155.3 5.6 collective-permute-start
  160.9 3.3 collective-permute-done
  164.3 5.6 collective-permute-start
  169.9 3.3 collective-permute-done
  173.2 71.4 %while.23 = (s32[]{:T(128)}, f32[16,4096]{1,0:T(8,128)S(1)}, f32[16,8,4096]{2,1,0:T(8,128)}, f32[16,8,4096]{2,1,0:T(8,128)}, f32[16,4096]{1,0:T(8,128)S(1)}, /*i...) while((s32[]{:T(128)}, f32[16,4096]{1,0:T(8,128)S(1)}, ...), condition=%wide.region_20.21_spmd, body=%wide.region_11.20_spmd.sunk | while | flops 4685833 | bytes 3741845 | solution.py:44
  253.0 66.3 %scatter_fusion = bf16[16,20,4096]{2,0,1:T(8,128)(2,1)} fusion(bf16[16,20,4096]{2,0,1:T(8,128)(2,1)} %broadcast_in_dim.17, s32[256]{0:T(256)S(1)} %bitcast.211, bf16[256,4096]{1,0:T(8,128)(2,1)} %gather_fusion), kind=kCustom, calls=%fused_computation.3 | custom fusion | bytes 6293504 | tf_op jit(solution)/shard_map/scatter | solution.py:96
  322.6 3.4 broadcast_in_dim.18
  326.0 9.5 %all-to-all-start = ((bf16[32,20,4096]{2,1,0:T(8,128)(2,1)}), bf16[32,20,4096]{2,1,0:T(8,128)(2,1)}, u32[]{:S(2)}, u32[]{:S(2)}) async-start(bf16[32,20,4096]{2,1,0:T(8,128)(2,1)} %bitcast.209), calls=%async_computation | async-start | bytes 12582912 | tf_op jit(solution)/shard_map/all_to_all | solution.py:99
  336.3 133.5 %all-to-all-done = bf16[32,20,4096]{2,1,0:T(8,128)(2,1)} async-done(((bf16[32,20,4096]{2,1,0:T(8,128)(2,1)}), bf16[32,20,4096]{2,1,0:T(8,128)(2,1)}, u32[]{:S(2)}, u32[]{:S(2)}) %all-to-all-start) | async-done | bytes 5242912 | tf_op jit(solution)/shard_map/all_to_all | solution.py:99
  469.8 18.5 %reshape.407 = bf16[640,4096]{1,0:T(8,128)(2,1)} reshape(bf16[32,20,4096]{2,1,0:T(8,128)(2,1)} %all-to-all-done) | data formatting | bytes 10485760 | tf_op jit(solution)/shard_map/reshape | solution.py:100
  488.3 8.4 %multiply_convert_fusion = bf16[640,640]{1,0:T(8,128)(2,1)S(1)} fusion(bf16[640,4096]{1,0:T(8,128)(2,1)} %reshape.407, bf16[1,4096,640]{2,1,0:T(8,128)(2,1)} %all-gather.3.cloned.1.call-done), kind=kOutput, calls=%fused_computation.87 | convolution fusion | flops 3357491200 | bytes 11304960 | tf_op jit(solution)/shard_map/dot_general | solution.py:101
  496.7 8.6 %convolution_convert_fusion = bf16[640,4096]{1,0:T(8,128)(2,1)} fusion(bf16[640,640]{1,0:T(8,128)(2,1)S(1)} %multiply_convert_fusion, bf16[1,640,4096]{2,1,0:T(8,128)(2,1)} %all-gather.5.cloned.1.call-done), kind=kOutput, calls=%fused_computation.56 | convolution fusion | flops 3358064640 | bytes 11304960 | tf_op jit(solution)/shard_map/dot_general | solution.py:106
  505.3 7.7 %reshape.408 = bf16[32,20,4096]{2,1,0:T(8,128)(2,1)} reshape(bf16[640,4096]{1,0:T(8,128)(2,1)} %convolution_convert_fusion) | data formatting | bytes 10485760 | tf_op jit(solution)/shard_map/reshape | solution.py:112
  513.0 7.5 %all-to-all-start.1 = ((bf16[32,20,4096]{2,1,0:T(8,128)(2,1)}), bf16[32,20,4096]{2,1,0:T(8,128)(2,1)}, u32[]{:S(2)}, u32[]{:S(2)}) async-start(bf16[32,20,4096]{2,1,0:T(8,128)(2,1)} %reshape.408), calls=%async_computation.1 | async-start | bytes 12582912 | tf_op jit(solution)/shard_map/all_to_all | solution.py:113
  523.4 150.2 %all-to-all-done.1 = bf16[32,20,4096]{2,1,0:T(8,128)(2,1)} async-done(((bf16[32,20,4096]{2,1,0:T(8,128)(2,1)}), bf16[32,20,4096]{2,1,0:T(8,128)(2,1)}, u32[]{:S(2)}, u32[]{:S(2)}) %all-to-all-start.1) | async-done | bytes 5242912 | tf_op jit(solution)/shard_map/all_to_all | solution.py:113
  676.9 4.3 fusion.5
  681.2 7.2 %gather_fusion.1 = bf16[256,4096]{1,0:T(8,128)(2,1)} fusion(bf16[16,20,4096]{2,0,1:T(8,128)(2,1)} %fusion.5, s32[256]{0:T(256)S(1)} %bitcast.210), kind=kCustom, calls=%fused_computation.1 | custom fusion | bytes 4196352 | tf_op jit(solution)/shard_map/gather | solution.py:118
  688.4 5.4 reshape.411
  693.9 8.0 %fusion.32 = (f32[128,1,4096]{2,1,0:T(1,128)S(1)}, f32[128,1,4096]{2,1,0:T(1,128)S(1)}) fusion(f32[128,2,4096]{2,1,0:T(2,128)} %reshape.411), kind=kLoop, calls=%fused_computation.144 | loop fusion | bytes 8388608 | tf_op jit(solution)/shard_map/slice | solution.py:119
  701.9 5.3 fusion.13
  (241 shorter events, 108.1 us)
Async XLA Ops:
  6.5 1.6 copy-start
  6.5 481.8 %all-gather.3.cloned.1.call-start = ((), (), s32[]{:S(2)}) async-start(), calls=%async_computation.2 | async-start | bytes 5570560 | tf_op jit(solution)/shard_map/all_gather | solution.py:102
  12.9 4.9 copy-start.5
  16.4 1.4 copy-start.2
  16.4 4.6 copy-start.11
  21.1 5.4 copy-start.9
  21.1 2.6 copy-start.6
  26.6 6.7 copy-start.10
  33.5 13.8 %collective-permute-start = (f32[16,4096]{1,0:T(8,128)S(1)}, f32[16,4096]{1,0:T(8,128)S(1)}, u32[]{:S(2)}, u32[]{:S(2)}) collective-permute-start(f32[16,4096]{1,0:T(8,128)S(1)} %multiply_add_fusion.12), channel_id=1, source_target_pairs={{0,32},{32,64},{64,96},{96,128},{128,160},{160,192},{192,224},{224... | collective-permute-start | bytes 786440 | tf_op jit(solution)/shard_map/while/body/eval_jaxpr/ppermute | solution.py:10
  47.3 9.6 %collective-permute-start = (f32[16,4096]{1,0:T(8,128)S(1)}, f32[16,4096]{1,0:T(8,128)S(1)}, u32[]{:S(2)}, u32[]{:S(2)}) collective-permute-start(f32[16,4096]{1,0:T(8,128)S(1)} %multiply_add_fusion.12), channel_id=1, source_target_pairs={{0,32},{32,64},{64,96},{96,128},{128,160},{160,192},{192,224},{224... | collective-permute-start | bytes 786440 | tf_op jit(solution)/shard_map/while/body/eval_jaxpr/ppermute | solution.py:10
  56.9 8.9 %collective-permute-start = (f32[16,4096]{1,0:T(8,128)S(1)}, f32[16,4096]{1,0:T(8,128)S(1)}, u32[]{:S(2)}, u32[]{:S(2)}) collective-permute-start(f32[16,4096]{1,0:T(8,128)S(1)} %multiply_add_fusion.12), channel_id=1, source_target_pairs={{0,32},{32,64},{64,96},{96,128},{128,160},{160,192},{192,224},{224... | collective-permute-start | bytes 786440 | tf_op jit(solution)/shard_map/while/body/eval_jaxpr/ppermute | solution.py:10
  65.9 8.9 %collective-permute-start = (f32[16,4096]{1,0:T(8,128)S(1)}, f32[16,4096]{1,0:T(8,128)S(1)}, u32[]{:S(2)}, u32[]{:S(2)}) collective-permute-start(f32[16,4096]{1,0:T(8,128)S(1)} %multiply_add_fusion.12), channel_id=1, source_target_pairs={{0,32},{32,64},{64,96},{96,128},{128,160},{160,192},{192,224},{224... | collective-permute-start | bytes 786440 | tf_op jit(solution)/shard_map/while/body/eval_jaxpr/ppermute | solution.py:10
  74.8 8.9 %collective-permute-start = (f32[16,4096]{1,0:T(8,128)S(1)}, f32[16,4096]{1,0:T(8,128)S(1)}, u32[]{:S(2)}, u32[]{:S(2)}) collective-permute-start(f32[16,4096]{1,0:T(8,128)S(1)} %multiply_add_fusion.12), channel_id=1, source_target_pairs={{0,32},{32,64},{64,96},{96,128},{128,160},{160,192},{192,224},{224... | collective-permute-start | bytes 786440 | tf_op jit(solution)/shard_map/while/body/eval_jaxpr/ppermute | solution.py:10
  83.8 8.9 %collective-permute-start = (f32[16,4096]{1,0:T(8,128)S(1)}, f32[16,4096]{1,0:T(8,128)S(1)}, u32[]{:S(2)}, u32[]{:S(2)}) collective-permute-start(f32[16,4096]{1,0:T(8,128)S(1)} %multiply_add_fusion.12), channel_id=1, source_target_pairs={{0,32},{32,64},{64,96},{96,128},{128,160},{160,192},{192,224},{224... | collective-permute-start | bytes 786440 | tf_op jit(solution)/shard_map/while/body/eval_jaxpr/ppermute | solution.py:10
  92.7 8.9 %collective-permute-start = (f32[16,4096]{1,0:T(8,128)S(1)}, f32[16,4096]{1,0:T(8,128)S(1)}, u32[]{:S(2)}, u32[]{:S(2)}) collective-permute-start(f32[16,4096]{1,0:T(8,128)S(1)} %multiply_add_fusion.12), channel_id=1, source_target_pairs={{0,32},{32,64},{64,96},{96,128},{128,160},{160,192},{192,224},{224... | collective-permute-start | bytes 786440 | tf_op jit(solution)/shard_map/while/body/eval_jaxpr/ppermute | solution.py:10
  101.7 8.9 %collective-permute-start = (f32[16,4096]{1,0:T(8,128)S(1)}, f32[16,4096]{1,0:T(8,128)S(1)}, u32[]{:S(2)}, u32[]{:S(2)}) collective-permute-start(f32[16,4096]{1,0:T(8,128)S(1)} %multiply_add_fusion.12), channel_id=1, source_target_pairs={{0,32},{32,64},{64,96},{96,128},{128,160},{160,192},{192,224},{224... | collective-permute-start | bytes 786440 | tf_op jit(solution)/shard_map/while/body/eval_jaxpr/ppermute | solution.py:10
  110.6 8.9 %collective-permute-start = (f32[16,4096]{1,0:T(8,128)S(1)}, f32[16,4096]{1,0:T(8,128)S(1)}, u32[]{:S(2)}, u32[]{:S(2)}) collective-permute-start(f32[16,4096]{1,0:T(8,128)S(1)} %multiply_add_fusion.12), channel_id=1, source_target_pairs={{0,32},{32,64},{64,96},{96,128},{128,160},{160,192},{192,224},{224... | collective-permute-start | bytes 786440 | tf_op jit(solution)/shard_map/while/body/eval_jaxpr/ppermute | solution.py:10
  119.6 8.9 %collective-permute-start = (f32[16,4096]{1,0:T(8,128)S(1)}, f32[16,4096]{1,0:T(8,128)S(1)}, u32[]{:S(2)}, u32[]{:S(2)}) collective-permute-start(f32[16,4096]{1,0:T(8,128)S(1)} %multiply_add_fusion.12), channel_id=1, source_target_pairs={{0,32},{32,64},{64,96},{96,128},{128,160},{160,192},{192,224},{224... | collective-permute-start | bytes 786440 | tf_op jit(solution)/shard_map/while/body/eval_jaxpr/ppermute | solution.py:10
  128.5 8.9 %collective-permute-start = (f32[16,4096]{1,0:T(8,128)S(1)}, f32[16,4096]{1,0:T(8,128)S(1)}, u32[]{:S(2)}, u32[]{:S(2)}) collective-permute-start(f32[16,4096]{1,0:T(8,128)S(1)} %multiply_add_fusion.12), channel_id=1, source_target_pairs={{0,32},{32,64},{64,96},{96,128},{128,160},{160,192},{192,224},{224... | collective-permute-start | bytes 786440 | tf_op jit(solution)/shard_map/while/body/eval_jaxpr/ppermute | solution.py:10
  137.4 8.9 %collective-permute-start = (f32[16,4096]{1,0:T(8,128)S(1)}, f32[16,4096]{1,0:T(8,128)S(1)}, u32[]{:S(2)}, u32[]{:S(2)}) collective-permute-start(f32[16,4096]{1,0:T(8,128)S(1)} %multiply_add_fusion.12), channel_id=1, source_target_pairs={{0,32},{32,64},{64,96},{96,128},{128,160},{160,192},{192,224},{224... | collective-permute-start | bytes 786440 | tf_op jit(solution)/shard_map/while/body/eval_jaxpr/ppermute | solution.py:10
  146.4 8.9 %collective-permute-start = (f32[16,4096]{1,0:T(8,128)S(1)}, f32[16,4096]{1,0:T(8,128)S(1)}, u32[]{:S(2)}, u32[]{:S(2)}) collective-permute-start(f32[16,4096]{1,0:T(8,128)S(1)} %multiply_add_fusion.12), channel_id=1, source_target_pairs={{0,32},{32,64},{64,96},{96,128},{128,160},{160,192},{192,224},{224... | collective-permute-start | bytes 786440 | tf_op jit(solution)/shard_map/while/body/eval_jaxpr/ppermute | solution.py:10
  155.3 8.9 %collective-permute-start = (f32[16,4096]{1,0:T(8,128)S(1)}, f32[16,4096]{1,0:T(8,128)S(1)}, u32[]{:S(2)}, u32[]{:S(2)}) collective-permute-start(f32[16,4096]{1,0:T(8,128)S(1)} %multiply_add_fusion.12), channel_id=1, source_target_pairs={{0,32},{32,64},{64,96},{96,128},{128,160},{160,192},{192,224},{224... | collective-permute-start | bytes 786440 | tf_op jit(solution)/shard_map/while/body/eval_jaxpr/ppermute | solution.py:10
  164.3 8.9 %collective-permute-start = (f32[16,4096]{1,0:T(8,128)S(1)}, f32[16,4096]{1,0:T(8,128)S(1)}, u32[]{:S(2)}, u32[]{:S(2)}) collective-permute-start(f32[16,4096]{1,0:T(8,128)S(1)} %multiply_add_fusion.12), channel_id=1, source_target_pairs={{0,32},{32,64},{64,96},{96,128},{128,160},{160,192},{192,224},{224... | collective-permute-start | bytes 786440 | tf_op jit(solution)/shard_map/while/body/eval_jaxpr/ppermute | solution.py:10
  173.2 71.4 %copy-start.12 = (s32[1,128,2]{1,2,0:T(2,128)S(1)}, s32[1,128,2]{1,2,0:T(2,128)}, u32[]{:S(2)}) copy-start(s32[1,128,2]{1,2,0:T(2,128)} %param.23) | copy-start | bytes 3076
  173.2 72.8 %copy-start.4 = (bf16[1,128,4096]{2,1,0:T(8,128)(2,1)S(1)}, bf16[1,128,4096]{2,1,0:T(8,128)(2,1)}, u32[]{:S(2)}) copy-start(bf16[1,128,4096]{2,1,0:T(8,128)(2,1)} %param.15) | copy-start | bytes 3145732
  173.2 72.9 %copy-start.8 = (f32[4096]{0:T(1024)S(1)}, f32[4096]{0:T(1024)}, u32[]{:S(2)}) copy-start(f32[4096]{0:T(1024)} %param.21) | copy-start | bytes 49156
  326.0 143.8 %all-to-all-start = ((bf16[32,20,4096]{2,1,0:T(8,128)(2,1)}), bf16[32,20,4096]{2,1,0:T(8,128)(2,1)}, u32[]{:S(2)}, u32[]{:S(2)}) async-start(bf16[32,20,4096]{2,1,0:T(8,128)(2,1)} %bitcast.209), calls=%async_computation | async-start | bytes 12582912 | tf_op jit(solution)/shard_map/all_to_all | solution.py:99
  335.5 161.2 %all-gather.5.cloned.1.call-start = ((), (), s32[]{:S(2)}) async-start(), calls=%async_computation.3 | async-start | bytes 5570560 | tf_op jit(solution)/shard_map/all_gather | solution.py:108
  513.0 7.7 %copy-start.7 = (bf16[16,4096]{1,0:T(8,128)(2,1)S(1)}, bf16[16,4096]{1,0:T(8,128)(2,1)}, u32[]{:S(2)}) copy-start(bf16[16,4096]{1,0:T(8,128)(2,1)} %param.22) | copy-start | bytes 393220
  513.0 160.7 %all-to-all-start.1 = ((bf16[32,20,4096]{2,1,0:T(8,128)(2,1)}), bf16[32,20,4096]{2,1,0:T(8,128)(2,1)}, u32[]{:S(2)}, u32[]{:S(2)}) async-start(bf16[32,20,4096]{2,1,0:T(8,128)(2,1)} %reshape.408), calls=%async_computation.1 | async-start | bytes 12582912 | tf_op jit(solution)/shard_map/all_to_all | solution.py:113
  693.9 8.0 %copy-start.3 = (f32[16,8,4096]{2,1,0:T(8,128)S(1)}, f32[16,8,4096]{2,1,0:T(8,128)}, u32[]{:S(2)}) copy-start(f32[16,8,4096]{2,1,0:T(8,128)} %get-tuple-element.70) | copy-start | bytes 6291460
  701.9 5.3 copy-start.1
Sparse Core Ops, SparseCore 0:
  9.5 49.8 all-gather.2
  338.4 56.3 all-gather.4
where the time goes:
time: 720 us; the launch traced here: 714 us
  waiting for transfers between devices  341 us (47%)
  local copies, waits for them, and re-layouts  188 us (26%)
  starting transfers between devices  100 us (14%)
  other arithmetic  48 us (7%)
  matrix products  22.1 us (3%)
  between operations  13.9 us (2%)
    all_to_all x1, waiting for transfers between devices, per_device(): lax.all_to_all(partial_out, 'exp', split_axis=0, concat_axis=0, tiled=True)  150 us
    all_to_all x1, waiting for transfers between devices, per_device(): lax.all_to_all(outgoing, 'exp', split_axis=0, concat_axis=0, tiled=True)  134 us
    ppermute x15, starting transfers between devices, from_behind(): return lax.ppermute(value, axis, pairs)  83.4 us
    scatter x2, local copies, waits for them, and re-layouts, per_device(): buffer = jnp.zeros((experts_count, capacity, channels), jnp.bfloat16).at[...  69.5 us
    ppermute x15, waiting for transfers between devices, from_behind(): return lax.ppermute(value, axis, pairs)  55.6 us
    slice x16, local copies, waits for them, and re-layouts, advance(): drive[inner][None, :] * b_rows[inner][:, None]  36.8 us
    reduce_sum x48, other arithmetic, advance(): results.append(jnp.sum(c_rows[inner][:, None] * state, axis=0))  19.5 us
    reshape x1, local copies, waits for them, and re-layouts, per_device(): rows = incoming.reshape(-1, channels)  18.5 us
  transfers between devices with their start and end apart: 19, of which 17 were waited for; matrix products, arithmetic and copies ran while one was open for 29% of the time, Pallas kernels for 0%

commit v1 on v0

--- a/solution.py
+++ b/solution.py
@@ -10,12 +10,17 @@
     return lax.ppermute(value, axis, pairs)
 
 
-def carry_in(decay_total, end_state):
-
-    def relay(index, incoming):
-        return from_behind(decay_total * incoming + end_state, "seq", 1)
-
-    return lax.fori_loop(0, lax.axis_size("seq") - 1, relay, jnp.zeros_like(end_state))
+def carry_in(a_neg, total_delta, end_state):
+    count = lax.axis_size("seq")
+    packed = from_behind(jnp.concatenate([total_delta[None], end_state], axis=0), "seq", 1)
+    covered = 1
+    while covered < count - 1:
+        older = from_behind(packed, "seq", covered)
+        mine = packed[0]
+        state = jnp.exp(a_neg * mine[None, :]) * older[1:] + packed[1:]
+        packed = jnp.concatenate([(older[0] + mine)[None], state], axis=0)
+        covered *= 2
+    return packed[1:]
 
 
 def sweep(start_state, a_neg, delta, driven, b_in, c_out):
@@ -59,7 +64,6 @@
     b_in = b_c[0, :, :nstate]
     c_out = b_c[0, :, nstate:]
     cumulated = jnp.cumsum(delta, axis=0)
-    decay_total = jnp.exp(a_neg * cumulated[-1][None, :])
     pieces = max(1, channels // 512)
     span = channels // pieces
     ends = []
@@ -73,7 +77,7 @@
                 jnp.exp(exponent) * driven[:, None, lower : lower + span] * b_in[:, :, None], axis=0
             )
         )
-    start = carry_in(decay_total, jnp.concatenate(ends, axis=1))
+    start = carry_in(a_neg, cumulated[-1], jnp.concatenate(ends, axis=1))
     _, scanned = sweep(start, a_neg, delta, driven, b_in, c_out)
     mixer = (scanned + d_skip * xfloat).astype(jnp.bfloat16)
     experts_count = w_router.shape[0]
@@ -88,35 +92,39 @@
     onehot = (flat_ids[:, None] == jnp.arange(experts_count, dtype=jnp.int32)[None, :]).astype(
         jnp.int32
     )
-    position = jnp.sum(onehot * jnp.cumsum(onehot, axis=0), axis=1) - 1
-    token_index = jnp.arange(2 * tokens_here, dtype=jnp.int32) // 2
-    buffer = (
-        jnp.zeros((experts_count, capacity, channels), jnp.bfloat16)
-        .at[flat_ids, position]
-        .set(mixer[token_index])
-    )
-    outgoing = jnp.repeat(buffer, 2, axis=0)
+    position = (jnp.sum(onehot * jnp.cumsum(onehot, axis=0), axis=1) - 1).reshape(tokens_here, 2)
+    halves = owners // experts_count
+    dest = jnp.arange(owners, dtype=jnp.int32)[:, None, None] // halves
+    slot = jnp.arange(capacity, dtype=jnp.int32)[None, :, None]
+    hit = [
+        (dest == picks[None, None, :, c]) & (slot == position[None, None, :, c]) for c in range(2)
+    ]
+    dispatch = (hit[0] | hit[1]).astype(jnp.bfloat16)
+    outgoing = jnp.einsum(
+        "jst,tc->jsc", dispatch, mixer, preferred_element_type=jnp.float32
+    ).astype(jnp.bfloat16)
     incoming = lax.all_to_all(outgoing, "exp", split_axis=0, concat_axis=0, tiled=True)
-    rows = incoming.reshape(-1, channels)
-    pre_hidden = jnp.dot(
-        rows, lax.all_gather(w_up, "seq", axis=1, tiled=True)[0], preferred_element_type=jnp.float32
+    pre_hidden = jnp.einsum(
+        "jsc,ch->jsh",
+        incoming,
+        lax.all_gather(w_up, "seq", axis=1, tiled=True)[0],
+        preferred_element_type=jnp.float32,
     )
     hidden = jax.nn.silu(pre_hidden).astype(jnp.bfloat16)
     partial_out = lax.optimization_barrier(
-        jnp.dot(
+        jnp.einsum(
+            "jsh,hc->jsc",
             hidden,
             lax.all_gather(w_down, "seq", axis=2, tiled=True)[0],
             preferred_element_type=jnp.float32,
         ).astype(jnp.bfloat16)
     )
-    partial_out = partial_out.reshape(owners, capacity, channels)
     returned = lax.all_to_all(partial_out, "exp", split_axis=0, concat_axis=0, tiled=True)
-    paired = returned.reshape(experts_count, 2, capacity, channels)
-    combined = (paired[:, 0].astype(jnp.float32) + paired[:, 1].astype(jnp.float32)).astype(
-        jnp.bfloat16
-    )
-    picked = combined[flat_ids, position].reshape(tokens_here, 2, channels).astype(jnp.float32)
-    routed = first[:, None] * picked[:, 0] + second[:, None] * picked[:, 1]
+    gather = jnp.stack(hit).astype(jnp.bfloat16)
+    picked = jnp.einsum(
+        "kjst,jsc->ktc", gather, returned, preferred_element_type=jnp.float32
+    ).astype(jnp.bfloat16).astype(jnp.float32)
+    routed = first[:, None] * picked[0] + second[:, None] * picked[1]
     return (mixer.astype(jnp.float32) + routed).astype(jnp.bfloat16)[None]
 
 

time: 720 us -> 567 us (0.79)
  the two profiles are of different devices: /device:TPU:223 before, /device:TPU:47 now
where the time goes in v1:
time: 567 us; the launch traced here: 566 us
  waiting for transfers between devices  362 us (64%)
  local copies, waits for them, and re-layouts  72.9 us (13%)
  starting transfers between devices  48.6 us (9%)
  other arithmetic  37.5 us (7%)
  matrix products  30 us (5%)
  between operations  13.9 us (2%)
    all_to_all x1, waiting for transfers between devices, per_device(): lax.all_to_all(outgoing, 'exp', split_axis=0, concat_axis=0, tiled=True)  143 us
    all_to_all x1, waiting for transfers between devices, per_device(): lax.all_to_all(partial_out, 'exp', split_axis=0, concat_axis=0, tiled=True)  141 us
    ppermute x5, waiting for transfers between devices, from_behind(): return lax.ppermute(value, axis, pairs)  77.3 us
    slice x16, local copies, waits for them, and re-layouts, advance(): drive[inner][None, :] * b_rows[inner][:, None]  36.8 us
    all_to_all x1, starting transfers between devices, per_device(): lax.all_to_all(outgoing, 'exp', split_axis=0, concat_axis=0, tiled=True)  26.7 us
    reduce_sum x48, other arithmetic, advance(): results.append(jnp.sum(c_rows[inner][:, None] * state, axis=0))  19.5 us
    ppermute x5, starting transfers between devices, from_behind(): return lax.ppermute(value, axis, pairs)  13 us
  transfers between devices with their start and end apart: 9, of which 7 were waited for; matrix products, arithmetic and copies ran while one was open for 17% of the time, Pallas kernels for 0%

profile of v1, /device:TPU:47, one launch (start us, length us, event | category | flops | bytes accessed | tf_op | source)
XLA Modules:
  0.0 566.3 jit_solution(7532421831346907547)
XLA Ops:
  6.5 1.6 copy-done
  8.1 4.8 fusion.12
  12.9 3.5 reduce_window_sum.26
  17.7 2.7 fusion.51
  21.2 1.8 slice_subtract_fusion.2
  23.1 1.8 multiply_reduce_fusion.9
  24.9 5.5 multiply_reduce_fusion.8
  30.6 2.9 collective-permute-start
  33.4 0.8 copy.46
  34.4 3.7 collective-permute-done
  38.1 4.4 collective-permute-start.1
  43.6 3.6 collective-permute-done.1
  47.4 2.3 collective-permute-start.2
  50.0 13.9 %collective-permute-done.2 = f32[17,4096]{1,0:T(8,128)S(1)} collective-permute-done((f32[17,4096]{1,0:T(8,128)S(1)}, f32[17,4096]{1,0:T(8,128)S(1)}, u32[]{:S(2)}, u32[]{:S(2)}) %collective-permute-start.2) | collective-permute-done | bytes 278560 | tf_op jit(solution)/shard_map/ppermute | solution.py:10
  64.1 2.0 collective-permute-start.3
  66.3 33.7 %collective-permute-done.3 = f32[17,4096]{1,0:T(8,128)S(1)} collective-permute-done((f32[17,4096]{1,0:T(8,128)S(1)}, f32[17,4096]{1,0:T(8,128)S(1)}, u32[]{:S(2)}, u32[]{:S(2)}) %collective-permute-start.3) | collective-permute-done | bytes 278560 | tf_op jit(solution)/shard_map/ppermute | solution.py:10
  100.2 1.5 collective-permute-start.4
  102.0 22.3 %collective-permute-done.4 = f32[17,4096]{1,0:T(8,128)S(1)} collective-permute-done((f32[17,4096]{1,0:T(8,128)S(1)}, f32[17,4096]{1,0:T(8,128)S(1)}, u32[]{:S(2)}, u32[]{:S(2)}) %collective-permute-start.4) | collective-permute-done | bytes 278560 | tf_op jit(solution)/shard_map/ppermute | solution.py:10
  124.4 71.5 %while.12 = (s32[]{:T(128)}, f32[16,4096]{1,0:T(8,128)S(1)}, f32[16,8,4096]{2,1,0:T(8,128)}, f32[16,8,4096]{2,1,0:T(8,128)}, f32[16,4096]{1,0:T(8,128)S(1)}, /*i...) while((s32[]{:T(128)}, f32[16,4096]{1,0:T(8,128)S(1)}, ...), condition=%wide.region_18.19_spmd, body=%wide.region_9.18_spmd.sunk | while | flops 4685833 | bytes 3741845 | solution.py:49
  124.5 2.2 constant_dynamic-slice_fusion.21
  128.8 2.6 constant_dynamic-slice_fusion.21
  133.5 2.3 constant_dynamic-slice_fusion.21
  138.0 2.3 constant_dynamic-slice_fusion.21
  142.4 2.3 constant_dynamic-slice_fusion.21
  146.9 2.3 constant_dynamic-slice_fusion.21
  151.3 2.3 constant_dynamic-slice_fusion.21
  155.8 2.3 constant_dynamic-slice_fusion.21
  160.3 2.4 constant_dynamic-slice_fusion.21
  164.8 2.3 constant_dynamic-slice_fusion.21
  169.3 2.4 constant_dynamic-slice_fusion.21
  173.8 2.1 constant_dynamic-slice_fusion.21
  178.0 2.3 constant_dynamic-slice_fusion.21
  182.5 2.3 constant_dynamic-slice_fusion.21
  186.9 2.3 constant_dynamic-slice_fusion.21
  191.4 2.4 constant_dynamic-slice_fusion.21
  195.9 1.9 fusion.14
  197.8 1.5 convolution_convert_fusion.1
  199.3 5.6 copy.51
  204.9 26.7 %all-to-all-start = ((bf16[32,20,4096]{2,1,0:T(8,128)(2,1)}), bf16[32,20,4096]{2,1,0:T(8,128)(2,1)}, u32[]{:S(2)}, u32[]{:S(2)}) async-start(bf16[32,20,4096]{2,1,0:T(8,128)(2,1)} %copy.51), calls=%async_computation | async-start | bytes 12582912 | tf_op jit(solution)/shard_map/all_to_all | solution.py:106
  232.4 143.5 %all-to-all-done = bf16[32,20,4096]{2,1,0:T(8,128)(2,1)} async-done(((bf16[32,20,4096]{2,1,0:T(8,128)(2,1)}), bf16[32,20,4096]{2,1,0:T(8,128)(2,1)}, u32[]{:S(2)}, u32[]{:S(2)}) %all-to-all-start) | async-done | bytes 5242912 | tf_op jit(solution)/shard_map/all_to_all | solution.py:106
  375.8 9.6 %multiply_convert_fusion = bf16[32,20,640]{2,1,0:T(8,128)(2,1)} fusion(bf16[32,20,4096]{2,1,0:T(8,128)(2,1)} %all-to-all-done, bf16[1,4096,640]{2,1,0:T(8,128)(2,1)} %all-gather.3.cloned.1.call-done), kind=kOutput, calls=%fused_computation.85 | convolution fusion | flops 3357491200 | bytes 11304960 | tf_op jit(solution)/shard_map/jsc,ch->jsh/dot_general | solution.py:107
  385.5 7.0 %convolution_convert_fusion = bf16[32,20,4096]{2,0,1:T(8,128)(2,1)S(1)} fusion(bf16[1,640,4096]{2,1,0:T(8,128)(2,1)} %all-gather.5.cloned.1.call-done, bf16[32,20,640]{2,1,0:T(8,128)(2,1)} %multiply_convert_fusion), kind=kOutput, calls=%fused_computation.52 | convolution fusion | flops 3358064640 | bytes 11304960 | tf_op jit(solution)/shard_map/jsh,hc->jsc/dot_general | solution.py:115
  392.5 5.6 copy.53
  398.1 8.6 %all-to-all-start.1 = ((bf16[32,20,4096]{2,1,0:T(8,128)(2,1)}), bf16[32,20,4096]{2,1,0:T(8,128)(2,1)}, u32[]{:S(2)}, u32[]{:S(2)}) async-start(bf16[32,20,4096]{2,1,0:T(8,128)(2,1)} %copy.53), calls=%async_computation.1 | async-start | bytes 12582912 | tf_op jit(solution)/shard_map/all_to_all | solution.py:122
  407.5 2.0 gather_fusion
  409.8 141.0 %all-to-all-done.1 = bf16[32,20,4096]{2,1,0:T(8,128)(2,1)} async-done(((bf16[32,20,4096]{2,1,0:T(8,128)(2,1)}), bf16[32,20,4096]{2,1,0:T(8,128)(2,1)}, u32[]{:S(2)}, u32[]{:S(2)}) %all-to-all-start.1) | async-done | bytes 5242912 | tf_op jit(solution)/shard_map/all_to_all | solution.py:122
  550.9 6.7 %fusion.8 = f32[2,128,4096]{2,1,0:T(8,128)S(1)} fusion(bf16[32,20,4096]{2,1,0:T(8,128)(2,1)} %all-to-all-done.1, pred[1,32,20,128]{3,1,2,0:T(32,128)(4,1)S(1)} %broadcast_and_fusion, pred[1,32,20,128]{3,1,2,0:T(32,128)(4,1)S(1)} %broadcast_and_fusion.1), kind=kOutput, calls=%fused_computation.62 | convolution fusion | flops 1344438272 | bytes 9601024 | tf_op jit(solution)/shard_map/kjst,jsc->ktc/dot_general | solution.py:124
  557.6 1.8 fusion.19
  (217 shorter events, 40.3 us)
Async XLA Ops:
  6.5 1.6 copy-start
  6.5 225.8 %all-gather.3.cloned.1.call-start = ((), (), s32[]{:S(2)}) async-start(), calls=%async_computation.2 | async-start | bytes 5570560 | tf_op jit(solution)/shard_map/all_gather | solution.py:110
  12.9 7.5 %copy-start.4 = (f32[16,4096]{1,0:T(8,128)S(1)}, f32[16,4096]{1,0:T(8,128)}, u32[]{:S(2)}) copy-start(f32[16,4096]{1,0:T(8,128)} %param.18) | copy-start | bytes 786436
  16.4 1.4 copy-start.2
  16.4 4.1 copy-start.14
  20.4 2.6 copy-start.8
  21.1 3.8 copy-start.6
  21.1 3.8 copy-start.7
  21.2 1.9 copy-start.9
  30.4 71.3 %copy-start.13 = (f32[1,128,16]{1,2,0:T(8,128)S(1)}, f32[1,128,16]{1,2,0:T(8,128)}, u32[]{:S(2)}) copy-start(f32[1,128,16]{1,2,0:T(8,128)} %get-tuple-element.166) | copy-start | bytes 24580
  30.4 71.4 %copy-start.12 = (f32[1,128,16]{1,2,0:T(8,128)S(1)}, f32[1,128,16]{1,2,0:T(8,128)}, u32[]{:S(2)}) copy-start(f32[1,128,16]{1,2,0:T(8,128)} %get-tuple-element.164) | copy-start | bytes 24580
  30.6 7.6 %collective-permute-start = (f32[17,4096]{1,0:T(8,128)S(1)}, f32[17,4096]{1,0:T(8,128)S(1)}, u32[]{:S(2)}, u32[]{:S(2)}) collective-permute-start(f32[17,4096]{1,0:T(8,128)S(1)} %pad_maximum_fusion), channel_id=1, source_target_pairs={{0,32},{32,64},{64,96},{96,128},{128,160},{160,192},{192,224},{224... | collective-permute-start | bytes 835592 | tf_op jit(solution)/shard_map/ppermute | solution.py:10
  38.1 9.1 %collective-permute-start.1 = (f32[17,4096]{1,0:T(8,128)S(1)}, f32[17,4096]{1,0:T(8,128)S(1)}, u32[]{:S(2)}, u32[]{:S(2)}) collective-permute-start(f32[17,4096]{1,0:T(8,128)S(1)} %collective-permute-done), channel_id=1, source_target_pairs={{0,32},{32,64},{64,96},{96,128},{128,160},{160,192},{192,224},{224... | collective-permute-start | bytes 835592 | tf_op jit(solution)/shard_map/ppermute | solution.py:10
  47.4 16.5 %collective-permute-start.2 = (f32[17,4096]{1,0:T(8,128)S(1)}, f32[17,4096]{1,0:T(8,128)S(1)}, u32[]{:S(2)}, u32[]{:S(2)}) collective-permute-start(f32[17,4096]{1,0:T(8,128)S(1)} %pad_maximum_fusion.1), channel_id=1, source_target_pairs={{0,64},{32,96},{64,128},{96,160},{128,192},{160,224},{192,256},{22... | collective-permute-start | bytes 835592 | tf_op jit(solution)/shard_map/ppermute | solution.py:10
  64.1 35.9 %collective-permute-start.3 = (f32[17,4096]{1,0:T(8,128)S(1)}, f32[17,4096]{1,0:T(8,128)S(1)}, u32[]{:S(2)}, u32[]{:S(2)}) collective-permute-start(f32[17,4096]{1,0:T(8,128)S(1)} %pad_maximum_fusion.2), channel_id=1, source_target_pairs={{0,128},{32,160},{64,192},{96,224},{128,256},{160,288},{192,320},{... | collective-permute-start | bytes 835592 | tf_op jit(solution)/shard_map/ppermute | solution.py:10
  100.2 24.1 %collective-permute-start.4 = (f32[17,4096]{1,0:T(8,128)S(1)}, f32[17,4096]{1,0:T(8,128)S(1)}, u32[]{:S(2)}, u32[]{:S(2)}) collective-permute-start(f32[17,4096]{1,0:T(8,128)S(1)} %pad_maximum_fusion.3), channel_id=1, source_target_pairs={{0,256},{32,288},{64,320},{96,352},{128,384},{160,416},{192,448},{... | collective-permute-start | bytes 835592 | tf_op jit(solution)/shard_map/ppermute | solution.py:10
  124.4 71.5 %copy-start.5 = (bf16[1,128,4096]{2,1,0:T(8,128)(2,1)S(1)}, bf16[1,128,4096]{2,1,0:T(8,128)(2,1)}, u32[]{:S(2)}) copy-start(bf16[1,128,4096]{2,1,0:T(8,128)(2,1)} %param.13) | copy-start | bytes 3145732
  124.4 71.5 %copy-start.11 = (f32[4096]{0:T(1024)S(1)}, f32[4096]{0:T(1024)}, u32[]{:S(2)}) copy-start(f32[4096]{0:T(1024)} %param.19) | copy-start | bytes 49156
  204.9 171.0 %all-to-all-start = ((bf16[32,20,4096]{2,1,0:T(8,128)(2,1)}), bf16[32,20,4096]{2,1,0:T(8,128)(2,1)}, u32[]{:S(2)}, u32[]{:S(2)}) async-start(bf16[32,20,4096]{2,1,0:T(8,128)(2,1)} %copy.51), calls=%async_computation | async-start | bytes 12582912 | tf_op jit(solution)/shard_map/all_to_all | solution.py:106
  231.6 153.9 %all-gather.5.cloned.1.call-start = ((), (), s32[]{:S(2)}) async-start(), calls=%async_computation.3 | async-start | bytes 5570560 | tf_op jit(solution)/shard_map/all_gather | solution.py:118
  398.1 8.6 %copy-start.15 = (s32[1,128,2]{1,2,0:T(2,128)S(1)}, s32[1,128,2]{1,2,0:T(2,128)}, u32[]{:S(2)}) copy-start(s32[1,128,2]{1,2,0:T(2,128)} %param.21) | copy-start | bytes 3076
  398.1 9.0 %copy-start.10 = (bf16[16,4096]{1,0:T(8,128)(2,1)S(1)}, bf16[16,4096]{1,0:T(8,128)(2,1)}, u32[]{:S(2)}) copy-start(bf16[16,4096]{1,0:T(8,128)(2,1)} %param.20) | copy-start | bytes 393220
  398.1 152.8 %all-to-all-start.1 = ((bf16[32,20,4096]{2,1,0:T(8,128)(2,1)}), bf16[32,20,4096]{2,1,0:T(8,128)(2,1)}, u32[]{:S(2)}, u32[]{:S(2)}) async-start(bf16[32,20,4096]{2,1,0:T(8,128)(2,1)} %copy.53), calls=%async_computation.1 | async-start | bytes 12582912 | tf_op jit(solution)/shard_map/all_to_all | solution.py:122
  550.9 6.8 %copy-start.3 = (f32[16,8,4096]{2,1,0:T(8,128)S(1)}, f32[16,8,4096]{2,1,0:T(8,128)}, u32[]{:S(2)}) copy-start(f32[16,8,4096]{2,1,0:T(8,128)} %get-tuple-element.47) | copy-start | bytes 6291460
  557.6 1.8 copy-start.1
Sparse Core Ops, SparseCore 0:
  33.6 69.8 all-gather.2
  234.5 53.3 all-gather.4

commit v2 on v1

--- a/solution.py
+++ b/solution.py
@@ -26,7 +26,7 @@
 def sweep(start_state, a_neg, delta, driven, b_in, c_out):
     tokens_here, channels = delta.shape
     nstate = b_in.shape[1]
-    group = 8
+    group = 32
     turns = tokens_here // group
 
     def advance(state, inputs):
@@ -78,6 +78,7 @@
             )
         )
     start = carry_in(a_neg, cumulated[-1], jnp.concatenate(ends, axis=1))
+    start, w_up, w_down = lax.optimization_barrier((start, w_up, w_down))
     _, scanned = sweep(start, a_neg, delta, driven, b_in, c_out)
     mixer = (scanned + d_skip * xfloat).astype(jnp.bfloat16)
     experts_count = w_router.shape[0]

time: 567 us -> 580 us (1.023); the launches traced: 566 us -> 571 us
  local copies, waits for them, and re-layouts: 72.9 us -> 89.9 us
  waiting for transfers between devices: 362 us -> 349 us
  starting transfers between devices: 48.6 us -> 36.5 us
  other arithmetic: 37.5 us -> 48.2 us
    slice x1 -> x9, local copies, waits for them, and re-layouts: 0.18 us -> 18.2 us  [the longest x8 18 us: advance(): rate[inner][None, :]]
    slice x16 -> x8, local copies, waits for them, and re-layouts: 36.8 us -> 20.5 us  [advance(): drive[inner][None, :] * b_rows[inner][:, None]]
    all_to_all x1, starting transfers between devices: 26.7 us -> 12.9 us  [per_device(): lax.all_to_all(outgoing, 'exp', split_axis=0, concat_axis=0, tiled=True)]
    ppermute x5, waiting for transfers between devices: 77.3 us -> 64.3 us  [from_behind(): return lax.ppermute(value, axis, pairs)]
    mul x16 -> x8, local copies, waits for them, and re-layouts: 0.13 us -> 11.3 us  [advance(): drive[inner][None, :] * b_rows[inner][:, None]]
    reduce_sum x48 -> x36, other arithmetic: 19.5 us -> 27.5 us  [advance(): results.append(jnp.sum(c_rows[inner][:, None] * state, axis=0))]
    dynamic_update_slice x16 -> x4, local copies, waits for them, and re-layouts: 10.6 us -> 3.39 us  [sweep(): final, results = lax.scan(advance, start_state, inputs)]
    mul x16 -> x4, local copies, waits for them, and re-layouts: 0.13 us -> 6.91 us  [advance(): results.append(jnp.sum(c_rows[inner][:, None] * state, axis=0))]
  transfers between devices with their start and end apart: 9 -> 9, of which waited for: 7 -> 7; matrix products, arithmetic and copies ran while one was open for 17% -> 21% of each run, Pallas kernels for 0% -> 0%
where the time goes in v2:
time: 580 us; the launch traced here: 571 us
  waiting for transfers between devices  349 us (60%)
  local copies, waits for them, and re-layouts  89.9 us (16%)
  other arithmetic  48.2 us (8%)
  starting transfers between devices  36.5 us (6%)
  matrix products  30.2 us (5%)
  between operations  14.3 us (2%)
    all_to_all x1, waiting for transfers between devices, per_device(): lax.all_to_all(outgoing, 'exp', split_axis=0, concat_axis=0, tiled=True)  144 us
    all_to_all x1, waiting for transfers between devices, per_device(): lax.all_to_all(partial_out, 'exp', split_axis=0, concat_axis=0, tiled=True)  141 us
    ppermute x5, waiting for transfers between devices, from_behind(): return lax.ppermute(value, axis, pairs)  64.3 us
    reduce_sum x36, other arithmetic, advance(): results.append(jnp.sum(c_rows[inner][:, None] * state, axis=0))  27.5 us
    slice x8, local copies, waits for them, and re-layouts, advance(): drive[inner][None, :] * b_rows[inner][:, None]  20.5 us
    slice x8, local copies, waits for them, and re-layouts, advance(): rate[inner][None, :]  18 us
    ppermute x5, starting transfers between devices, from_behind(): return lax.ppermute(value, axis, pairs)  14.6 us
    all_to_all x1, starting transfers between devices, per_device(): lax.all_to_all(outgoing, 'exp', split_axis=0, concat_axis=0, tiled=True)  12.9 us
  transfers between devices with their start and end apart: 9, of which 7 were waited for; matrix products, arithmetic and copies ran while one was open for 21% of the time, Pallas kernels for 0%

profile of v2, /device:TPU:47, one launch (start us, length us, event | category | flops | bytes accessed | tf_op | source)
XLA Modules:
  0.0 571.1 jit_solution(7723402049467722093)
XLA Ops:
  8.1 4.8 fusion.76
  12.9 4.8 reduce_window_sum.26
  22.7 1.9 slice_subtract_fusion.2
  26.5 5.5 multiply_reduce_fusion.32
  32.2 2.9 collective-permute-start
  36.0 3.8 collective-permute-done
  39.7 4.4 collective-permute-start.1
  45.2 3.6 collective-permute-done.1
  49.0 2.3 collective-permute-start.2
  51.7 5.9 %collective-permute-done.2 = f32[17,4096]{1,0:T(8,128)S(1)} collective-permute-done((f32[17,4096]{1,0:T(8,128)S(1)}, f32[17,4096]{1,0:T(8,128)S(1)}, u32[]{:S(2)}, u32[]{:S(2)}) %collective-permute-start.2) | collective-permute-done | bytes 278560 | tf_op jit(solution)/shard_map/ppermute | solution.py:10
  57.7 3.4 collective-permute-start.3
  61.9 31.3 %collective-permute-done.3 = f32[17,4096]{1,0:T(8,128)S(1)} collective-permute-done((f32[17,4096]{1,0:T(8,128)S(1)}, f32[17,4096]{1,0:T(8,128)S(1)}, u32[]{:S(2)}, u32[]{:S(2)}) %collective-permute-start.3) | collective-permute-done | bytes 278560 | tf_op jit(solution)/shard_map/ppermute | solution.py:10
  97.2 19.7 %collective-permute-done.4 = f32[17,4096]{1,0:T(8,128)S(1)} collective-permute-done((f32[17,4096]{1,0:T(8,128)S(1)}, f32[17,4096]{1,0:T(8,128)S(1)}, u32[]{:S(2)}, u32[]{:S(2)}) %collective-permute-start.4) | collective-permute-done | bytes 278560 | tf_op jit(solution)/shard_map/ppermute | solution.py:10
  117.0 96.8 %while.12 = (s32[]{:T(128)}, f32[16,4096]{1,0:T(8,128)S(1)}, f32[4,32,4096]{2,1,0:T(8,128)}, f32[4,32,4096]{2,1,0:T(8,128)}, f32[16,4096]{1,0:T(8,128)S(1)}, /*i...) while((s32[]{:T(128)}, f32[16,4096]{1,0:T(8,128)S(1)}, ...), condition=%wide.region_42.43_spmd, body=%wide.region_9.42_spmd.sunk | while | flops 18743328 | bytes 13393673 | solution.py:49
  117.0 3.0 constant_dynamic-slice_fusion.133
  120.0 1.7 fusion.127
  121.8 1.8 fusion.128
  125.0 2.2 constant_dynamic-slice_fusion.135
  127.2 2.1 constant_dynamic-slice_fusion.132
  129.6 2.1 constant_dynamic-slice_fusion.134
  131.7 4.0 multiply_reduce_fusion.49
  140.9 3.0 constant_dynamic-slice_fusion.133
  148.8 2.5 constant_dynamic-slice_fusion.135
  151.3 2.1 constant_dynamic-slice_fusion.132
  153.8 2.2 constant_dynamic-slice_fusion.134
  156.0 4.0 multiply_reduce_fusion.49
  165.2 3.0 constant_dynamic-slice_fusion.133
  173.0 2.4 constant_dynamic-slice_fusion.135
  175.4 2.1 constant_dynamic-slice_fusion.132
  177.9 2.1 constant_dynamic-slice_fusion.134
  180.1 4.0 multiply_reduce_fusion.49
  189.3 3.0 constant_dynamic-slice_fusion.133
  197.1 2.3 constant_dynamic-slice_fusion.135
  199.4 2.1 constant_dynamic-slice_fusion.132
  201.9 2.2 constant_dynamic-slice_fusion.134
  204.0 4.0 multiply_reduce_fusion.49
  213.8 1.9 fusion.78
  217.2 5.6 copy.51
  222.8 12.9 %all-to-all-start = ((bf16[32,20,4096]{2,1,0:T(8,128)(2,1)}), bf16[32,20,4096]{2,1,0:T(8,128)(2,1)}, u32[]{:S(2)}, u32[]{:S(2)}) async-start(bf16[32,20,4096]{2,1,0:T(8,128)(2,1)} %copy.51), calls=%async_computation | async-start | bytes 12582912 | tf_op jit(solution)/shard_map/all_to_all | solution.py:107
  236.5 143.5 %all-to-all-done = bf16[32,20,4096]{2,1,0:T(8,128)(2,1)} async-done(((bf16[32,20,4096]{2,1,0:T(8,128)(2,1)}), bf16[32,20,4096]{2,1,0:T(8,128)(2,1)}, u32[]{:S(2)}, u32[]{:S(2)}) %all-to-all-start) | async-done | bytes 5242912 | tf_op jit(solution)/shard_map/all_to_all | solution.py:107
  380.0 9.8 %multiply_convert_fusion = bf16[32,20,640]{2,1,0:T(8,128)(2,1)} fusion(bf16[32,20,4096]{2,1,0:T(8,128)(2,1)} %all-to-all-done, bf16[1,4096,640]{2,1,0:T(8,128)(2,1)} %all-gather.3.cloned.1.call-done), kind=kOutput, calls=%fused_computation.291 | convolution fusion | flops 3357491200 | bytes 11304960 | tf_op jit(solution)/shard_map/jsc,ch->jsh/dot_general | solution.py:108
  389.8 7.0 %convolution_convert_fusion = bf16[32,20,4096]{2,0,1:T(8,128)(2,1)S(1)} fusion(bf16[1,640,4096]{2,1,0:T(8,128)(2,1)} %all-gather.5.cloned.1.call-done, bf16[32,20,640]{2,1,0:T(8,128)(2,1)} %multiply_convert_fusion), kind=kOutput, calls=%fused_computation.258 | convolution fusion | flops 3358064640 | bytes 11304960 | tf_op jit(solution)/shard_map/jsh,hc->jsc/dot_general | solution.py:116
  396.8 5.6 copy.53
  402.4 9.0 %all-to-all-start.1 = ((bf16[32,20,4096]{2,1,0:T(8,128)(2,1)}), bf16[32,20,4096]{2,1,0:T(8,128)(2,1)}, u32[]{:S(2)}, u32[]{:S(2)}) async-start(bf16[32,20,4096]{2,1,0:T(8,128)(2,1)} %copy.53), calls=%async_computation.1 | async-start | bytes 12582912 | tf_op jit(solution)/shard_map/all_to_all | solution.py:123
  412.1 2.0 gather_fusion
  414.5 140.9 %all-to-all-done.1 = bf16[32,20,4096]{2,1,0:T(8,128)(2,1)} async-done(((bf16[32,20,4096]{2,1,0:T(8,128)(2,1)}), bf16[32,20,4096]{2,1,0:T(8,128)(2,1)}, u32[]{:S(2)}, u32[]{:S(2)}) %all-to-all-start.1) | async-done | bytes 5242912 | tf_op jit(solution)/shard_map/all_to_all | solution.py:123
  555.4 6.8 %fusion.72 = f32[2,128,4096]{2,1,0:T(8,128)S(1)} fusion(bf16[32,20,4096]{2,1,0:T(8,128)(2,1)} %all-to-all-done.1, pred[1,32,20,128]{3,1,2,0:T(32,128)(4,1)S(1)} %broadcast_and_fusion, pred[1,32,20,128]{3,1,2,0:T(32,128)(4,1)S(1)} %broadcast_and_fusion.1), kind=kOutput, calls=%fused_computation.268 | convolution fusion | flops 1344438272 | bytes 9601024 | tf_op jit(solution)/shard_map/kjst,jsc->ktc/dot_general | solution.py:125
  562.2 1.8 fusion.83
  (413 shorter events, 55.2 us)
Async XLA Ops:
  6.5 229.9 %all-gather.3.cloned.1.call-start = ((), (), s32[]{:S(2)}) async-start(), calls=%async_computation.2 | async-start | bytes 5570560 | tf_op jit(solution)/shard_map/all_gather | solution.py:111
  32.0 63.0 %copy-start.52 = (f32[1,128,16]{1,2,0:T(8,128)S(1)}, f32[1,128,16]{1,2,0:T(8,128)}, u32[]{:S(2)}) copy-start(f32[1,128,16]{1,2,0:T(8,128)} %get-tuple-element.302) | copy-start | bytes 24580
  32.0 63.8 %copy-start.51 = (f32[1,128,16]{1,2,0:T(8,128)S(1)}, f32[1,128,16]{1,2,0:T(8,128)}, u32[]{:S(2)}) copy-start(f32[1,128,16]{1,2,0:T(8,128)} %get-tuple-element.300) | copy-start | bytes 24580
  32.2 7.6 %collective-permute-start = (f32[17,4096]{1,0:T(8,128)S(1)}, f32[17,4096]{1,0:T(8,128)S(1)}, u32[]{:S(2)}, u32[]{:S(2)}) collective-permute-start(f32[17,4096]{1,0:T(8,128)S(1)} %pad_maximum_fusion), channel_id=1, source_target_pairs={{0,32},{32,64},{64,96},{96,128},{128,160},{160,192},{192,224},{224... | collective-permute-start | bytes 835592 | tf_op jit(solution)/shard_map/ppermute | solution.py:10
  39.7 9.1 %collective-permute-start.1 = (f32[17,4096]{1,0:T(8,128)S(1)}, f32[17,4096]{1,0:T(8,128)S(1)}, u32[]{:S(2)}, u32[]{:S(2)}) collective-permute-start(f32[17,4096]{1,0:T(8,128)S(1)} %collective-permute-done), channel_id=1, source_target_pairs={{0,32},{32,64},{64,96},{96,128},{128,160},{160,192},{192,224},{224... | collective-permute-start | bytes 835592 | tf_op jit(solution)/shard_map/ppermute | solution.py:10
  49.0 8.5 %collective-permute-start.2 = (f32[17,4096]{1,0:T(8,128)S(1)}, f32[17,4096]{1,0:T(8,128)S(1)}, u32[]{:S(2)}, u32[]{:S(2)}) collective-permute-start(f32[17,4096]{1,0:T(8,128)S(1)} %pad_maximum_fusion.1), channel_id=1, source_target_pairs={{0,64},{32,96},{64,128},{96,160},{128,192},{160,224},{192,256},{22... | collective-permute-start | bytes 835592 | tf_op jit(solution)/shard_map/ppermute | solution.py:10
  57.7 35.5 %collective-permute-start.3 = (f32[17,4096]{1,0:T(8,128)S(1)}, f32[17,4096]{1,0:T(8,128)S(1)}, u32[]{:S(2)}, u32[]{:S(2)}) collective-permute-start(f32[17,4096]{1,0:T(8,128)S(1)} %pad_maximum_fusion.2), channel_id=1, source_target_pairs={{0,128},{32,160},{64,192},{96,224},{128,256},{160,288},{192,320},{... | collective-permute-start | bytes 835592 | tf_op jit(solution)/shard_map/ppermute | solution.py:10
  93.4 23.4 %collective-permute-start.4 = (f32[17,4096]{1,0:T(8,128)S(1)}, f32[17,4096]{1,0:T(8,128)S(1)}, u32[]{:S(2)}, u32[]{:S(2)}) collective-permute-start(f32[17,4096]{1,0:T(8,128)S(1)} %pad_maximum_fusion.3), channel_id=1, source_target_pairs={{0,256},{32,288},{64,320},{96,352},{128,384},{160,416},{192,448},{... | collective-permute-start | bytes 835592 | tf_op jit(solution)/shard_map/ppermute | solution.py:10
  117.0 96.8 %copy-start.5 = (bf16[1,128,4096]{2,1,0:T(8,128)(2,1)S(1)}, bf16[1,128,4096]{2,1,0:T(8,128)(2,1)}, u32[]{:S(2)}) copy-start(bf16[1,128,4096]{2,1,0:T(8,128)(2,1)} %param.13) | copy-start | bytes 3145732
  123.7 12.9 %copy-start.21 = (f32[16]{0:T(128)S(1)}, f32[16]{0:T(128)}, u32[]{:S(2)}) copy-start(f32[16]{0:T(128)} %get-tuple-element.553) | copy-start | bytes 196 | tf_op jit(solution)/shard_map/while
  123.7 12.9 %copy-start.22 = (f32[16]{0:T(128)S(1)}, f32[16]{0:T(128)}, u32[]{:S(2)}) copy-start(f32[16]{0:T(128)} %get-tuple-element.555) | copy-start | bytes 196 | tf_op jit(solution)/shard_map/while
  123.8 12.9 %copy-start.23 = (f32[16]{0:T(128)S(1)}, f32[16]{0:T(128)}, u32[]{:S(2)}) copy-start(f32[16]{0:T(128)} %get-tuple-element.557) | copy-start | bytes 196 | tf_op jit(solution)/shard_map/while
  123.8 12.9 %copy-start.24 = (f32[16]{0:T(128)S(1)}, f32[16]{0:T(128)}, u32[]{:S(2)}) copy-start(f32[16]{0:T(128)} %get-tuple-element.666) | copy-start | bytes 196 | tf_op jit(solution)/shard_map/while
  123.8 12.9 %copy-start.25 = (f32[16]{0:T(128)S(1)}, f32[16]{0:T(128)}, u32[]{:S(2)}) copy-start(f32[16]{0:T(128)} %get-tuple-element.668) | copy-start | bytes 196 | tf_op jit(solution)/shard_map/while
  123.8 12.9 %copy-start.26 = (f32[16]{0:T(128)S(1)}, f32[16]{0:T(128)}, u32[]{:S(2)}) copy-start(f32[16]{0:T(128)} %get-tuple-element.669) | copy-start | bytes 196 | tf_op jit(solution)/shard_map/while
  123.8 12.9 %copy-start.27 = (f32[16]{0:T(128)S(1)}, f32[16]{0:T(128)}, u32[]{:S(2)}) copy-start(f32[16]{0:T(128)} %get-tuple-element.670) | copy-start | bytes 196 | tf_op jit(solution)/shard_map/while
  147.5 12.9 %copy-start.28 = (f32[16]{0:T(128)S(1)}, f32[16]{0:T(128)}, u32[]{:S(2)}) copy-start(f32[16]{0:T(128)} %get-tuple-element.541) | copy-start | bytes 196 | tf_op jit(solution)/shard_map/while
  147.5 12.9 %copy-start.29 = (f32[16]{0:T(128)S(1)}, f32[16]{0:T(128)}, u32[]{:S(2)}) copy-start(f32[16]{0:T(128)} %get-tuple-element.543) | copy-start | bytes 196 | tf_op jit(solution)/shard_map/while
  147.5 12.9 %copy-start.30 = (f32[16]{0:T(128)S(1)}, f32[16]{0:T(128)}, u32[]{:S(2)}) copy-start(f32[16]{0:T(128)} %get-tuple-element.545) | copy-start | bytes 196 | tf_op jit(solution)/shard_map/while
  147.5 12.9 %copy-start.31 = (f32[16]{0:T(128)S(1)}, f32[16]{0:T(128)}, u32[]{:S(2)}) copy-start(f32[16]{0:T(128)} %get-tuple-element.675) | copy-start | bytes 196 | tf_op jit(solution)/shard_map/while
  147.5 12.9 %copy-start.32 = (f32[16]{0:T(128)S(1)}, f32[16]{0:T(128)}, u32[]{:S(2)}) copy-start(f32[16]{0:T(128)} %get-tuple-element.677) | copy-start | bytes 196 | tf_op jit(solution)/shard_map/while
  147.5 12.9 %copy-start.33 = (f32[16]{0:T(128)S(1)}, f32[16]{0:T(128)}, u32[]{:S(2)}) copy-start(f32[16]{0:T(128)} %get-tuple-element.678) | copy-start | bytes 196 | tf_op jit(solution)/shard_map/while
  147.6 12.9 %copy-start.34 = (f32[16]{0:T(128)S(1)}, f32[16]{0:T(128)}, u32[]{:S(2)}) copy-start(f32[16]{0:T(128)} %get-tuple-element.679) | copy-start | bytes 196 | tf_op jit(solution)/shard_map/while
  147.6 13.3 %copy-start.21 = (f32[16]{0:T(128)S(1)}, f32[16]{0:T(128)}, u32[]{:S(2)}) copy-start(f32[16]{0:T(128)} %get-tuple-element.553) | copy-start | bytes 196 | tf_op jit(solution)/shard_map/while
  147.6 13.3 %copy-start.22 = (f32[16]{0:T(128)S(1)}, f32[16]{0:T(128)}, u32[]{:S(2)}) copy-start(f32[16]{0:T(128)} %get-tuple-element.555) | copy-start | bytes 196 | tf_op jit(solution)/shard_map/while
  147.6 13.3 %copy-start.23 = (f32[16]{0:T(128)S(1)}, f32[16]{0:T(128)}, u32[]{:S(2)}) copy-start(f32[16]{0:T(128)} %get-tuple-element.557) | copy-start | bytes 196 | tf_op jit(solution)/shard_map/while
  147.6 13.3 %copy-start.24 = (f32[16]{0:T(128)S(1)}, f32[16]{0:T(128)}, u32[]{:S(2)}) copy-start(f32[16]{0:T(128)} %get-tuple-element.666) | copy-start | bytes 196 | tf_op jit(solution)/shard_map/while
  147.6 13.3 %copy-start.25 = (f32[16]{0:T(128)S(1)}, f32[16]{0:T(128)}, u32[]{:S(2)}) copy-start(f32[16]{0:T(128)} %get-tuple-element.668) | copy-start | bytes 196 | tf_op jit(solution)/shard_map/while
  147.6 13.3 %copy-start.26 = (f32[16]{0:T(128)S(1)}, f32[16]{0:T(128)}, u32[]{:S(2)}) copy-start(f32[16]{0:T(128)} %get-tuple-element.669) | copy-start | bytes 196 | tf_op jit(solution)/shard_map/while
  147.6 13.3 %copy-start.27 = (f32[16]{0:T(128)S(1)}, f32[16]{0:T(128)}, u32[]{:S(2)}) copy-start(f32[16]{0:T(128)} %get-tuple-element.670) | copy-start | bytes 196 | tf_op jit(solution)/shard_map/while
  171.8 13.1 %copy-start.21 = (f32[16]{0:T(128)S(1)}, f32[16]{0:T(128)}, u32[]{:S(2)}) copy-start(f32[16]{0:T(128)} %get-tuple-element.553) | copy-start | bytes 196 | tf_op jit(solution)/shard_map/while
  171.8 13.1 %copy-start.22 = (f32[16]{0:T(128)S(1)}, f32[16]{0:T(128)}, u32[]{:S(2)}) copy-start(f32[16]{0:T(128)} %get-tuple-element.555) | copy-start | bytes 196 | tf_op jit(solution)/shard_map/while
  171.8 13.1 %copy-start.23 = (f32[16]{0:T(128)S(1)}, f32[16]{0:T(128)}, u32[]{:S(2)}) copy-start(f32[16]{0:T(128)} %get-tuple-element.557) | copy-start | bytes 196 | tf_op jit(solution)/shard_map/while
  171.8 13.1 %copy-start.24 = (f32[16]{0:T(128)S(1)}, f32[16]{0:T(128)}, u32[]{:S(2)}) copy-start(f32[16]{0:T(128)} %get-tuple-element.666) | copy-start | bytes 196 | tf_op jit(solution)/shard_map/while
  171.8 13.1 %copy-start.25 = (f32[16]{0:T(128)S(1)}, f32[16]{0:T(128)}, u32[]{:S(2)}) copy-start(f32[16]{0:T(128)} %get-tuple-element.668) | copy-start | bytes 196 | tf_op jit(solution)/shard_map/while
  171.8 13.1 %copy-start.26 = (f32[16]{0:T(128)S(1)}, f32[16]{0:T(128)}, u32[]{:S(2)}) copy-start(f32[16]{0:T(128)} %get-tuple-element.669) | copy-start | bytes 196 | tf_op jit(solution)/shard_map/while
  171.8 13.1 %copy-start.27 = (f32[16]{0:T(128)S(1)}, f32[16]{0:T(128)}, u32[]{:S(2)}) copy-start(f32[16]{0:T(128)} %get-tuple-element.670) | copy-start | bytes 196 | tf_op jit(solution)/shard_map/while
  195.8 13.1 %copy-start.21 = (f32[16]{0:T(128)S(1)}, f32[16]{0:T(128)}, u32[]{:S(2)}) copy-start(f32[16]{0:T(128)} %get-tuple-element.553) | copy-start | bytes 196 | tf_op jit(solution)/shard_map/while
  195.8 13.1 %copy-start.22 = (f32[16]{0:T(128)S(1)}, f32[16]{0:T(128)}, u32[]{:S(2)}) copy-start(f32[16]{0:T(128)} %get-tuple-element.555) | copy-start | bytes 196 | tf_op jit(solution)/shard_map/while
  195.8 13.1 %copy-start.23 = (f32[16]{0:T(128)S(1)}, f32[16]{0:T(128)}, u32[]{:S(2)}) copy-start(f32[16]{0:T(128)} %get-tuple-element.557) | copy-start | bytes 196 | tf_op jit(solution)/shard_map/while
  195.9 13.1 %copy-start.24 = (f32[16]{0:T(128)S(1)}, f32[16]{0:T(128)}, u32[]{:S(2)}) copy-start(f32[16]{0:T(128)} %get-tuple-element.666) | copy-start | bytes 196 | tf_op jit(solution)/shard_map/while
  195.9 13.1 %copy-start.25 = (f32[16]{0:T(128)S(1)}, f32[16]{0:T(128)}, u32[]{:S(2)}) copy-start(f32[16]{0:T(128)} %get-tuple-element.668) | copy-start | bytes 196 | tf_op jit(solution)/shard_map/while
  195.9 13.1 %copy-start.26 = (f32[16]{0:T(128)S(1)}, f32[16]{0:T(128)}, u32[]{:S(2)}) copy-start(f32[16]{0:T(128)} %get-tuple-element.669) | copy-start | bytes 196 | tf_op jit(solution)/shard_map/while
  195.9 13.1 %copy-start.27 = (f32[16]{0:T(128)S(1)}, f32[16]{0:T(128)}, u32[]{:S(2)}) copy-start(f32[16]{0:T(128)} %get-tuple-element.670) | copy-start | bytes 196 | tf_op jit(solution)/shard_map/while
  222.8 157.2 %all-to-all-start = ((bf16[32,20,4096]{2,1,0:T(8,128)(2,1)}), bf16[32,20,4096]{2,1,0:T(8,128)(2,1)}, u32[]{:S(2)}, u32[]{:S(2)}) async-start(bf16[32,20,4096]{2,1,0:T(8,128)(2,1)} %copy.51), calls=%async_computation | async-start | bytes 12582912 | tf_op jit(solution)/shard_map/all_to_all | solution.py:107
  235.7 154.1 %all-gather.5.cloned.1.call-start = ((), (), s32[]{:S(2)}) async-start(), calls=%async_computation.3 | async-start | bytes 5570560 | tf_op jit(solution)/shard_map/all_gather | solution.py:119
  402.4 153.0 %all-to-all-start.1 = ((bf16[32,20,4096]{2,1,0:T(8,128)(2,1)}), bf16[32,20,4096]{2,1,0:T(8,128)(2,1)}, u32[]{:S(2)}, u32[]{:S(2)}) async-start(bf16[32,20,4096]{2,1,0:T(8,128)(2,1)} %copy.53), calls=%async_computation.1 | async-start | bytes 12582912 | tf_op jit(solution)/shard_map/all_to_all | solution.py:123
  414.5 147.7 %copy-start.11 = (f32[4096]{0:T(1024)S(1)}, f32[4096]{0:T(1024)}, u32[]{:S(2)}) copy-start(f32[4096]{0:T(1024)} %param.19) | copy-start | bytes 49156
  (111 other events, 1148.1 us)
Sparse Core Ops, SparseCore 0:
  117.1 47.5 all-gather.2
  238.6 53.3 all-gather.4

commit v3 on v2

--- a/solution.py
+++ b/solution.py
@@ -1,6 +1,7 @@
 import jax
 import jax.numpy as jnp
 from jax import lax
+from jax.experimental import pallas as pl
 from jax.sharding import PartitionSpec as P
 
 
@@ -23,31 +24,54 @@
     return packed[1:]
 
 
+def sweep_kernel(delta_ref, driven_ref, a_ref, start_ref, b_ref, c_ref, y_ref):
+    tokens_here = delta_ref.shape[0]
+    lanes = b_ref.shape[2]
+    subs = delta_ref.shape[1] // lanes
+    rates = [a_ref[:, i * lanes : (i + 1) * lanes] for i in range(subs)]
+
+    def step(t, states):
+        b_rows = b_ref[t]
+        c_rows = c_ref[t]
+        d_row = delta_ref[pl.ds(t, 1), :]
+        u_row = driven_ref[pl.ds(t, 1), :]
+        new_states = []
+        outs = []
+        for i in range(subs):
+            d = d_row[:, i * lanes : (i + 1) * lanes]
+            u = u_row[:, i * lanes : (i + 1) * lanes]
+            state = jnp.exp(rates[i] * d) * states[i] + u * b_rows
+            new_states.append(state)
+            outs.append(jnp.sum(c_rows * state, axis=0, keepdims=True))
+        y_ref[pl.ds(t, 1), :] = jnp.concatenate(outs, axis=1)
+        return tuple(new_states)
+
+    first = tuple(start_ref[:, i * lanes : (i + 1) * lanes] for i in range(subs))
+    lax.fori_loop(0, tokens_here, step, first, unroll=8)
+
+
 def sweep(start_state, a_neg, delta, driven, b_in, c_out):
     tokens_here, channels = delta.shape
     nstate = b_in.shape[1]
-    group = 32
-    turns = tokens_here // group
-
-    def advance(state, inputs):
-        rate, drive, b_rows, c_rows = inputs
-        results = []
-        for inner in range(group):
-            state = (
-                jnp.exp(a_neg * rate[inner][None, :]) * state
-                + drive[inner][None, :] * b_rows[inner][:, None]
-            )
-            results.append(jnp.sum(c_rows[inner][:, None] * state, axis=0))
-        return (state, jnp.stack(results))
-
-    inputs = (
-        delta.reshape(turns, group, channels),
-        driven.reshape(turns, group, channels),
-        b_in.reshape(turns, group, nstate),
-        c_out.reshape(turns, group, nstate),
-    )
-    final, results = lax.scan(advance, start_state, inputs)
-    return (final, results.reshape(tokens_here, channels))
+    lanes = 128
+    block = 512
+    b_wide = jnp.broadcast_to(b_in[:, :, None], (tokens_here, nstate, lanes))
+    c_wide = jnp.broadcast_to(c_out[:, :, None], (tokens_here, nstate, lanes))
+    row_spec = pl.BlockSpec((tokens_here, block), lambda k: (0, k))
+    state_spec = pl.BlockSpec((nstate, block), lambda k: (0, k))
+    wide_spec = pl.BlockSpec((tokens_here, nstate, lanes), lambda k: (0, 0, 0))
+    return pl.pallas_call(
+        sweep_kernel,
+        out_shape=jax.ShapeDtypeStruct((tokens_here, channels), jnp.float32),
+        grid=(channels // block,),
+        in_specs=[row_spec, row_spec, state_spec, state_spec, wide_spec, wide_spec],
+        out_specs=row_spec,
+        cost_estimate=pl.CostEstimate(
+            flops=8 * tokens_here * nstate * channels,
+            transcendentals=tokens_here * nstate * channels,
+            bytes_accessed=4 * (3 * tokens_here * channels + 2 * nstate * channels),
+        ),
+    )(delta, driven, a_neg, start_state, b_wide, c_wide)
 
 
 def per_device(
@@ -79,7 +103,7 @@
         )
     start = carry_in(a_neg, cumulated[-1], jnp.concatenate(ends, axis=1))
     start, w_up, w_down = lax.optimization_barrier((start, w_up, w_down))
-    _, scanned = sweep(start, a_neg, delta, driven, b_in, c_out)
+    scanned = sweep(start, a_neg, delta, driven, b_in, c_out)
     mixer = (scanned + d_skip * xfloat).astype(jnp.bfloat16)
     experts_count = w_router.shape[0]
     owners = lax.axis_size("exp")

time: 580 us -> 494 us (0.85); the launches traced: 571 us -> 493 us
  local copies, waits for them, and re-layouts: 89.9 us -> 24.5 us
  other arithmetic: 48.2 us -> 17.7 us
  Pallas kernels: 0 us -> 17.3 us
  waiting for transfers between devices: 349 us -> 355 us
    slice x20 -> x1, local copies, waits for them, and re-layouts: 40.7 us -> 0.18 us  [the longest x8 20.5 us: advance(): drive[inner][None, :] * b_rows[inner][:, None]]
    reduce_sum x36 -> x0, other arithmetic: 27.5 us -> none  [advance(): results.append(jnp.sum(c_rows[inner][:, None] * state, axis=0))]
    mul x12 -> x0, local copies, waits for them, and re-layouts: 18.2 us -> none  [the longest x8 11.3 us: advance(): drive[inner][None, :] * b_rows[inner][:, None]]
    pallas_call x0 -> x1, Pallas kernels: none -> 17.3 us  [sweep(): pl.pallas_call(sweep_kernel, out_shape=jax.ShapeDtypeStruct((tokens_here,...]
    another operation x5 -> x1, local copies, waits for them, and re-layouts: 5.96 us -> 0.01 us  [the longest x4 5.95 us: advance(): return (state, jnp.stack(results))]
  transfers between devices with their start and end apart: 9 -> 9, of which waited for: 7 -> 8; matrix products, arithmetic and copies ran while one was open for 21% -> 5% of each run, Pallas kernels for 0% -> 4%
where the time goes in v3:
time: 494 us; the launch traced here: 493 us
  waiting for transfers between devices  355 us (72%)
  starting transfers between devices  35.9 us (7%)
  matrix products  29.1 us (6%)
  local copies, waits for them, and re-layouts  24.5 us (5%)
  other arithmetic  17.7 us (4%)
  Pallas kernels  17.3 us (4%)
  between operations  14 us (3%)
    all_to_all x1, waiting for transfers between devices, per_device(): lax.all_to_all(partial_out, 'exp', split_axis=0, concat_axis=0, tiled=True)  141 us
    all_to_all x1, waiting for transfers between devices, per_device(): lax.all_to_all(outgoing, 'exp', split_axis=0, concat_axis=0, tiled=True)  141 us
    ppermute x5, waiting for transfers between devices, from_behind(): return lax.ppermute(value, axis, pairs)  69.6 us
    pallas_call x1, Pallas kernels, sweep(): pl.pallas_call(sweep_kernel, out_shape=jax.ShapeDtypeStruct((tokens_here,...  17.3 us
    ppermute x5, starting transfers between devices, from_behind(): return lax.ppermute(value, axis, pairs)  14.5 us
    all_to_all x1, starting transfers between devices, per_device(): lax.all_to_all(outgoing, 'exp', split_axis=0, concat_axis=0, tiled=True)  12.9 us
  transfers between devices with their start and end apart: 9, of which 8 were waited for; matrix products, arithmetic and copies ran while one was open for 5% of the time, Pallas kernels for 4%

profile of v3, /device:TPU:47, one launch (start us, length us, event | category | flops | bytes accessed | tf_op | source)
XLA Modules:
  0.0 493.3 jit_solution(11607115219775254380)
XLA Ops:
  6.5 1.6 copy-done
  8.1 4.8 convert_multiply_fusion.1
  12.9 3.5 reduce_window_sum.26
  16.4 0.6 fusion.49
  17.0 2.6 fusion.50
  19.7 0.7 fusion.51
  20.4 0.6 slice_bitcast_fusion.2
  21.0 0.8 copy.43
  21.9 1.0 slice_subtract_fusion.2
  23.0 1.7 multiply_reduce_fusion.1
  24.8 5.5 %multiply_reduce_fusion = (f32[16,512]{1,0:T(8,128)S(1)}, f32[16,512]{1,0:T(8,128)S(1)}, f32[16,512]{1,0:T(8,128)S(1)}, f32[16,512]{1,0:T(8,128)S(1)}, f32[16,512]{1,0:T(8,128)S(1)}, /*index=5*/f32[16,512]{1,0:T(8,128)S(1)}) fusion(f32[128,512]{1,0:T(8,128)S(1)} %get-tuple-element.42, f32[128,512]{1,0:T(8,128)S(1)} %get-tuple-element.26, ...), kind=kLoop, calls=%fused_computation.13 | loop fusion | flops 25116672 | bytes 3547136 | tf_op jit(solution)/shard_map/reduce_sum | solution.py:100
  30.5 2.9 collective-permute-start
  33.4 4.7 collective-permute-done
  38.1 4.4 collective-permute-start.1
  42.5 4.7 collective-permute-done.1
  47.4 2.3 collective-permute-start.2
  49.7 6.2 %collective-permute-done.2 = f32[17,4096]{1,0:T(8,128)S(1)} collective-permute-done((f32[17,4096]{1,0:T(8,128)S(1)}, f32[17,4096]{1,0:T(8,128)S(1)}, u32[]{:S(2)}, u32[]{:S(2)}) %collective-permute-start.2) | collective-permute-done | bytes 278560 | tf_op jit(solution)/shard_map/ppermute | solution.py:11
  56.1 3.4 collective-permute-start.3
  59.5 32.1 %collective-permute-done.3 = f32[17,4096]{1,0:T(8,128)S(1)} collective-permute-done((f32[17,4096]{1,0:T(8,128)S(1)}, f32[17,4096]{1,0:T(8,128)S(1)}, u32[]{:S(2)}, u32[]{:S(2)}) %collective-permute-start.3) | collective-permute-done | bytes 278560 | tf_op jit(solution)/shard_map/ppermute | solution.py:11
  91.8 1.5 collective-permute-start.4
  93.3 21.9 %collective-permute-done.4 = f32[17,4096]{1,0:T(8,128)S(1)} collective-permute-done((f32[17,4096]{1,0:T(8,128)S(1)}, f32[17,4096]{1,0:T(8,128)S(1)}, u32[]{:S(2)}, u32[]{:S(2)}) %collective-permute-start.4) | collective-permute-done | bytes 278560 | tf_op jit(solution)/shard_map/ppermute | solution.py:11
  115.2 0.8 fusion.29.start_ref
  116.6 0.6 reduce-window.6
  117.2 0.2 slice_reduce_fusion.4
  117.5 0.1 sub.138
  117.6 0.2 slice_reduce_fusion.2
  117.8 0.2 slice_reduce_fusion.3
  118.1 1.3 broadcast_in_dim.11.b_ref
  119.4 1.3 broadcast_in_dim.13.c_ref
  120.8 17.3 %shard_map.109 = f32[128,4096]{1,0:T(8,128)} custom-call(f32[128,4096]{1,0:T(8,128)} %get-tuple-element.64.delta_ref, f32[128,4096]{1,0:T(8,128)} %get-tuple-element.63.driven_ref, f32[16,4096]{1,0:T(8,128)} %copy-done.3, f32[16,4096]{1,0:T(8,128)} %fusion.29.start_ref, f32[128,16,128]{2,1,0:T(8,128)} %broadcast_in_dim.11.b_ref, ...), custom_call_target="tpu_custom_call" | custom-call | flops 67108864 | bytes 6815744 | tf_op jit(solution)/shard_map/pallas_call | solution.py:63
  138.1 1.9 fusion.12
  140.0 1.5 convolution_convert_fusion.1
  141.5 5.6 %copy.51 = bf16[32,20,4096]{2,1,0:T(8,128)(2,1)} copy(bf16[32,20,4096]{2,0,1:T(8,128)(2,1)S(1)} %convolution_convert_fusion.1) | data formatting | bytes 10485760 | tf_op jit(solution)/shard_map/convert_element_type | solution.py:130
  147.1 12.9 %all-to-all-start = ((bf16[32,20,4096]{2,1,0:T(8,128)(2,1)}), bf16[32,20,4096]{2,1,0:T(8,128)(2,1)}, u32[]{:S(2)}, u32[]{:S(2)}) async-start(bf16[32,20,4096]{2,1,0:T(8,128)(2,1)} %copy.51), calls=%async_computation | async-start | bytes 12582912 | tf_op jit(solution)/shard_map/all_to_all | solution.py:131
  160.0 0.3 all-gather.5.cloned.1.call-start
  160.3 0.5 all-gather.5.cloned.1.call-update
  160.7 3.0 all-gather.3.cloned.1.call-done
  163.8 140.7 %all-to-all-done = bf16[32,20,4096]{2,1,0:T(8,128)(2,1)} async-done(((bf16[32,20,4096]{2,1,0:T(8,128)(2,1)}), bf16[32,20,4096]{2,1,0:T(8,128)(2,1)}, u32[]{:S(2)}, u32[]{:S(2)}) %all-to-all-start) | async-done | bytes 5242912 | tf_op jit(solution)/shard_map/all_to_all | solution.py:131
  304.5 8.9 %multiply_convert_fusion = bf16[32,20,640]{2,1,0:T(8,128)(2,1)S(1)} fusion(bf16[32,20,4096]{2,1,0:T(8,128)(2,1)} %all-to-all-done, bf16[1,4096,640]{2,1,0:T(8,128)(2,1)} %all-gather.3.cloned.1.call-done), kind=kOutput, calls=%fused_computation.32 | convolution fusion | flops 3357491200 | bytes 11304960 | tf_op jit(solution)/shard_map/jsc,ch->jsh/dot_general | solution.py:132
  313.4 6.9 %convolution_convert_fusion = bf16[32,20,4096]{2,0,1:T(8,128)(2,1)S(1)} fusion(bf16[1,640,4096]{2,1,0:T(8,128)(2,1)} %all-gather.5.cloned.1.call-done, bf16[32,20,640]{2,1,0:T(8,128)(2,1)S(1)} %multiply_convert_fusion), kind=kOutput, calls=%fused_computation.1 | convolution fusion | flops 3358064640 | bytes 11304960 | tf_op jit(solution)/shard_map/jsh,hc->jsc/dot_general | solution.py:140
  320.3 5.6 %copy.53 = bf16[32,20,4096]{2,1,0:T(8,128)(2,1)} copy(bf16[32,20,4096]{2,0,1:T(8,128)(2,1)S(1)} %convolution_convert_fusion) | data formatting | bytes 10485760 | tf_op jit(solution)/shard_map/optimization_barrier | solution.py:139
  325.9 8.3 %all-to-all-start.1 = ((bf16[32,20,4096]{2,1,0:T(8,128)(2,1)}), bf16[32,20,4096]{2,1,0:T(8,128)(2,1)}, u32[]{:S(2)}, u32[]{:S(2)}) async-start(bf16[32,20,4096]{2,1,0:T(8,128)(2,1)} %copy.53), calls=%async_computation.1 | async-start | bytes 12582912 | tf_op jit(solution)/shard_map/all_to_all | solution.py:147
  334.5 0.4 fusion.52
  334.9 2.0 gather_fusion
  337.1 0.2 fusion.48
  337.3 141.0 %all-to-all-done.1 = bf16[32,20,4096]{2,1,0:T(8,128)(2,1)} async-done(((bf16[32,20,4096]{2,1,0:T(8,128)(2,1)}), bf16[32,20,4096]{2,1,0:T(8,128)(2,1)}, u32[]{:S(2)}, u32[]{:S(2)}) %all-to-all-start.1) | async-done | bytes 5242912 | tf_op jit(solution)/shard_map/all_to_all | solution.py:147
  478.3 6.6 %fusion.8 = f32[2,128,4096]{2,1,0:T(8,128)S(1)} fusion(bf16[32,20,4096]{2,1,0:T(8,128)(2,1)} %all-to-all-done.1, pred[1,32,20,128]{3,1,2,0:T(32,128)(4,1)S(1)} %broadcast_and_fusion, pred[1,32,20,128]{3,1,2,0:T(32,128)(4,1)S(1)} %broadcast_and_fusion.1), kind=kOutput, calls=%fused_computation.11 | convolution fusion | flops 1344438272 | bytes 9601024 | tf_op jit(solution)/shard_map/kjst,jsc->ktc/dot_general | solution.py:149
  484.9 1.5 fusion.20
  (83 shorter events, 2.0 us)
Async XLA Ops:
  6.5 1.6 copy-start
  6.5 157.2 %all-gather.3.cloned.1.call-start = ((), (), s32[]{:S(2)}) async-start(), calls=%async_computation.2 | async-start | bytes 5570560 | tf_op jit(solution)/shard_map/all_gather | solution.py:135
  12.9 6.8 %copy-start.2 = (f32[16,4096]{1,0:T(8,128)S(1)}, f32[16,4096]{1,0:T(8,128)}, u32[]{:S(2)}) copy-start(f32[16,4096]{1,0:T(8,128)} %param.16) | copy-start | bytes 786436
  12.9 7.5 %copy-start.19 = (f32[1,128,32]{1,2,0:T(8,128)S(1)}, f32[1,128,32]{1,2,0:T(8,128)}, u32[]{:S(2)}) copy-start(f32[1,128,32]{1,2,0:T(8,128)} %param.13) | copy-start | bytes 49156
  19.7 5.1 %copy-start.3 = (f32[16,4096]{1,0:T(8,128)}, f32[16,4096]{1,0:T(8,128)S(1)}, u32[]{:S(2)}) copy-start(f32[16,4096]{1,0:T(8,128)S(1)} %exponential_negate_fusion.a_ref) | copy-start | bytes 786436
  21.8 1.2 copy-start.8
  21.8 1.2 copy-start.9
  21.9 1.2 copy-start.15
  21.9 1.2 copy-start.16
  21.9 2.9 copy-start.5
  21.9 2.9 copy-start.6
  21.9 2.9 copy-start.7
  21.9 2.9 copy-start.11
  21.9 2.9 copy-start.12
  21.9 2.9 copy-start.13
  21.9 2.9 copy-start.14
  30.4 85.7 %copy-start.20 = (s32[1,128,2]{1,2,0:T(2,128)S(1)}, s32[1,128,2]{1,2,0:T(2,128)}, u32[]{:S(2)}) copy-start(s32[1,128,2]{1,2,0:T(2,128)} %param.19) | copy-start | bytes 3076
  30.4 86.1 %copy-start.17 = (f32[128,16]{0,1:T(8,128)S(1)}, f32[128,16]{0,1:T(8,128)}, u32[]{:S(2)}) copy-start(f32[128,16]{0,1:T(8,128)} %get-tuple-element.59) | copy-start | bytes 24580
  30.5 7.6 %collective-permute-start = (f32[17,4096]{1,0:T(8,128)S(1)}, f32[17,4096]{1,0:T(8,128)S(1)}, u32[]{:S(2)}, u32[]{:S(2)}) collective-permute-start(f32[17,4096]{1,0:T(8,128)S(1)} %pad_maximum_fusion), channel_id=1, source_target_pairs={{0,32},{32,64},{64,96},{96,128},{128,160},{160,192},{192,224},{224... | collective-permute-start | bytes 835592 | tf_op jit(solution)/shard_map/ppermute | solution.py:11
  38.1 9.1 %collective-permute-start.1 = (f32[17,4096]{1,0:T(8,128)S(1)}, f32[17,4096]{1,0:T(8,128)S(1)}, u32[]{:S(2)}, u32[]{:S(2)}) collective-permute-start(f32[17,4096]{1,0:T(8,128)S(1)} %collective-permute-done), channel_id=1, source_target_pairs={{0,32},{32,64},{64,96},{96,128},{128,160},{160,192},{192,224},{224... | collective-permute-start | bytes 835592 | tf_op jit(solution)/shard_map/ppermute | solution.py:11
  47.4 8.5 %collective-permute-start.2 = (f32[17,4096]{1,0:T(8,128)S(1)}, f32[17,4096]{1,0:T(8,128)S(1)}, u32[]{:S(2)}, u32[]{:S(2)}) collective-permute-start(f32[17,4096]{1,0:T(8,128)S(1)} %pad_maximum_fusion.1), channel_id=1, source_target_pairs={{0,64},{32,96},{64,128},{96,160},{128,192},{160,224},{192,256},{22... | collective-permute-start | bytes 835592 | tf_op jit(solution)/shard_map/ppermute | solution.py:11
  56.1 35.5 %collective-permute-start.3 = (f32[17,4096]{1,0:T(8,128)S(1)}, f32[17,4096]{1,0:T(8,128)S(1)}, u32[]{:S(2)}, u32[]{:S(2)}) collective-permute-start(f32[17,4096]{1,0:T(8,128)S(1)} %pad_maximum_fusion.2), channel_id=1, source_target_pairs={{0,128},{32,160},{64,192},{96,224},{128,256},{160,288},{192,320},{... | collective-permute-start | bytes 835592 | tf_op jit(solution)/shard_map/ppermute | solution.py:11
  91.8 23.4 %collective-permute-start.4 = (f32[17,4096]{1,0:T(8,128)S(1)}, f32[17,4096]{1,0:T(8,128)S(1)}, u32[]{:S(2)}, u32[]{:S(2)}) collective-permute-start(f32[17,4096]{1,0:T(8,128)S(1)} %pad_maximum_fusion.3), channel_id=1, source_target_pairs={{0,256},{32,288},{64,320},{96,352},{128,384},{160,416},{192,448},{... | collective-permute-start | bytes 835592 | tf_op jit(solution)/shard_map/ppermute | solution.py:11
  120.8 17.3 %copy-start.4 = (bf16[1,128,4096]{2,1,0:T(8,128)(2,1)S(1)}, bf16[1,128,4096]{2,1,0:T(8,128)(2,1)}, u32[]{:S(2)}) copy-start(bf16[1,128,4096]{2,1,0:T(8,128)(2,1)} %param.11) | copy-start | bytes 3145732
  120.8 17.3 %copy-start.18 = (f32[4096]{0:T(1024)S(1)}, f32[4096]{0:T(1024)}, u32[]{:S(2)}) copy-start(f32[4096]{0:T(1024)} %param.17) | copy-start | bytes 49156
  147.1 157.4 %all-to-all-start = ((bf16[32,20,4096]{2,1,0:T(8,128)(2,1)}), bf16[32,20,4096]{2,1,0:T(8,128)(2,1)}, u32[]{:S(2)}, u32[]{:S(2)}) async-start(bf16[32,20,4096]{2,1,0:T(8,128)(2,1)} %copy.51), calls=%async_computation | async-start | bytes 12582912 | tf_op jit(solution)/shard_map/all_to_all | solution.py:131
  160.0 153.4 %all-gather.5.cloned.1.call-start = ((), (), s32[]{:S(2)}) async-start(), calls=%async_computation.3 | async-start | bytes 5570560 | tf_op jit(solution)/shard_map/all_gather | solution.py:143
  325.9 8.6 %copy-start.10 = (bf16[16,4096]{1,0:T(8,128)(2,1)S(1)}, bf16[16,4096]{1,0:T(8,128)(2,1)}, u32[]{:S(2)}) copy-start(bf16[16,4096]{1,0:T(8,128)(2,1)} %param.18) | copy-start | bytes 393220
  325.9 152.4 %all-to-all-start.1 = ((bf16[32,20,4096]{2,1,0:T(8,128)(2,1)}), bf16[32,20,4096]{2,1,0:T(8,128)(2,1)}, u32[]{:S(2)}, u32[]{:S(2)}) async-start(bf16[32,20,4096]{2,1,0:T(8,128)(2,1)} %copy.53), calls=%async_computation.1 | async-start | bytes 12582912 | tf_op jit(solution)/shard_map/all_to_all | solution.py:147
  478.3 8.2 %copy-start.1 = (bf16[256,4096]{1,0:T(8,128)(2,1)S(1)}, bf16[256,4096]{1,0:T(8,128)(2,1)}, u32[]{:S(2)}) copy-start(bf16[256,4096]{1,0:T(8,128)(2,1)} %param.14) | copy-start | bytes 6291460
Sparse Core Ops, SparseCore 0:
  116.2 47.5 all-gather.2
  165.8 53.5 all-gather.4

commit v4 on v3

--- a/solution.py
+++ b/solution.py
@@ -125,30 +125,35 @@
         (dest == picks[None, None, :, c]) & (slot == position[None, None, :, c]) for c in range(2)
     ]
     dispatch = (hit[0] | hit[1]).astype(jnp.bfloat16)
-    outgoing = jnp.einsum(
-        "jst,tc->jsc", dispatch, mixer, preferred_element_type=jnp.float32
-    ).astype(jnp.bfloat16)
-    incoming = lax.all_to_all(outgoing, "exp", split_axis=0, concat_axis=0, tiled=True)
-    pre_hidden = jnp.einsum(
-        "jsc,ch->jsh",
-        incoming,
-        lax.all_gather(w_up, "seq", axis=1, tiled=True)[0],
-        preferred_element_type=jnp.float32,
-    )
-    hidden = jax.nn.silu(pre_hidden).astype(jnp.bfloat16)
-    partial_out = lax.optimization_barrier(
-        jnp.einsum(
-            "jsh,hc->jsc",
-            hidden,
-            lax.all_gather(w_down, "seq", axis=2, tiled=True)[0],
+    gather = jnp.stack(hit).astype(jnp.bfloat16)
+    w_up_full = lax.all_gather(w_up, "seq", axis=1, tiled=True)[0]
+    w_down_full = lax.all_gather(w_down, "seq", axis=2, tiled=True)[0]
+    chunks = 2
+    step = capacity // chunks
+    picked = None
+    for lower in range(0, capacity, step):
+        outgoing = jnp.einsum(
+            "jst,tc->jsc", dispatch[:, lower : lower + step], mixer, preferred_element_type=jnp.float32
+        ).astype(jnp.bfloat16)
+        incoming = lax.all_to_all(outgoing, "exp", split_axis=0, concat_axis=0, tiled=True)
+        pre_hidden = jnp.einsum(
+            "jsc,ch->jsh", incoming, w_up_full, preferred_element_type=jnp.float32
+        )
+        hidden = jax.nn.silu(pre_hidden).astype(jnp.bfloat16)
+        partial_out = lax.optimization_barrier(
+            jnp.einsum(
+                "jsh,hc->jsc", hidden, w_down_full, preferred_element_type=jnp.float32
+            ).astype(jnp.bfloat16)
+        )
+        returned = lax.all_to_all(partial_out, "exp", split_axis=0, concat_axis=0, tiled=True)
+        part = jnp.einsum(
+            "kjst,jsc->ktc",
+            gather[:, :, lower : lower + step],
+            returned,
             preferred_element_type=jnp.float32,
-        ).astype(jnp.bfloat16)
-    )
-    returned = lax.all_to_all(partial_out, "exp", split_axis=0, concat_axis=0, tiled=True)
-    gather = jnp.stack(hit).astype(jnp.bfloat16)
-    picked = jnp.einsum(
-        "kjst,jsc->ktc", gather, returned, preferred_element_type=jnp.float32
-    ).astype(jnp.bfloat16).astype(jnp.float32)
+        )
+        picked = part if picked is None else picked + part
+    picked = picked.astype(jnp.bfloat16).astype(jnp.float32)
     routed = first[:, None] * picked[0] + second[:, None] * picked[1]
     return (mixer.astype(jnp.float32) + routed).astype(jnp.bfloat16)[None]
 

time: 494 us -> 574 us (1.16)
  the two profiles are of different devices: /device:TPU:47 before, /device:TPU:42 now
where the time goes in v4:
time: 574 us; the launch traced here: 573 us
  waiting for transfers between devices  409 us (71%)
  matrix products  45.1 us (8%)
  starting transfers between devices  38.6 us (7%)
  local copies, waits for them, and re-layouts  31.3 us (5%)
  other arithmetic  17.8 us (3%)
  Pallas kernels  17.3 us (3%)
  between operations  14 us (2%)
    all_to_all x2, waiting for transfers between devices, per_device(): lax.all_to_all(outgoing, 'exp', split_axis=0, concat_axis=0, tiled=True)  170 us
    all_to_all x2, waiting for transfers between devices, per_device(): lax.all_to_all(partial_out, 'exp', split_axis=0, concat_axis=0, tiled=True)  165 us
    ppermute x5, waiting for transfers between devices, from_behind(): return lax.ppermute(value, axis, pairs)  74.1 us
    dot_general x2, matrix products, per_device(): jnp.einsum('jsh,hc->jsc', hidden, w_down_full, preferred_element_type=jnp...  25.9 us
    all_to_all x2, starting transfers between devices, per_device(): lax.all_to_all(outgoing, 'exp', split_axis=0, concat_axis=0, tiled=True)  18.4 us
    pallas_call x1, Pallas kernels, sweep(): pl.pallas_call(sweep_kernel, out_shape=jax.ShapeDtypeStruct((tokens_here,...  17.3 us
    dot_general x2, matrix products, per_device(): jnp.einsum('kjst,jsc->ktc', gather[:, :, lower:lower + step], returned, p...  12.3 us
  transfers between devices with their start and end apart: 11, of which 9 were waited for; matrix products, arithmetic and copies ran while one was open for 11% of the time, Pallas kernels for 3%

profile of v4, /device:TPU:42, one launch (start us, length us, event | category | flops | bytes accessed | tf_op | source)
XLA Modules:
  0.0 573.3 jit_solution(17294766557621972806)
XLA Ops:
  6.5 1.6 copy-done
  8.1 4.8 convert_multiply_fusion.1
  13.0 3.5 reduce_window_sum.26
  16.4 0.6 fusion.68
  17.1 2.6 fusion.69
  19.7 0.7 fusion.70
  20.5 0.6 slice_bitcast_fusion.2
  21.1 0.8 copy.47
  22.0 1.0 slice_subtract_fusion.2
  23.1 1.7 multiply_reduce_fusion.1
  24.9 5.5 multiply_reduce_fusion
  30.6 1.9 collective-permute-start
  32.5 7.2 %collective-permute-done = f32[17,4096]{1,0:T(8,128)S(1)} collective-permute-done((f32[17,4096]{1,0:T(8,128)S(1)}, f32[17,4096]{1,0:T(8,128)S(1)}, u32[]{:S(2)}, u32[]{:S(2)}) %collective-permute-start) | collective-permute-done | bytes 278560 | tf_op jit(solution)/shard_map/ppermute | solution.py:11
  39.7 1.9 collective-permute-start.1
  41.6 7.2 %collective-permute-done.1 = f32[17,4096]{1,0:T(8,128)S(1)} collective-permute-done((f32[17,4096]{1,0:T(8,128)S(1)}, f32[17,4096]{1,0:T(8,128)S(1)}, u32[]{:S(2)}, u32[]{:S(2)}) %collective-permute-start.1) | collective-permute-done | bytes 278560 | tf_op jit(solution)/shard_map/ppermute | solution.py:11
  48.9 2.6 collective-permute-start.2
  51.5 8.8 %collective-permute-done.2 = f32[17,4096]{1,0:T(8,128)S(1)} collective-permute-done((f32[17,4096]{1,0:T(8,128)S(1)}, f32[17,4096]{1,0:T(8,128)S(1)}, u32[]{:S(2)}, u32[]{:S(2)}) %collective-permute-start.2) | collective-permute-done | bytes 278560 | tf_op jit(solution)/shard_map/ppermute | solution.py:11
  60.5 2.1 collective-permute-start.3
  62.7 28.8 %collective-permute-done.3 = f32[17,4096]{1,0:T(8,128)S(1)} collective-permute-done((f32[17,4096]{1,0:T(8,128)S(1)}, f32[17,4096]{1,0:T(8,128)S(1)}, u32[]{:S(2)}, u32[]{:S(2)}) %collective-permute-start.3) | collective-permute-done | bytes 278560 | tf_op jit(solution)/shard_map/ppermute | solution.py:11
  91.6 1.3 collective-permute-start.4
  92.9 22.1 %collective-permute-done.4 = f32[17,4096]{1,0:T(8,128)S(1)} collective-permute-done((f32[17,4096]{1,0:T(8,128)S(1)}, f32[17,4096]{1,0:T(8,128)S(1)}, u32[]{:S(2)}, u32[]{:S(2)}) %collective-permute-start.4) | collective-permute-done | bytes 278560 | tf_op jit(solution)/shard_map/ppermute | solution.py:11
  115.1 0.8 fusion.33.start_ref
  116.7 0.6 reduce-window.6
  118.2 1.3 broadcast_in_dim.11.b_ref
  119.5 1.3 broadcast_in_dim.13.c_ref
  120.9 17.3 %shard_map.109 = f32[128,4096]{1,0:T(8,128)} custom-call(f32[128,4096]{1,0:T(8,128)} %get-tuple-element.64.delta_ref, f32[128,4096]{1,0:T(8,128)} %get-tuple-element.63.driven_ref, f32[16,4096]{1,0:T(8,128)} %copy-done.3, f32[16,4096]{1,0:T(8,128)} %fusion.33.start_ref, f32[128,16,128]{2,1,0:T(8,128)} %broadcast_in_dim.11.b_ref, ...), custom_call_target="tpu_custom_call" | custom-call | flops 67108864 | bytes 6815744 | tf_op jit(solution)/shard_map/pallas_call | solution.py:63
  138.2 1.9 fusion.16
  140.1 0.8 convolution_convert_fusion
  140.9 3.7 copy.59
  144.7 13.5 %all-to-all-start.2 = ((bf16[32,10,4096]{2,1,0:T(8,128)(2,1)}), bf16[32,10,4096]{2,1,0:T(8,128)(2,1)}, u32[]{:S(2)}, u32[]{:S(2)}) async-start(bf16[32,10,4096]{2,1,0:T(8,128)(2,1)} %copy.59), calls=%async_computation.2 | async-start | bytes 8388608 | tf_op jit(solution)/shard_map/all_to_all | solution.py:138
  158.2 0.8 convolution_convert_fusion.1
  159.0 3.6 copy.55
  162.6 92.5 %all-to-all-done.2 = bf16[32,10,4096]{2,1,0:T(8,128)(2,1)} async-done(((bf16[32,10,4096]{2,1,0:T(8,128)(2,1)}), bf16[32,10,4096]{2,1,0:T(8,128)(2,1)}, u32[]{:S(2)}, u32[]{:S(2)}) %all-to-all-start.2) | async-done | bytes 2621472 | tf_op jit(solution)/shard_map/all_to_all | solution.py:138
  255.1 4.9 all-to-all-start
  260.0 13.0 %convolution_convert_fusion.2 = bf16[32,10,4096]{2,0,1:T(8,128)(2,1)} fusion(bf16[1,640,4096]{2,1,0:T(8,128)(2,1)} %all-gather.5.cloned.1.call-done, bf16[1,4096,640]{2,1,0:T(8,128)(2,1)} %all-gather.3.cloned.1.call-done, bf16[32,10,4096]{2,1,0:T(8,128)(2,1)} %all-to-all-done.2), kind=kOutput, calls=%fused_computation.6 | convolution fusion | flops 3357777920 | bytes 15728640 | tf_op jit(solution)/shard_map/jsh,hc->jsc/dot_general | solution.py:144
  273.0 5.4 copy.61
  278.4 77.5 %all-to-all-done = bf16[32,10,4096]{2,1,0:T(8,128)(2,1)} async-done(((bf16[32,10,4096]{2,1,0:T(8,128)(2,1)}), bf16[32,10,4096]{2,1,0:T(8,128)(2,1)}, u32[]{:S(2)}, u32[]{:S(2)}) %all-to-all-start) | async-done | bytes 2621472 | tf_op jit(solution)/shard_map/all_to_all | solution.py:138
  355.9 5.2 all-to-all-start.3
  361.1 13.0 %convolution_convert_fusion.3 = bf16[32,10,4096]{2,0,1:T(8,128)(2,1)} fusion(bf16[1,640,4096]{2,1,0:T(8,128)(2,1)} %all-gather.5.cloned.1.call-done, bf16[1,4096,640]{2,1,0:T(8,128)(2,1)} %all-gather.3.cloned.1.call-done, bf16[32,10,4096]{2,1,0:T(8,128)(2,1)} %all-to-all-done), kind=kOutput, calls=%fused_computation.7 | convolution fusion | flops 3357777920 | bytes 15728640 | tf_op jit(solution)/shard_map/jsh,hc->jsc/dot_general | solution.py:144
  374.1 5.3 copy.57
  379.4 78.5 %all-to-all-done.3 = bf16[32,10,4096]{2,1,0:T(8,128)(2,1)} async-done(((bf16[32,10,4096]{2,1,0:T(8,128)(2,1)}), bf16[32,10,4096]{2,1,0:T(8,128)(2,1)}, u32[]{:S(2)}, u32[]{:S(2)}) %all-to-all-start.3) | async-done | bytes 2621472 | tf_op jit(solution)/shard_map/all_to_all | solution.py:148
  457.9 4.9 all-to-all-start.1
  463.2 0.4 fusion.71
  463.6 2.0 gather_fusion
  466.0 6.3 %convolution_bitcast_fusion = f32[2,128,4096]{2,1,0:T(8,128)} fusion(bf16[32,10,4096]{2,1,0:T(8,128)(2,1)} %all-to-all-done.3, pred[1,32,20,128]{3,1,2,0:T(32,128)(4,1)S(1)} %broadcast_and_fusion, pred[1,32,20,128]{3,1,2,0:T(32,128)(4,1)S(1)} %broadcast_and_fusion.1), kind=kOutput, calls=%fused_computation.2 | convolution fusion | flops 671252480 | bytes 6979584 | tf_op jit(solution)/shard_map/kjst,jsc->ktc/dot_general | solution.py:149
  472.3 86.5 %all-to-all-done.1 = bf16[32,10,4096]{2,1,0:T(8,128)(2,1)} async-done(((bf16[32,10,4096]{2,1,0:T(8,128)(2,1)}), bf16[32,10,4096]{2,1,0:T(8,128)(2,1)}, u32[]{:S(2)}, u32[]{:S(2)}) %all-to-all-start.1) | async-done | bytes 2621472 | tf_op jit(solution)/shard_map/all_to_all | solution.py:148
  558.8 6.0 %fusion.8 = f32[2,128,4096]{2,1,0:T(8,128)S(1)} fusion(f32[2,128,4096]{2,1,0:T(8,128)} %convolution_bitcast_fusion, bf16[32,10,4096]{2,1,0:T(8,128)(2,1)} %all-to-all-done.1, pred[1,32,20,128]{3,1,2,0:T(32,128)(4,1)S(1)} %broadcast_and_fusion, pred[1,32,20,128]{3,1,2,0:T(32,128)(4,1)S(1)} %broadcast_and_fusion.1), kind=kOutput, calls=%fused_computation.16 | convolution fusion | flops 674398208 | bytes 11173888 | tf_op jit(solution)/shard_map/kjst,jsc->ktc/dot_general | solution.py:149
  564.8 1.6 fusion.22
  (91 shorter events, 3.1 us)
Async XLA Ops:
  6.5 1.6 copy-start
  6.5 253.4 %all-gather.3.cloned.1.call-start = ((), (), s32[]{:S(2)}) async-start(), calls=%async_computation.4 | async-start | bytes 5570560 | tf_op jit(solution)/shard_map/all_gather | solution.py:129
  12.9 6.7 %copy-start.2 = (f32[16,4096]{1,0:T(8,128)S(1)}, f32[16,4096]{1,0:T(8,128)}, u32[]{:S(2)}) copy-start(f32[16,4096]{1,0:T(8,128)} %param.16) | copy-start | bytes 786436
  12.9 7.5 %copy-start.19 = (f32[1,128,32]{1,2,0:T(8,128)S(1)}, f32[1,128,32]{1,2,0:T(8,128)}, u32[]{:S(2)}) copy-start(f32[1,128,32]{1,2,0:T(8,128)} %param.13) | copy-start | bytes 49156
  19.7 5.0 copy-start.3
  21.9 1.2 copy-start.8
  21.9 1.2 copy-start.9
  21.9 1.2 copy-start.15
  21.9 1.2 copy-start.16
  21.9 2.9 copy-start.5
  21.9 2.9 copy-start.6
  21.9 2.9 copy-start.7
  21.9 2.9 copy-start.11
  21.9 2.9 copy-start.12
  21.9 2.9 copy-start.13
  22.0 2.9 copy-start.14
  30.4 85.7 %copy-start.20 = (s32[1,128,2]{1,2,0:T(2,128)S(1)}, s32[1,128,2]{1,2,0:T(2,128)}, u32[]{:S(2)}) copy-start(s32[1,128,2]{1,2,0:T(2,128)} %param.19) | copy-start | bytes 3076
  30.4 86.1 %copy-start.17 = (f32[128,16]{0,1:T(8,128)S(1)}, f32[128,16]{0,1:T(8,128)}, u32[]{:S(2)}) copy-start(f32[128,16]{0,1:T(8,128)} %get-tuple-element.59) | copy-start | bytes 24580
  30.6 9.1 %collective-permute-start = (f32[17,4096]{1,0:T(8,128)S(1)}, f32[17,4096]{1,0:T(8,128)S(1)}, u32[]{:S(2)}, u32[]{:S(2)}) collective-permute-start(f32[17,4096]{1,0:T(8,128)S(1)} %pad_maximum_fusion), channel_id=1, source_target_pairs={{0,32},{32,64},{64,96},{96,128},{128,160},{160,192},{192,224},{224... | collective-permute-start | bytes 835592 | tf_op jit(solution)/shard_map/ppermute | solution.py:11
  39.7 9.1 %collective-permute-start.1 = (f32[17,4096]{1,0:T(8,128)S(1)}, f32[17,4096]{1,0:T(8,128)S(1)}, u32[]{:S(2)}, u32[]{:S(2)}) collective-permute-start(f32[17,4096]{1,0:T(8,128)S(1)} %collective-permute-done), channel_id=1, source_target_pairs={{0,32},{32,64},{64,96},{96,128},{128,160},{160,192},{192,224},{224... | collective-permute-start | bytes 835592 | tf_op jit(solution)/shard_map/ppermute | solution.py:11
  48.9 11.4 %collective-permute-start.2 = (f32[17,4096]{1,0:T(8,128)S(1)}, f32[17,4096]{1,0:T(8,128)S(1)}, u32[]{:S(2)}, u32[]{:S(2)}) collective-permute-start(f32[17,4096]{1,0:T(8,128)S(1)} %pad_maximum_fusion.1), channel_id=1, source_target_pairs={{0,64},{32,96},{64,128},{96,160},{128,192},{160,224},{192,256},{22... | collective-permute-start | bytes 835592 | tf_op jit(solution)/shard_map/ppermute | solution.py:11
  60.5 30.9 %collective-permute-start.3 = (f32[17,4096]{1,0:T(8,128)S(1)}, f32[17,4096]{1,0:T(8,128)S(1)}, u32[]{:S(2)}, u32[]{:S(2)}) collective-permute-start(f32[17,4096]{1,0:T(8,128)S(1)} %pad_maximum_fusion.2), channel_id=1, source_target_pairs={{0,128},{32,160},{64,192},{96,224},{128,256},{160,288},{192,320},{... | collective-permute-start | bytes 835592 | tf_op jit(solution)/shard_map/ppermute | solution.py:11
  91.6 23.4 %collective-permute-start.4 = (f32[17,4096]{1,0:T(8,128)S(1)}, f32[17,4096]{1,0:T(8,128)S(1)}, u32[]{:S(2)}, u32[]{:S(2)}) collective-permute-start(f32[17,4096]{1,0:T(8,128)S(1)} %pad_maximum_fusion.3), channel_id=1, source_target_pairs={{0,256},{32,288},{64,320},{96,352},{128,384},{160,416},{192,448},{... | collective-permute-start | bytes 835592 | tf_op jit(solution)/shard_map/ppermute | solution.py:11
  115.9 144.1 %all-gather.5.cloned.1.call-start = ((), (), s32[]{:S(2)}) async-start(), calls=%async_computation.5 | async-start | bytes 5570560 | tf_op jit(solution)/shard_map/all_gather | solution.py:130
  120.9 17.3 %copy-start.4 = (bf16[1,128,4096]{2,1,0:T(8,128)(2,1)S(1)}, bf16[1,128,4096]{2,1,0:T(8,128)(2,1)}, u32[]{:S(2)}) copy-start(bf16[1,128,4096]{2,1,0:T(8,128)(2,1)} %param.11) | copy-start | bytes 3145732
  120.9 17.3 %copy-start.18 = (f32[4096]{0:T(1024)S(1)}, f32[4096]{0:T(1024)}, u32[]{:S(2)}) copy-start(f32[4096]{0:T(1024)} %param.17) | copy-start | bytes 49156
  144.7 110.4 %all-to-all-start.2 = ((bf16[32,10,4096]{2,1,0:T(8,128)(2,1)}), bf16[32,10,4096]{2,1,0:T(8,128)(2,1)}, u32[]{:S(2)}, u32[]{:S(2)}) async-start(bf16[32,10,4096]{2,1,0:T(8,128)(2,1)} %copy.59), calls=%async_computation.2 | async-start | bytes 8388608 | tf_op jit(solution)/shard_map/all_to_all | solution.py:138
  255.1 100.8 %all-to-all-start = ((bf16[32,10,4096]{2,1,0:T(8,128)(2,1)}), bf16[32,10,4096]{2,1,0:T(8,128)(2,1)}, u32[]{:S(2)}, u32[]{:S(2)}) async-start(bf16[32,10,4096]{2,1,0:T(8,128)(2,1)} %copy.55), calls=%async_computation | async-start | bytes 8388608 | tf_op jit(solution)/shard_map/all_to_all | solution.py:138
  355.9 102.0 %all-to-all-start.3 = ((bf16[32,10,4096]{2,1,0:T(8,128)(2,1)}), bf16[32,10,4096]{2,1,0:T(8,128)(2,1)}, u32[]{:S(2)}, u32[]{:S(2)}) async-start(bf16[32,10,4096]{2,1,0:T(8,128)(2,1)} %copy.61), calls=%async_computation.3 | async-start | bytes 8388608 | tf_op jit(solution)/shard_map/all_to_all | solution.py:148
  379.4 83.9 %copy-start.10 = (bf16[16,4096]{1,0:T(8,128)(2,1)S(1)}, bf16[16,4096]{1,0:T(8,128)(2,1)}, u32[]{:S(2)}) copy-start(bf16[16,4096]{1,0:T(8,128)(2,1)} %param.18) | copy-start | bytes 393220
  457.9 100.9 %all-to-all-start.1 = ((bf16[32,10,4096]{2,1,0:T(8,128)(2,1)}), bf16[32,10,4096]{2,1,0:T(8,128)(2,1)}, u32[]{:S(2)}, u32[]{:S(2)}) async-start(bf16[32,10,4096]{2,1,0:T(8,128)(2,1)} %copy.57), calls=%async_computation.1 | async-start | bytes 8388608 | tf_op jit(solution)/shard_map/all_to_all | solution.py:148
  558.8 7.6 %copy-start.1 = (bf16[256,4096]{1,0:T(8,128)(2,1)S(1)}, bf16[256,4096]{1,0:T(8,128)(2,1)}, u32[]{:S(2)}) copy-start(bf16[256,4096]{1,0:T(8,128)(2,1)} %param.14) | copy-start | bytes 6291460
Sparse Core Ops, SparseCore 0:
  116.0 47.3 all-gather.2
  165.5 53.5 all-gather.4

commit v5 on v3

--- a/solution.py
+++ b/solution.py
@@ -11,17 +11,27 @@
     return lax.ppermute(value, axis, pairs)
 
 
+def compose(a_neg, older, newer):
+    total = older[0] + newer[0]
+    state = jnp.exp(a_neg * newer[0][None, :]) * older[1:] + newer[1:]
+    return jnp.concatenate([total[None], state], axis=0)
+
+
 def carry_in(a_neg, total_delta, end_state):
     count = lax.axis_size("seq")
-    packed = from_behind(jnp.concatenate([total_delta[None], end_state], axis=0), "seq", 1)
-    covered = 1
-    while covered < count - 1:
-        older = from_behind(packed, "seq", covered)
-        mine = packed[0]
-        state = jnp.exp(a_neg * mine[None, :]) * older[1:] + packed[1:]
-        packed = jnp.concatenate([(older[0] + mine)[None], state], axis=0)
-        covered *= 2
-    return packed[1:]
+    radix = 4
+    packed = jnp.concatenate([total_delta[None], end_state], axis=0)
+    pieces = [from_behind(packed, "seq", k) for k in range(radix, 0, -1)]
+    covered = radix
+    while True:
+        merged = pieces[0]
+        for piece in pieces[1:]:
+            merged = compose(a_neg, merged, piece)
+        if covered >= count - 1:
+            return merged[1:]
+        pieces = [from_behind(merged, "seq", k * covered) for k in range(radix - 1, 0, -1)]
+        pieces.append(merged)
+        covered *= radix
 
 
 def sweep_kernel(delta_ref, driven_ref, a_ref, start_ref, b_ref, c_ref, y_ref):
@@ -124,30 +134,27 @@
     hit = [
         (dest == picks[None, None, :, c]) & (slot == position[None, None, :, c]) for c in range(2)
     ]
-    dispatch = (hit[0] | hit[1]).astype(jnp.bfloat16)
-    outgoing = jnp.einsum(
-        "jst,tc->jsc", dispatch, mixer, preferred_element_type=jnp.float32
-    ).astype(jnp.bfloat16)
+    rows_out = owners * capacity
+    dispatch = (hit[0] | hit[1]).astype(jnp.bfloat16).reshape(rows_out, tokens_here)
+    outgoing = jnp.dot(dispatch, mixer, preferred_element_type=jnp.float32).astype(jnp.bfloat16)
     incoming = lax.all_to_all(outgoing, "exp", split_axis=0, concat_axis=0, tiled=True)
-    pre_hidden = jnp.einsum(
-        "jsc,ch->jsh",
+    pre_hidden = jnp.dot(
         incoming,
         lax.all_gather(w_up, "seq", axis=1, tiled=True)[0],
         preferred_element_type=jnp.float32,
     )
     hidden = jax.nn.silu(pre_hidden).astype(jnp.bfloat16)
     partial_out = lax.optimization_barrier(
-        jnp.einsum(
-            "jsh,hc->jsc",
+        jnp.dot(
             hidden,
             lax.all_gather(w_down, "seq", axis=2, tiled=True)[0],
             preferred_element_type=jnp.float32,
         ).astype(jnp.bfloat16)
     )
     returned = lax.all_to_all(partial_out, "exp", split_axis=0, concat_axis=0, tiled=True)
-    gather = jnp.stack(hit).astype(jnp.bfloat16)
+    gather = jnp.stack(hit).astype(jnp.bfloat16).reshape(2, rows_out, tokens_here)
     picked = jnp.einsum(
-        "kjst,jsc->ktc", gather, returned, preferred_element_type=jnp.float32
+        "kqt,qc->ktc", gather, returned, preferred_element_type=jnp.float32
     ).astype(jnp.bfloat16).astype(jnp.float32)
     routed = first[:, None] * picked[0] + second[:, None] * picked[1]
     return (mixer.astype(jnp.float32) + routed).astype(jnp.bfloat16)[None]

time: 494 us -> 514 us (1.040)
  the two profiles are of different devices: /device:TPU:47 before, /device:TPU:7 now
where the time goes in v5:
time: 514 us; the launch traced here: 513 us
  waiting for transfers between devices  337 us (66%)
  starting transfers between devices  58 us (11%)
  local copies, waits for them, and re-layouts  36.6 us (7%)
  matrix products  32.4 us (6%)
  other arithmetic  17.7 us (3%)
  Pallas kernels  17.3 us (3%)
  between operations  14 us (3%)
    all_to_all x1, waiting for transfers between devices, per_device(): lax.all_to_all(outgoing, 'exp', split_axis=0, concat_axis=0, tiled=True)  144 us
    all_to_all x1, waiting for transfers between devices, per_device(): lax.all_to_all(partial_out, 'exp', split_axis=0, concat_axis=0, tiled=True)  141 us
    ppermute x7, waiting for transfers between devices, from_behind(): return lax.ppermute(value, axis, pairs)  51.5 us
    ppermute x7, starting transfers between devices, from_behind(): return lax.ppermute(value, axis, pairs)  36.5 us
    pallas_call x1, Pallas kernels, sweep(): pl.pallas_call(sweep_kernel, out_shape=jax.ShapeDtypeStruct((tokens_here,...  17.3 us
    all_to_all x2, local copies, waits for them, and re-layouts, per_device(): lax.all_to_all(outgoing, 'exp', split_axis=0, concat_axis=0, tiled=True)  15.6 us
    all_to_all x1, starting transfers between devices, per_device(): lax.all_to_all(outgoing, 'exp', split_axis=0, concat_axis=0, tiled=True)  12.9 us
  transfers between devices with their start and end apart: 11, of which 8 were waited for; matrix products, arithmetic and copies ran while one was open for 4% of the time, Pallas kernels for 3%

profile of v5, /device:TPU:7, one launch (start us, length us, event | category | flops | bytes accessed | tf_op | source)
XLA Modules:
  0.0 512.8 jit_solution(13187932265635551798)
XLA Ops:
  6.5 1.6 copy-done
  8.1 4.8 convert_multiply_fusion.1
  12.9 3.5 reduce_window_sum.26
  16.4 0.6 fusion.44
  17.0 2.6 fusion.45
  19.7 0.7 fusion.46
  20.4 0.6 slice_bitcast_fusion.2
  21.0 0.8 copy.43
  21.9 1.0 slice_subtract_fusion.2
  23.0 1.7 multiply_reduce_fusion.1
  24.8 5.5 %multiply_reduce_fusion = (f32[16,512]{1,0:T(8,128)S(1)}, f32[16,512]{1,0:T(8,128)S(1)}, f32[16,512]{1,0:T(8,128)S(1)}, f32[16,512]{1,0:T(8,128)S(1)}, f32[16,512]{1,0:T(8,128)S(1)}, /*index=5*/f32[16,512]{1,0:T(8,128)S(1)}) fusion(f32[128,512]{1,0:T(8,128)S(1)} %get-tuple-element.42, f32[128,512]{1,0:T(8,128)S(1)} %get-tuple-element.26, ...), kind=kLoop, calls=%fused_computation.13 | loop fusion | flops 25116672 | bytes 3547136 | tf_op jit(solution)/shard_map/reduce_sum | solution.py:110
  30.5 4.2 collective-permute-start
  34.8 6.3 %collective-permute-start.1 = (f32[17,4096]{1,0:T(8,128)S(1)}, f32[17,4096]{1,0:T(8,128)S(1)}, u32[]{:S(2)}, u32[]{:S(2)}) collective-permute-start(f32[17,4096]{1,0:T(8,128)S(1)} %pad_maximum_fusion), channel_id=1, source_target_pairs={{0,96},{32,128},{64,160},{96,192},{128,224},{160,256},{192,288},{2... | collective-permute-start | bytes 835592 | tf_op jit(solution)/shard_map/ppermute | solution.py:11
  41.1 2.3 collective-permute-start.2
  43.4 2.1 collective-permute-start.3
  45.5 5.5 %collective-permute-done.1 = f32[17,4096]{1,0:T(8,128)S(1)} collective-permute-done((f32[17,4096]{1,0:T(8,128)S(1)}, f32[17,4096]{1,0:T(8,128)S(1)}, u32[]{:S(2)}, u32[]{:S(2)}) %collective-permute-start.1) | collective-permute-done | bytes 278560 | tf_op jit(solution)/shard_map/ppermute | solution.py:11
  51.0 8.4 %collective-permute-done.2 = f32[17,4096]{1,0:T(8,128)S(1)} collective-permute-done((f32[17,4096]{1,0:T(8,128)S(1)}, f32[17,4096]{1,0:T(8,128)S(1)}, u32[]{:S(2)}, u32[]{:S(2)}) %collective-permute-start.2) | collective-permute-done | bytes 278560 | tf_op jit(solution)/shard_map/ppermute | solution.py:11
  59.4 5.4 %collective-permute-done.3 = f32[17,4096]{1,0:T(8,128)S(1)} collective-permute-done((f32[17,4096]{1,0:T(8,128)S(1)}, f32[17,4096]{1,0:T(8,128)S(1)}, u32[]{:S(2)}, u32[]{:S(2)}) %collective-permute-start.3) | collective-permute-done | bytes 278560 | tf_op jit(solution)/shard_map/ppermute | solution.py:11
  64.8 0.2 slice_add_fusion.2
  65.1 18.0 %collective-permute-start.4 = (f32[17,4096]{1,0:T(8,128)S(1)}, f32[17,4096]{1,0:T(8,128)S(1)}, u32[]{:S(2)}, u32[]{:S(2)}) collective-permute-start(f32[17,4096]{1,0:T(8,128)S(1)} %pad_maximum_fusion.1), channel_id=1, source_target_pairs={{0,128},{32,160},{64,192},{96,224},{128,256},{160,288},{192,320},{... | collective-permute-start | bytes 835592 | tf_op jit(solution)/shard_map/ppermute | solution.py:11
  83.1 2.3 collective-permute-start.5
  85.4 1.3 collective-permute-start.6
  86.7 4.9 collective-permute-done.4
  91.6 8.5 %collective-permute-done.5 = f32[17,4096]{1,0:T(8,128)S(1)} collective-permute-done((f32[17,4096]{1,0:T(8,128)S(1)}, f32[17,4096]{1,0:T(8,128)S(1)}, u32[]{:S(2)}, u32[]{:S(2)}) %collective-permute-start.5) | collective-permute-done | bytes 278560 | tf_op jit(solution)/shard_map/ppermute | solution.py:11
  100.1 18.8 %collective-permute-done.6 = f32[17,4096]{1,0:T(8,128)S(1)} collective-permute-done((f32[17,4096]{1,0:T(8,128)S(1)}, f32[17,4096]{1,0:T(8,128)S(1)}, u32[]{:S(2)}, u32[]{:S(2)}) %collective-permute-start.6) | collective-permute-done | bytes 278560 | tf_op jit(solution)/shard_map/ppermute | solution.py:11
  118.9 0.9 fusion.25.start_ref
  120.4 0.6 reduce-window.6
  120.9 0.2 slice_reduce_fusion.4
  122.0 1.3 broadcast_in_dim.11.b_ref
  123.3 1.3 broadcast_in_dim.13.c_ref
  124.7 17.3 %shard_map.109 = f32[128,4096]{1,0:T(8,128)} custom-call(f32[128,4096]{1,0:T(8,128)} %get-tuple-element.66.delta_ref, f32[128,4096]{1,0:T(8,128)} %get-tuple-element.65.driven_ref, f32[16,4096]{1,0:T(8,128)} %copy-done.3, f32[16,4096]{1,0:T(8,128)} %fusion.25.start_ref, f32[128,16,128]{2,1,0:T(8,128)} %broadcast_in_dim.11.b_ref, ...), custom_call_target="tpu_custom_call" | custom-call | flops 67108864 | bytes 6815744 | tf_op jit(solution)/shard_map/pallas_call | solution.py:73
  142.0 1.9 fusion.12
  143.9 3.8 convolution_convert_fusion.1
  147.7 7.7 %all_to_all.14 = bf16[32,20,4096]{2,1,0:T(8,128)(2,1)} reshape(bf16[640,4096]{1,0:T(8,128)(2,1)} %convolution_convert_fusion.1) | data formatting | bytes 10485760 | tf_op jit(solution)/shard_map/all_to_all | solution.py:140
  155.5 12.9 %all-to-all-start = ((bf16[32,20,4096]{2,1,0:T(8,128)(2,1)}), bf16[32,20,4096]{2,1,0:T(8,128)(2,1)}, u32[]{:S(2)}, u32[]{:S(2)}) async-start(bf16[32,20,4096]{2,1,0:T(8,128)(2,1)} %all_to_all.14), calls=%async_computation | async-start | bytes 12582912 | tf_op jit(solution)/shard_map/all_to_all | solution.py:140
  168.4 0.7 all-gather.5.cloned.1.call-update
  169.1 143.6 %all-to-all-done = bf16[32,20,4096]{2,1,0:T(8,128)(2,1)} async-done(((bf16[32,20,4096]{2,1,0:T(8,128)(2,1)}), bf16[32,20,4096]{2,1,0:T(8,128)(2,1)}, u32[]{:S(2)}, u32[]{:S(2)}) %all-to-all-start) | async-done | bytes 5242912 | tf_op jit(solution)/shard_map/all_to_all | solution.py:140
  312.7 7.8 %all_to_all.16 = bf16[640,4096]{1,0:T(8,128)(2,1)} reshape(bf16[32,20,4096]{2,1,0:T(8,128)(2,1)} %all-to-all-done) | data formatting | bytes 10485760 | tf_op jit(solution)/shard_map/all_to_all | solution.py:140
  320.5 8.4 %multiply_convert_fusion = bf16[640,640]{1,0:T(8,128)(2,1)S(1)} fusion(bf16[640,4096]{1,0:T(8,128)(2,1)} %all_to_all.16, bf16[1,4096,640]{2,1,0:T(8,128)(2,1)} %all-gather.3.cloned.1.call-done), kind=kOutput, calls=%fused_computation.32 | convolution fusion | flops 3357491200 | bytes 11304960 | tf_op jit(solution)/shard_map/dot_general | solution.py:141
  328.9 8.5 %convolution_convert_fusion = bf16[640,4096]{1,0:T(8,128)(2,1)} fusion(bf16[640,640]{1,0:T(8,128)(2,1)S(1)} %multiply_convert_fusion, bf16[1,640,4096]{2,1,0:T(8,128)(2,1)} %all-gather.5.cloned.1.call-done), kind=kOutput, calls=%fused_computation.1 | convolution fusion | flops 3358064640 | bytes 11304960 | tf_op jit(solution)/shard_map/dot_general | solution.py:148
  337.4 7.7 %all_to_all.17 = bf16[32,20,4096]{2,1,0:T(8,128)(2,1)} reshape(bf16[640,4096]{1,0:T(8,128)(2,1)} %convolution_convert_fusion) | data formatting | bytes 10485760 | tf_op jit(solution)/shard_map/all_to_all | solution.py:154
  345.1 8.6 %all-to-all-start.1 = ((bf16[32,20,4096]{2,1,0:T(8,128)(2,1)}), bf16[32,20,4096]{2,1,0:T(8,128)(2,1)}, u32[]{:S(2)}, u32[]{:S(2)}) async-start(bf16[32,20,4096]{2,1,0:T(8,128)(2,1)} %all_to_all.17), calls=%async_computation.1 | async-start | bytes 12582912 | tf_op jit(solution)/shard_map/all_to_all | solution.py:154
  354.0 0.4 fusion.47
  354.4 2.0 gather_fusion
  356.6 0.2 fusion.43
  356.8 141.0 %all-to-all-done.1 = bf16[32,20,4096]{2,1,0:T(8,128)(2,1)} async-done(((bf16[32,20,4096]{2,1,0:T(8,128)(2,1)}), bf16[32,20,4096]{2,1,0:T(8,128)(2,1)}, u32[]{:S(2)}, u32[]{:S(2)}) %all-to-all-start.1) | async-done | bytes 5242912 | tf_op jit(solution)/shard_map/all_to_all | solution.py:154
  497.8 6.6 %fusion.8 = f32[2,128,4096]{2,1,0:T(8,128)S(1)} fusion(bf16[32,20,4096]{2,1,0:T(8,128)(2,1)} %all-to-all-done.1, pred[1,32,20,128]{3,1,2,0:T(32,128)(4,1)S(1)} %broadcast_and_fusion, pred[1,32,20,128]{3,1,2,0:T(32,128)(4,1)S(1)} %broadcast_and_fusion.1), kind=kOutput, calls=%fused_computation.11 | convolution fusion | flops 1344438272 | bytes 9601024 | tf_op jit(solution)/shard_map/kqt,qc->ktc/dot_general | solution.py:156
  504.4 1.5 fusion.20
  (86 shorter events, 2.3 us)
Async XLA Ops:
  6.5 1.6 copy-start
  6.5 314.0 %all-gather.3.cloned.1.call-start = ((), (), s32[]{:S(2)}) async-start(), calls=%async_computation.2 | async-start | bytes 5570560 | tf_op jit(solution)/shard_map/all_gather | solution.py:143
  12.9 6.8 %copy-start.2 = (f32[16,4096]{1,0:T(8,128)S(1)}, f32[16,4096]{1,0:T(8,128)}, u32[]{:S(2)}) copy-start(f32[16,4096]{1,0:T(8,128)} %param.16) | copy-start | bytes 786436
  12.9 7.5 %copy-start.19 = (f32[1,128,32]{1,2,0:T(8,128)S(1)}, f32[1,128,32]{1,2,0:T(8,128)}, u32[]{:S(2)}) copy-start(f32[1,128,32]{1,2,0:T(8,128)} %param.13) | copy-start | bytes 49156
  19.7 5.1 copy-start.3
  21.8 1.2 copy-start.8
  21.8 1.2 copy-start.9
  21.9 1.2 copy-start.15
  21.9 1.2 copy-start.16
  21.9 2.9 copy-start.5
  21.9 2.9 copy-start.6
  21.9 2.9 copy-start.7
  21.9 2.9 copy-start.11
  21.9 2.9 copy-start.12
  21.9 2.9 copy-start.13
  21.9 2.9 copy-start.14
  30.4 89.4 %copy-start.20 = (s32[1,128,2]{1,2,0:T(2,128)S(1)}, s32[1,128,2]{1,2,0:T(2,128)}, u32[]{:S(2)}) copy-start(s32[1,128,2]{1,2,0:T(2,128)} %param.19) | copy-start | bytes 3076
  30.4 89.8 %copy-start.17 = (f32[128,16]{0,1:T(8,128)S(1)}, f32[128,16]{0,1:T(8,128)}, u32[]{:S(2)}) copy-start(f32[128,16]{0,1:T(8,128)} %get-tuple-element.61) | copy-start | bytes 24580
  30.5 14.9 %collective-permute-start = (f32[17,4096]{1,0:T(8,128)S(1)}, f32[17,4096]{1,0:T(8,128)S(1)}, u32[]{:S(2)}, u32[]{:S(2)}) collective-permute-start(f32[17,4096]{1,0:T(8,128)S(1)} %pad_maximum_fusion), channel_id=1, source_target_pairs={{0,128},{32,160},{64,192},{96,224},{128,256},{160,288},{192,320},{... | collective-permute-start | bytes 835592 | tf_op jit(solution)/shard_map/ppermute | solution.py:11
  34.8 16.2 %collective-permute-start.1 = (f32[17,4096]{1,0:T(8,128)S(1)}, f32[17,4096]{1,0:T(8,128)S(1)}, u32[]{:S(2)}, u32[]{:S(2)}) collective-permute-start(f32[17,4096]{1,0:T(8,128)S(1)} %pad_maximum_fusion), channel_id=1, source_target_pairs={{0,96},{32,128},{64,160},{96,192},{128,224},{160,256},{192,288},{2... | collective-permute-start | bytes 835592 | tf_op jit(solution)/shard_map/ppermute | solution.py:11
  41.1 18.4 %collective-permute-start.2 = (f32[17,4096]{1,0:T(8,128)S(1)}, f32[17,4096]{1,0:T(8,128)S(1)}, u32[]{:S(2)}, u32[]{:S(2)}) collective-permute-start(f32[17,4096]{1,0:T(8,128)S(1)} %pad_maximum_fusion), channel_id=1, source_target_pairs={{0,64},{32,96},{64,128},{96,160},{128,192},{160,224},{192,256},{22... | collective-permute-start | bytes 835592 | tf_op jit(solution)/shard_map/ppermute | solution.py:11
  43.4 21.4 %collective-permute-start.3 = (f32[17,4096]{1,0:T(8,128)S(1)}, f32[17,4096]{1,0:T(8,128)S(1)}, u32[]{:S(2)}, u32[]{:S(2)}) collective-permute-start(f32[17,4096]{1,0:T(8,128)S(1)} %pad_maximum_fusion), channel_id=1, source_target_pairs={{0,32},{32,64},{64,96},{96,128},{128,160},{160,192},{192,224},{224... | collective-permute-start | bytes 835592 | tf_op jit(solution)/shard_map/ppermute | solution.py:11
  65.1 26.5 %collective-permute-start.4 = (f32[17,4096]{1,0:T(8,128)S(1)}, f32[17,4096]{1,0:T(8,128)S(1)}, u32[]{:S(2)}, u32[]{:S(2)}) collective-permute-start(f32[17,4096]{1,0:T(8,128)S(1)} %pad_maximum_fusion.1), channel_id=1, source_target_pairs={{0,128},{32,160},{64,192},{96,224},{128,256},{160,288},{192,320},{... | collective-permute-start | bytes 835592 | tf_op jit(solution)/shard_map/ppermute | solution.py:11
  83.1 16.9 %collective-permute-start.5 = (f32[17,4096]{1,0:T(8,128)S(1)}, f32[17,4096]{1,0:T(8,128)S(1)}, u32[]{:S(2)}, u32[]{:S(2)}) collective-permute-start(f32[17,4096]{1,0:T(8,128)S(1)} %pad_maximum_fusion.1), channel_id=1, source_target_pairs={{0,256},{32,288},{64,320},{96,352},{128,384},{160,416},{192,448},{... | collective-permute-start | bytes 835592 | tf_op jit(solution)/shard_map/ppermute | solution.py:11
  85.4 33.5 %collective-permute-start.6 = (f32[17,4096]{1,0:T(8,128)S(1)}, f32[17,4096]{1,0:T(8,128)S(1)}, u32[]{:S(2)}, u32[]{:S(2)}) collective-permute-start(f32[17,4096]{1,0:T(8,128)S(1)} %pad_maximum_fusion.1), channel_id=1, source_target_pairs={{0,384},{32,416},{64,448},{96,480},{1,385},{33,417},{65,449},{97,4... | collective-permute-start | bytes 835592 | tf_op jit(solution)/shard_map/ppermute | solution.py:11
  124.7 17.3 %copy-start.4 = (bf16[1,128,4096]{2,1,0:T(8,128)(2,1)S(1)}, bf16[1,128,4096]{2,1,0:T(8,128)(2,1)}, u32[]{:S(2)}) copy-start(bf16[1,128,4096]{2,1,0:T(8,128)(2,1)} %param.11) | copy-start | bytes 3145732
  124.7 17.3 %copy-start.18 = (f32[4096]{0:T(1024)S(1)}, f32[4096]{0:T(1024)}, u32[]{:S(2)}) copy-start(f32[4096]{0:T(1024)} %param.17) | copy-start | bytes 49156
  155.5 157.2 %all-to-all-start = ((bf16[32,20,4096]{2,1,0:T(8,128)(2,1)}), bf16[32,20,4096]{2,1,0:T(8,128)(2,1)}, u32[]{:S(2)}, u32[]{:S(2)}) async-start(bf16[32,20,4096]{2,1,0:T(8,128)(2,1)} %all_to_all.14), calls=%async_computation | async-start | bytes 12582912 | tf_op jit(solution)/shard_map/all_to_all | solution.py:140
  168.3 160.6 %all-gather.5.cloned.1.call-start = ((), (), s32[]{:S(2)}) async-start(), calls=%async_computation.3 | async-start | bytes 5570560 | tf_op jit(solution)/shard_map/all_gather | solution.py:150
  345.1 8.9 %copy-start.10 = (bf16[16,4096]{1,0:T(8,128)(2,1)S(1)}, bf16[16,4096]{1,0:T(8,128)(2,1)}, u32[]{:S(2)}) copy-start(bf16[16,4096]{1,0:T(8,128)(2,1)} %param.18) | copy-start | bytes 393220
  345.1 152.7 %all-to-all-start.1 = ((bf16[32,20,4096]{2,1,0:T(8,128)(2,1)}), bf16[32,20,4096]{2,1,0:T(8,128)(2,1)}, u32[]{:S(2)}, u32[]{:S(2)}) async-start(bf16[32,20,4096]{2,1,0:T(8,128)(2,1)} %all_to_all.17), calls=%async_computation.1 | async-start | bytes 12582912 | tf_op jit(solution)/shard_map/all_to_all | solution.py:154
  497.8 8.2 %copy-start.1 = (bf16[256,4096]{1,0:T(8,128)(2,1)S(1)}, bf16[256,4096]{1,0:T(8,128)(2,1)}, u32[]{:S(2)}) copy-start(bf16[256,4096]{1,0:T(8,128)(2,1)} %param.14) | copy-start | bytes 6291460
Sparse Core Ops, SparseCore 0:
  119.9 49.3 all-gather.2
  171.4 54.3 all-gather.4

commit v6 on v3

--- a/solution.py
+++ b/solution.py
@@ -13,15 +13,14 @@
 
 def carry_in(a_neg, total_delta, end_state):
     count = lax.axis_size("seq")
-    packed = from_behind(jnp.concatenate([total_delta[None], end_state], axis=0), "seq", 1)
-    covered = 1
-    while covered < count - 1:
-        older = from_behind(packed, "seq", covered)
-        mine = packed[0]
-        state = jnp.exp(a_neg * mine[None, :]) * older[1:] + packed[1:]
-        packed = jnp.concatenate([(older[0] + mine)[None], state], axis=0)
-        covered *= 2
-    return packed[1:]
+    me = lax.axis_index("seq")
+    packed = jnp.concatenate([total_delta[None], end_state], axis=0)
+    every = lax.all_gather(packed, "seq")
+    state = jnp.zeros_like(end_state)
+    for k in range(count - 1):
+        folded = jnp.exp(a_neg * every[k, 0][None, :]) * state + every[k, 1:]
+        state = jnp.where(k < me, folded, state)
+    return state
 
 
 def sweep_kernel(delta_ref, driven_ref, a_ref, start_ref, b_ref, c_ref, y_ref):

time: 494 us -> 468 us (0.947)
  the two profiles are of different devices: /device:TPU:47 before, /device:TPU:7 now
where the time goes in v6:
time: 468 us
  waiting for transfers between devices  339 us (72%)
  matrix products  29.1 us (6%)
  local copies, waits for them, and re-layouts  26.1 us (6%)
  other arithmetic  21.7 us (5%)
  starting transfers between devices  20.6 us (4%)
  Pallas kernels  17.3 us (4%)
  between operations  13.6 us (3%)
    all_to_all x1, waiting for transfers between devices, per_device(): lax.all_to_all(partial_out, 'exp', split_axis=0, concat_axis=0, tiled=True)  141 us
    all_to_all x1, waiting for transfers between devices, per_device(): lax.all_to_all(outgoing, 'exp', split_axis=0, concat_axis=0, tiled=True)  141 us
    all_gather x1, waiting for transfers between devices, carry_in(): every = lax.all_gather(packed, 'seq')  53.4 us
    pallas_call x1, Pallas kernels, sweep(): pl.pallas_call(sweep_kernel, out_shape=jax.ShapeDtypeStruct((tokens_here,...  17.3 us
    all_to_all x1, starting transfers between devices, per_device(): lax.all_to_all(partial_out, 'exp', split_axis=0, concat_axis=0, tiled=True)  10.1 us
    all_to_all x1, starting transfers between devices, per_device(): lax.all_to_all(outgoing, 'exp', split_axis=0, concat_axis=0, tiled=True)  9.98 us
  transfers between devices with their start and end apart: 5, of which 4 were waited for; matrix products, arithmetic and copies ran while one was open for 5% of the time, Pallas kernels for 4%

profile of v6, /device:TPU:7, one launch (start us, length us, event | category | flops | bytes accessed | tf_op | source)
XLA Modules:
  0.0 467.7 jit_solution(7045669504644995519)
XLA Ops:
  6.5 1.6 copy-done
  8.1 4.8 %convert_multiply_fusion.1 = (f32[128,4096]{1,0:T(8,128)}, f32[128,4096]{1,0:T(8,128)}) fusion(bf16[1,128,4096]{2,1,0:T(8,128)(2,1)} %param.11, f32[4096]{0:T(1024)} %param.15, bf16[256,4096]{1,0:T(8,128)(2,1)S(1)} %copy-done, bf16[1,128,256]{2,1,0:T(8,128)(2,1)} %param.12), kind=kOutput, calls=%fused_computation.22 | convolution fusion | flops 273154048 | bytes 7421952 | tf_op jit(solution)/shard_map/dot_general | solution.py:83
  12.9 3.5 reduce_window_sum.26
  16.4 0.6 fusion.77
  17.0 2.6 fusion.78
  19.7 0.8 fusion.79
  20.5 0.6 slice_bitcast_fusion.17
  21.1 0.8 copy.43
  22.0 1.0 slice_subtract_fusion.2
  23.0 1.7 multiply_reduce_fusion.1
  24.9 5.5 %multiply_reduce_fusion = (f32[16,512]{1,0:T(8,128)S(1)}, f32[16,512]{1,0:T(8,128)S(1)}, f32[16,512]{1,0:T(8,128)S(1)}, f32[16,512]{1,0:T(8,128)S(1)}, f32[16,512]{1,0:T(8,128)S(1)}, /*index=5*/f32[16,512]{1,0:T(8,128)S(1)}) fusion(f32[128,512]{1,0:T(8,128)S(1)} %get-tuple-element.57, f32[128,512]{1,0:T(8,128)S(1)} %get-tuple-element.41, ...), kind=kLoop, calls=%fused_computation.13 | loop fusion | flops 25116672 | bytes 3547136 | tf_op jit(solution)/shard_map/reduce_sum | solution.py:99
  30.5 0.8 maximum_bitcast_fusion
  31.3 0.2 all-gather.6.cloned.1.call-start
  31.6 53.4 %all-gather.10.cloned.1.call-done = f32[16,17,4096]{2,1,0:T(8,128)} async-done(((f32[1,17,4096]{2,1,0:T(8,128)}), f32[16,17,4096]{2,1,0:T(8,128)}) %all-gather.10.cloned.1.call-update) | async-done | bytes 4456464 | tf_op jit(solution)/shard_map/all_gather | solution.py:18
  85.0 1.7 fusion.76
  86.7 4.5 fusion.30.start_ref
  91.2 0.1 copy.46
  91.3 0.1 eq.114
  91.5 0.1 eq.110
  91.7 0.6 reduce-window.6
  92.3 0.2 slice_reduce_fusion.4
  92.7 0.1 sub.138
  92.8 0.2 slice_reduce_fusion.2
  93.0 0.2 slice_reduce_fusion.3
  93.3 1.3 broadcast_in_dim.14.b_ref
  94.6 1.3 broadcast_in_dim.16.c_ref
  95.9 17.3 %shard_map.109 = f32[128,4096]{1,0:T(8,128)} custom-call(f32[128,4096]{1,0:T(8,128)} %get-tuple-element.77.delta_ref, f32[128,4096]{1,0:T(8,128)} %get-tuple-element.76.driven_ref, f32[16,4096]{1,0:T(8,128)} %copy-done.3, f32[16,4096]{1,0:T(8,128)} %fusion.30.start_ref, f32[128,16,128]{2,1,0:T(8,128)} %broadcast_in_dim.14.b_ref, ...), custom_call_target="tpu_custom_call" | custom-call | flops 67108864 | bytes 6815744 | tf_op jit(solution)/shard_map/pallas_call | solution.py:62
  113.3 1.9 fusion.12
  115.2 1.5 convolution_convert_fusion.1
  116.7 5.6 %copy.51 = bf16[32,20,4096]{2,1,0:T(8,128)(2,1)} copy(bf16[32,20,4096]{2,0,1:T(8,128)(2,1)S(1)} %convolution_convert_fusion.1) | data formatting | bytes 10485760 | tf_op jit(solution)/shard_map/convert_element_type | solution.py:129
  122.3 10.0 %all-to-all-start = ((bf16[32,20,4096]{2,1,0:T(8,128)(2,1)}), bf16[32,20,4096]{2,1,0:T(8,128)(2,1)}, u32[]{:S(2)}, u32[]{:S(2)}) async-start(bf16[32,20,4096]{2,1,0:T(8,128)(2,1)} %copy.51), calls=%async_computation | async-start | bytes 12582912 | tf_op jit(solution)/shard_map/all_to_all | solution.py:130
  132.3 0.3 all-gather.8.cloned.1.call-start
  132.5 0.5 all-gather.8.cloned.1.call-update
  133.0 3.2 all-gather.6.cloned.1.call-done
  136.2 141.0 %all-to-all-done = bf16[32,20,4096]{2,1,0:T(8,128)(2,1)} async-done(((bf16[32,20,4096]{2,1,0:T(8,128)(2,1)}), bf16[32,20,4096]{2,1,0:T(8,128)(2,1)}, u32[]{:S(2)}, u32[]{:S(2)}) %all-to-all-start) | async-done | bytes 5242912 | tf_op jit(solution)/shard_map/all_to_all | solution.py:130
  277.2 8.9 %multiply_convert_fusion = bf16[32,20,640]{2,1,0:T(8,128)(2,1)S(1)} fusion(bf16[32,20,4096]{2,1,0:T(8,128)(2,1)} %all-to-all-done, bf16[1,4096,640]{2,1,0:T(8,128)(2,1)} %all-gather.6.cloned.1.call-done), kind=kOutput, calls=%fused_computation.32 | convolution fusion | flops 3357491200 | bytes 11304960 | tf_op jit(solution)/shard_map/jsc,ch->jsh/dot_general | solution.py:131
  286.0 6.9 %convolution_convert_fusion = bf16[32,20,4096]{2,0,1:T(8,128)(2,1)S(1)} fusion(bf16[1,640,4096]{2,1,0:T(8,128)(2,1)} %all-gather.8.cloned.1.call-done, bf16[32,20,640]{2,1,0:T(8,128)(2,1)S(1)} %multiply_convert_fusion), kind=kOutput, calls=%fused_computation.1 | convolution fusion | flops 3358064640 | bytes 11304960 | tf_op jit(solution)/shard_map/jsh,hc->jsc/dot_general | solution.py:139
  293.0 5.6 %copy.53 = bf16[32,20,4096]{2,1,0:T(8,128)(2,1)} copy(bf16[32,20,4096]{2,0,1:T(8,128)(2,1)S(1)} %convolution_convert_fusion) | data formatting | bytes 10485760 | tf_op jit(solution)/shard_map/optimization_barrier | solution.py:138
  298.6 10.1 %all-to-all-start.1 = ((bf16[32,20,4096]{2,1,0:T(8,128)(2,1)}), bf16[32,20,4096]{2,1,0:T(8,128)(2,1)}, u32[]{:S(2)}, u32[]{:S(2)}) async-start(bf16[32,20,4096]{2,1,0:T(8,128)(2,1)} %copy.53), calls=%async_computation.1 | async-start | bytes 12582912 | tf_op jit(solution)/shard_map/all_to_all | solution.py:146
  308.7 0.1 copy.47
  308.8 0.1 reshape.297
  309.1 0.4 fusion.80
  309.5 2.0 gather_fusion
  311.5 0.1 reshape.300
  311.6 0.2 fusion.75
  311.8 141.2 %all-to-all-done.1 = bf16[32,20,4096]{2,1,0:T(8,128)(2,1)} async-done(((bf16[32,20,4096]{2,1,0:T(8,128)(2,1)}), bf16[32,20,4096]{2,1,0:T(8,128)(2,1)}, u32[]{:S(2)}, u32[]{:S(2)}) %all-to-all-start.1) | async-done | bytes 5242912 | tf_op jit(solution)/shard_map/all_to_all | solution.py:146
  453.0 6.6 %fusion.8 = f32[2,128,4096]{2,1,0:T(8,128)S(1)} fusion(bf16[32,20,4096]{2,1,0:T(8,128)(2,1)} %all-to-all-done.1, pred[1,32,20,128]{3,1,2,0:T(32,128)(4,1)S(1)} %broadcast_and_fusion, pred[1,32,20,128]{3,1,2,0:T(32,128)(4,1)S(1)} %broadcast_and_fusion.1), kind=kOutput, calls=%fused_computation.11 | convolution fusion | flops 1344438272 | bytes 9601024 | tf_op jit(solution)/shard_map/kjst,jsc->ktc/dot_general | solution.py:148
  459.7 1.5 fusion.20
  (68 shorter events, 0.7 us)
Async XLA Ops:
  6.5 1.6 copy-start
  6.5 78.5 %all-gather.10.cloned.1.call-start = ((), (), s32[]{:S(2)}) async-start(), calls=%async_computation.4 | async-start | bytes 6684672 | tf_op jit(solution)/shard_map/all_gather | solution.py:18
  12.9 6.7 %copy-start.2 = (f32[16,4096]{1,0:T(8,128)S(1)}, f32[16,4096]{1,0:T(8,128)}, u32[]{:S(2)}) copy-start(f32[16,4096]{1,0:T(8,128)} %param.16) | copy-start | bytes 786436
  12.9 7.6 %copy-start.19 = (f32[1,128,32]{1,2,0:T(8,128)S(1)}, f32[1,128,32]{1,2,0:T(8,128)}, u32[]{:S(2)}) copy-start(f32[1,128,32]{1,2,0:T(8,128)} %param.13) | copy-start | bytes 49156
  19.7 5.1 %copy-start.3 = (f32[16,4096]{1,0:T(8,128)}, f32[16,4096]{1,0:T(8,128)S(1)}, u32[]{:S(2)}) copy-start(f32[16,4096]{1,0:T(8,128)S(1)} %exponential_negate_fusion.a_ref) | copy-start | bytes 786436
  21.9 1.2 copy-start.8
  21.9 1.2 copy-start.9
  21.9 1.2 copy-start.15
  21.9 1.2 copy-start.16
  21.9 2.9 copy-start.5
  21.9 2.9 copy-start.6
  21.9 2.9 copy-start.7
  21.9 2.9 copy-start.11
  21.9 2.9 copy-start.12
  21.9 2.9 copy-start.13
  22.0 2.9 copy-start.14
  30.4 60.8 %copy-start.20 = (s32[1,128,2]{1,2,0:T(2,128)S(1)}, s32[1,128,2]{1,2,0:T(2,128)}, u32[]{:S(2)}) copy-start(s32[1,128,2]{1,2,0:T(2,128)} %param.19) | copy-start | bytes 3076
  30.4 61.2 %copy-start.17 = (f32[128,16]{0,1:T(8,128)S(1)}, f32[128,16]{0,1:T(8,128)}, u32[]{:S(2)}) copy-start(f32[128,16]{0,1:T(8,128)} %get-tuple-element.72) | copy-start | bytes 24580
  31.3 104.9 %all-gather.6.cloned.1.call-start = ((), (), s32[]{:S(2)}) async-start(), calls=%async_computation.2 | async-start | bytes 5570560 | tf_op jit(solution)/shard_map/all_gather | solution.py:134
  95.9 17.3 %copy-start.4 = (bf16[1,128,4096]{2,1,0:T(8,128)(2,1)S(1)}, bf16[1,128,4096]{2,1,0:T(8,128)(2,1)}, u32[]{:S(2)}) copy-start(bf16[1,128,4096]{2,1,0:T(8,128)(2,1)} %param.11) | copy-start | bytes 3145732
  95.9 17.3 %copy-start.18 = (f32[4096]{0:T(1024)S(1)}, f32[4096]{0:T(1024)}, u32[]{:S(2)}) copy-start(f32[4096]{0:T(1024)} %param.17) | copy-start | bytes 49156
  122.3 154.9 %all-to-all-start = ((bf16[32,20,4096]{2,1,0:T(8,128)(2,1)}), bf16[32,20,4096]{2,1,0:T(8,128)(2,1)}, u32[]{:S(2)}, u32[]{:S(2)}) async-start(bf16[32,20,4096]{2,1,0:T(8,128)(2,1)} %copy.51), calls=%async_computation | async-start | bytes 12582912 | tf_op jit(solution)/shard_map/all_to_all | solution.py:130
  132.3 153.8 %all-gather.8.cloned.1.call-start = ((), (), s32[]{:S(2)}) async-start(), calls=%async_computation.3 | async-start | bytes 5570560 | tf_op jit(solution)/shard_map/all_gather | solution.py:142
  298.6 10.5 %copy-start.10 = (bf16[16,4096]{1,0:T(8,128)(2,1)S(1)}, bf16[16,4096]{1,0:T(8,128)(2,1)}, u32[]{:S(2)}) copy-start(bf16[16,4096]{1,0:T(8,128)(2,1)} %param.18) | copy-start | bytes 393220
  298.6 154.5 %all-to-all-start.1 = ((bf16[32,20,4096]{2,1,0:T(8,128)(2,1)}), bf16[32,20,4096]{2,1,0:T(8,128)(2,1)}, u32[]{:S(2)}, u32[]{:S(2)}) async-start(bf16[32,20,4096]{2,1,0:T(8,128)(2,1)} %copy.53), calls=%async_computation.1 | async-start | bytes 12582912 | tf_op jit(solution)/shard_map/all_to_all | solution.py:146
  453.0 8.2 %copy-start.1 = (bf16[256,4096]{1,0:T(8,128)(2,1)S(1)}, bf16[256,4096]{1,0:T(8,128)(2,1)}, u32[]{:S(2)}) copy-start(bf16[256,4096]{1,0:T(8,128)(2,1)} %param.14) | copy-start | bytes 6291460
Sparse Core Ops, SparseCore 0:
  31.4 53.4 all-gather.9
  91.3 44.8 all-gather.5
  138.3 52.9 all-gather.7

commit v7 on v6

--- a/solution.py
+++ b/solution.py
@@ -100,9 +100,16 @@
                 jnp.exp(exponent) * driven[:, None, lower : lower + span] * b_in[:, :, None], axis=0
             )
         )
+    local = sweep(jnp.zeros_like(a_neg), a_neg, delta, driven, b_in, c_out)
     start = carry_in(a_neg, cumulated[-1], jnp.concatenate(ends, axis=1))
-    start, w_up, w_down = lax.optimization_barrier((start, w_up, w_down))
-    scanned = sweep(start, a_neg, delta, driven, b_in, c_out)
+    start, local, w_up, w_down = lax.optimization_barrier((start, local, w_up, w_down))
+    carried = []
+    for lower in range(0, channels, span):
+        decay = jnp.exp(a_neg[None, :, lower : lower + span] * cumulated[:, None, lower : lower + span])
+        carried.append(
+            jnp.sum(decay * start[None, :, lower : lower + span] * c_out[:, :, None], axis=1)
+        )
+    scanned = local + jnp.concatenate(carried, axis=1)
     mixer = (scanned + d_skip * xfloat).astype(jnp.bfloat16)
     experts_count = w_router.shape[0]
     owners = lax.axis_size("exp")

time: 468 us -> 460 us (0.983)
  waiting for transfers between devices: 339 us -> 319 us
  other arithmetic: 21.7 us -> 33.3 us
    all_gather x1, waiting for transfers between devices: 53.4 us -> 32.8 us  [carry_in(): every = lax.all_gather(packed, 'seq')]
    reduce_sum x0 -> x2, other arithmetic: none -> 13.7 us  [per_device(): jnp.sum(decay * start[None, :, lower:lower + span] * c_out[:, :, None], a...]
    all_to_all x1, waiting for transfers between devices: 141 us -> 135 us  [per_device(): lax.all_to_all(outgoing, 'exp', split_axis=0, concat_axis=0, tiled=True)]
    all_gather x1, waiting for transfers between devices: 3.21 us -> 8.83 us  [per_device(): lax.all_gather(w_up, 'seq', axis=1, tiled=True)[0]]
  transfers between devices with their start and end apart: 5 -> 5, of which waited for: 4 -> 4; matrix products, arithmetic and copies ran while one was open for 5% -> 8% of each run, Pallas kernels for 4% -> 4%
where the time goes in v7:
time: 460 us; the launch traced here: 459 us
  waiting for transfers between devices  319 us (69%)
  other arithmetic  33.3 us (7%)
  matrix products  29.1 us (6%)
  local copies, waits for them, and re-layouts  27.7 us (6%)
  starting transfers between devices  19.5 us (4%)
  Pallas kernels  17.3 us (4%)
  between operations  13.9 us (3%)
    all_to_all x1, waiting for transfers between devices, per_device(): lax.all_to_all(partial_out, 'exp', split_axis=0, concat_axis=0, tiled=True)  141 us
    all_to_all x1, waiting for transfers between devices, per_device(): lax.all_to_all(outgoing, 'exp', split_axis=0, concat_axis=0, tiled=True)  135 us
    all_gather x1, waiting for transfers between devices, carry_in(): every = lax.all_gather(packed, 'seq')  32.8 us
    pallas_call x1, Pallas kernels, sweep(): pl.pallas_call(sweep_kernel, out_shape=jax.ShapeDtypeStruct((tokens_here,...  17.3 us
    reduce_sum x2, other arithmetic, per_device(): jnp.sum(decay * start[None, :, lower:lower + span] * c_out[:, :, None], a...  13.7 us
    all_to_all x1, starting transfers between devices, per_device(): lax.all_to_all(outgoing, 'exp', split_axis=0, concat_axis=0, tiled=True)  9.98 us
    all_to_all x1, starting transfers between devices, per_device(): lax.all_to_all(partial_out, 'exp', split_axis=0, concat_axis=0, tiled=True)  9.48 us
  transfers between devices with their start and end apart: 5, of which 4 were waited for; matrix products, arithmetic and copies ran while one was open for 8% of the time, Pallas kernels for 4%

profile of v7, /device:TPU:7, one launch (start us, length us, event | category | flops | bytes accessed | tf_op | source)
XLA Modules:
  0.0 459.4 jit_solution(8460091930314633990)
XLA Ops:
  6.5 1.6 copy-done
  8.1 4.8 %convert_multiply_fusion.1 = (f32[128,4096]{1,0:T(8,128)}, f32[128,4096]{1,0:T(8,128)}) fusion(bf16[1,128,4096]{2,1,0:T(8,128)(2,1)} %param.11, f32[4096]{0:T(1024)} %param.15, bf16[256,4096]{1,0:T(8,128)(2,1)S(1)} %copy-done, bf16[1,128,256]{2,1,0:T(8,128)(2,1)} %param.12), kind=kOutput, calls=%fused_computation.30 | convolution fusion | flops 273154048 | bytes 7421952 | tf_op jit(solution)/shard_map/dot_general | solution.py:83
  12.9 3.5 reduce_window_sum.26
  16.4 0.6 fusion.79
  17.0 2.8 fusion.80
  19.9 0.7 fusion.82
  20.9 1.1 fusion.77
  22.1 1.7 multiply_reduce_fusion.9
  23.9 5.6 %multiply_reduce_fusion.8 = (f32[16,512]{1,0:T(8,128)S(1)}, f32[16,512]{1,0:T(8,128)S(1)}, f32[16,512]{1,0:T(8,128)S(1)}, f32[16,512]{1,0:T(8,128)S(1)}, f32[16,512]{1,0:T(8,128)S(1)}, /*index=5*/f32[16,512]{1,0:T(8,128)S(1)}) fusion(f32[128,512]{1,0:T(8,128)S(1)} %copy-done.7, f32[128,512]{1,0:T(8,128)S(1)} %get-tuple-element.58, ...), kind=kLoop, calls=%fused_computation.21 | loop fusion | flops 25116672 | bytes 3547136 | tf_op jit(solution)/shard_map/reduce_sum | solution.py:99
  29.6 0.8 maximum_bitcast_fusion
  30.6 1.3 broadcast_in_dim.11.b_ref
  31.9 1.4 broadcast_in_dim.13.c_ref
  33.3 0.7 broadcast_5_start_ref.2.start_ref
  34.0 17.3 %shard_map.109 = f32[128,4096]{1,0:T(8,128)} custom-call(f32[128,4096]{1,0:T(8,128)} %get-tuple-element.103.delta_ref, f32[128,4096]{1,0:T(8,128)} %get-tuple-element.102.driven_ref, f32[16,4096]{1,0:T(8,128)} %copy-done.4, f32[16,4096]{1,0:T(8,128)} %broadcast_5_start_ref.2.start_ref, f32[128,16,128]{2,1,0:T(8,128)} %broadcast_in_dim.11.b_ref, ...), custom_call_target="tpu_custom_call" | custom-call | flops 67108864 | bytes 6815744 | tf_op jit(solution)/shard_map/pallas_call | solution.py:62
  51.2 32.8 %all-gather.10.cloned.1.call-done = f32[16,17,4096]{2,1,0:T(8,128)} async-done(((f32[1,17,4096]{2,1,0:T(8,128)}), f32[16,17,4096]{2,1,0:T(8,128)}) %all-gather.10.cloned.1.call-update) | async-done | bytes 4456464 | tf_op jit(solution)/shard_map/all_gather | solution.py:18
  84.1 1.7 fusion.76
  85.8 3.8 fusion.30
  89.6 0.1 copy.51
  89.8 0.1 eq.114
  89.9 0.1 eq.110
  90.0 0.6 reduce-window.6
  90.6 0.2 slice_reduce_fusion.4
  91.0 0.1 sub.138
  91.1 0.2 slice_reduce_fusion.2
  91.3 0.2 slice_reduce_fusion.3
  91.7 3.5 multiply_reduce_fusion.1
  95.3 10.2 %multiply_reduce_fusion = (f32[128,512]{1,0:T(8,128)S(1)}, f32[128,512]{1,0:T(8,128)S(1)}, f32[128,512]{1,0:T(8,128)S(1)}, f32[128,512]{1,0:T(8,128)S(1)}, f32[128,512]{1,0:T(8,128)S(1)}, /*index=5*/f32[128,512]{1,0:T(8,128)S(1)}) fusion(f32[16,512]{1,0:T(8,128)S(1)} %get-tuple-element.83, f32[128,512]{1,0:T(8,128)S(1)} %get-tuple-element.59, ...), kind=kLoop, calls=%fused_computation.13 | loop fusion | flops 24772608 | bytes 3547136 | tf_op jit(solution)/shard_map/reduce_sum | solution.py:110
  105.7 1.4 copy-done.2
  107.1 0.3 copy-done.5
  107.4 0.4 fusion.12
  107.8 1.5 convolution_convert_fusion.1
  109.3 5.6 %copy.56 = bf16[32,20,4096]{2,1,0:T(8,128)(2,1)} copy(bf16[32,20,4096]{2,0,1:T(8,128)(2,1)S(1)} %convolution_convert_fusion.1) | data formatting | bytes 10485760 | tf_op jit(solution)/shard_map/convert_element_type | solution.py:136
  114.9 10.0 %all-to-all-start = ((bf16[32,20,4096]{2,1,0:T(8,128)(2,1)}), bf16[32,20,4096]{2,1,0:T(8,128)(2,1)}, u32[]{:S(2)}, u32[]{:S(2)}) async-start(bf16[32,20,4096]{2,1,0:T(8,128)(2,1)} %copy.56), calls=%async_computation | async-start | bytes 12582912 | tf_op jit(solution)/shard_map/all_to_all | solution.py:137
  124.9 0.7 all-gather.8.cloned.1.call-update
  125.6 8.8 %all-gather.6.cloned.1.call-done = bf16[1,4096,640]{2,1,0:T(8,128)(2,1)} async-done(((bf16[1,256,640]{2,1,0:T(8,128)(2,1)}), bf16[1,4096,640]{2,1,0:T(8,128)(2,1)}) %all-gather.6.cloned.1.call-update) | async-done | bytes 5242896 | tf_op jit(solution)/shard_map/all_gather | solution.py:141
  134.4 135.1 %all-to-all-done = bf16[32,20,4096]{2,1,0:T(8,128)(2,1)} async-done(((bf16[32,20,4096]{2,1,0:T(8,128)(2,1)}), bf16[32,20,4096]{2,1,0:T(8,128)(2,1)}, u32[]{:S(2)}, u32[]{:S(2)}) %all-to-all-start) | async-done | bytes 5242912 | tf_op jit(solution)/shard_map/all_to_all | solution.py:137
  269.5 8.9 %multiply_convert_fusion = bf16[32,20,640]{2,1,0:T(8,128)(2,1)S(1)} fusion(bf16[32,20,4096]{2,1,0:T(8,128)(2,1)} %all-to-all-done, bf16[1,4096,640]{2,1,0:T(8,128)(2,1)} %all-gather.6.cloned.1.call-done), kind=kOutput, calls=%fused_computation.40 | convolution fusion | flops 3357491200 | bytes 11304960 | tf_op jit(solution)/shard_map/jsc,ch->jsh/dot_general | solution.py:138
  278.4 6.9 %convolution_convert_fusion = bf16[32,20,4096]{2,0,1:T(8,128)(2,1)S(1)} fusion(bf16[1,640,4096]{2,1,0:T(8,128)(2,1)} %all-gather.8.cloned.1.call-done, bf16[32,20,640]{2,1,0:T(8,128)(2,1)S(1)} %multiply_convert_fusion), kind=kOutput, calls=%fused_computation.1 | convolution fusion | flops 3358064640 | bytes 11304960 | tf_op jit(solution)/shard_map/jsh,hc->jsc/dot_general | solution.py:146
  285.4 5.6 %copy.58 = bf16[32,20,4096]{2,1,0:T(8,128)(2,1)} copy(bf16[32,20,4096]{2,0,1:T(8,128)(2,1)S(1)} %convolution_convert_fusion) | data formatting | bytes 10485760 | tf_op jit(solution)/shard_map/optimization_barrier | solution.py:145
  291.0 9.5 %all-to-all-start.1 = ((bf16[32,20,4096]{2,1,0:T(8,128)(2,1)}), bf16[32,20,4096]{2,1,0:T(8,128)(2,1)}, u32[]{:S(2)}, u32[]{:S(2)}) async-start(bf16[32,20,4096]{2,1,0:T(8,128)(2,1)} %copy.58), calls=%async_computation.1 | async-start | bytes 12582912 | tf_op jit(solution)/shard_map/all_to_all | solution.py:153
  300.6 0.1 reshape.313
  300.8 0.4 fusion.83
  301.2 2.0 gather_fusion
  303.2 0.1 reshape.316
  303.4 0.2 fusion.75
  303.6 141.1 %all-to-all-done.1 = bf16[32,20,4096]{2,1,0:T(8,128)(2,1)} async-done(((bf16[32,20,4096]{2,1,0:T(8,128)(2,1)}), bf16[32,20,4096]{2,1,0:T(8,128)(2,1)}, u32[]{:S(2)}, u32[]{:S(2)}) %all-to-all-start.1) | async-done | bytes 5242912 | tf_op jit(solution)/shard_map/all_to_all | solution.py:153
  444.7 6.6 %fusion.8 = f32[2,128,4096]{2,1,0:T(8,128)S(1)} fusion(bf16[32,20,4096]{2,1,0:T(8,128)(2,1)} %all-to-all-done.1, pred[1,32,20,128]{3,1,2,0:T(32,128)(4,1)S(1)} %broadcast_and_fusion, pred[1,32,20,128]{3,1,2,0:T(32,128)(4,1)S(1)} %broadcast_and_fusion.1), kind=kOutput, calls=%fused_computation.11 | convolution fusion | flops 1344438272 | bytes 9601024 | tf_op jit(solution)/shard_map/kjst,jsc->ktc/dot_general | solution.py:155
  451.3 1.5 fusion.20
  (97 shorter events, 1.3 us)
Async XLA Ops:
  6.5 1.6 copy-start
  6.5 77.5 %all-gather.10.cloned.1.call-start = ((), (), s32[]{:S(2)}) async-start(), calls=%async_computation.4 | async-start | bytes 6684672 | tf_op jit(solution)/shard_map/all_gather | solution.py:18
  12.9 7.0 %copy-start.3 = (f32[16,4096]{1,0:T(8,128)S(1)}, f32[16,4096]{1,0:T(8,128)}, u32[]{:S(2)}) copy-start(f32[16,4096]{1,0:T(8,128)} %param.16) | copy-start | bytes 786436
  12.9 7.7 %copy-start.26 = (f32[1,128,32]{1,2,0:T(8,128)S(1)}, f32[1,128,32]{1,2,0:T(8,128)}, u32[]{:S(2)}) copy-start(f32[1,128,32]{1,2,0:T(8,128)} %param.13) | copy-start | bytes 49156
  19.9 3.9 copy-start.4
  20.6 3.2 copy-start.15
  20.8 1.3 copy-start.12
  20.8 1.3 copy-start.13
  20.8 1.3 copy-start.23
  20.8 1.3 copy-start.24
  20.8 3.0 copy-start.6
  20.8 3.0 copy-start.7
  20.8 3.0 copy-start.8
  20.8 3.0 copy-start.9
  20.8 3.0 copy-start.10
  20.8 3.0 copy-start.11
  20.9 3.0 copy-start.17
  20.9 3.0 copy-start.19
  20.9 3.0 copy-start.20
  20.9 3.0 copy-start.21
  20.9 3.0 copy-start.22
  30.4 104.1 %all-gather.6.cloned.1.call-start = ((), (), s32[]{:S(2)}) async-start(), calls=%async_computation.2 | async-start | bytes 5570560 | tf_op jit(solution)/shard_map/all_gather | solution.py:141
  51.2 38.4 %copy-start.27 = (s32[1,128,2]{1,2,0:T(2,128)S(1)}, s32[1,128,2]{1,2,0:T(2,128)}, u32[]{:S(2)}) copy-start(s32[1,128,2]{1,2,0:T(2,128)} %param.19) | copy-start | bytes 3076
  89.6 5.6 %copy-start.16 = (f32[16,512]{1,0:T(8,128)S(1)}, f32[16,512]{1,0:T(8,128)}, u32[]{:S(2)}) copy-start(f32[16,512]{1,0:T(8,128)} %copy-done.15) | copy-start | bytes 98308
  89.6 5.6 %copy-start.18 = (f32[16,512]{1,0:T(8,128)S(1)}, f32[16,512]{1,0:T(8,128)}, u32[]{:S(2)}) copy-start(f32[16,512]{1,0:T(8,128)} %get-tuple-element.91) | copy-start | bytes 98308
  95.2 10.5 %copy-start.25 = (f32[4096]{0:T(1024)S(1)}, f32[4096]{0:T(1024)}, u32[]{:S(2)}) copy-start(f32[4096]{0:T(1024)} %param.17) | copy-start | bytes 49156
  105.5 1.6 copy-start.2
  105.5 1.8 copy-start.5
  114.9 154.7 %all-to-all-start = ((bf16[32,20,4096]{2,1,0:T(8,128)(2,1)}), bf16[32,20,4096]{2,1,0:T(8,128)(2,1)}, u32[]{:S(2)}, u32[]{:S(2)}) async-start(bf16[32,20,4096]{2,1,0:T(8,128)(2,1)} %copy.56), calls=%async_computation | async-start | bytes 12582912 | tf_op jit(solution)/shard_map/all_to_all | solution.py:137
  124.9 153.5 %all-gather.8.cloned.1.call-start = ((), (), s32[]{:S(2)}) async-start(), calls=%async_computation.3 | async-start | bytes 5570560 | tf_op jit(solution)/shard_map/all_gather | solution.py:149
  290.9 9.5 %copy-start.28 = (s32[1,128,2]{1,2,0:T(2,128)S(1)}, s32[1,128,2]{1,2,0:T(2,128)}, u32[]{:S(2)}) copy-start(s32[1,128,2]{1,2,0:T(2,128)} %param.19) | copy-start | bytes 3076
  290.9 9.9 %copy-start.14 = (bf16[16,4096]{1,0:T(8,128)(2,1)S(1)}, bf16[16,4096]{1,0:T(8,128)(2,1)}, u32[]{:S(2)}) copy-start(bf16[16,4096]{1,0:T(8,128)(2,1)} %param.18) | copy-start | bytes 393220
  291.0 153.7 %all-to-all-start.1 = ((bf16[32,20,4096]{2,1,0:T(8,128)(2,1)}), bf16[32,20,4096]{2,1,0:T(8,128)(2,1)}, u32[]{:S(2)}, u32[]{:S(2)}) async-start(bf16[32,20,4096]{2,1,0:T(8,128)(2,1)} %copy.58), calls=%async_computation.1 | async-start | bytes 12582912 | tf_op jit(solution)/shard_map/all_to_all | solution.py:153
  444.7 8.2 %copy-start.1 = (bf16[256,4096]{1,0:T(8,128)(2,1)S(1)}, bf16[256,4096]{1,0:T(8,128)(2,1)}, u32[]{:S(2)}) copy-start(bf16[256,4096]{1,0:T(8,128)(2,1)} %param.14) | copy-start | bytes 6291460
Sparse Core Ops, SparseCore 0:
  30.5 53.5 all-gather.9
  89.7 44.6 all-gather.5
  136.5 53.0 all-gather.7

commit v8 on v7

--- a/solution.py
+++ b/solution.py
@@ -14,11 +14,14 @@
 def carry_in(a_neg, total_delta, end_state):
     count = lax.axis_size("seq")
     me = lax.axis_index("seq")
-    packed = jnp.concatenate([total_delta[None], end_state], axis=0)
-    every = lax.all_gather(packed, "seq")
+    high = total_delta.astype(jnp.bfloat16)
+    low = (total_delta - high.astype(jnp.float32)).astype(jnp.bfloat16)
+    packed = jnp.concatenate([high[None], low[None], end_state.astype(jnp.bfloat16)], axis=0)
+    every = lax.all_gather(packed, "seq").astype(jnp.float32)
     state = jnp.zeros_like(end_state)
     for k in range(count - 1):
-        folded = jnp.exp(a_neg * every[k, 0][None, :]) * state + every[k, 1:]
+        total = every[k, 0] + every[k, 1]
+        folded = jnp.exp(a_neg * total[None, :]) * state + every[k, 2:]
         state = jnp.where(k < me, folded, state)
     return state
 

time: 460 us -> 454 us (0.987)
  waiting for transfers between devices: 319 us -> 314 us
    all_gather x1, waiting for transfers between devices: 32.8 us -> 27.7 us  [carry_in(): every = lax.all_gather(packed, 'seq').astype(jnp.float32)]
  transfers between devices with their start and end apart: 5 -> 5, of which waited for: 4 -> 4; matrix products, arithmetic and copies ran while one was open for 8% -> 9% of each run, Pallas kernels for 4% -> 4%
where the time goes in v8:
time: 454 us; the launch traced here: 453 us
  waiting for transfers between devices  314 us (69%)
  other arithmetic  33.8 us (7%)
  matrix products  29.1 us (6%)
  local copies, waits for them, and re-layouts  26 us (6%)
  starting transfers between devices  19.7 us (4%)
  Pallas kernels  17.3 us (4%)
  between operations  13.9 us (3%)
    all_to_all x1, waiting for transfers between devices, per_device(): lax.all_to_all(partial_out, 'exp', split_axis=0, concat_axis=0, tiled=True)  141 us
    all_to_all x1, waiting for transfers between devices, per_device(): lax.all_to_all(outgoing, 'exp', split_axis=0, concat_axis=0, tiled=True)  135 us
    all_gather x1, waiting for transfers between devices, carry_in(): every = lax.all_gather(packed, 'seq').astype(jnp.float32)  27.7 us
    pallas_call x1, Pallas kernels, sweep(): pl.pallas_call(sweep_kernel, out_shape=jax.ShapeDtypeStruct((tokens_here,...  17.3 us
    reduce_sum x2, other arithmetic, per_device(): jnp.sum(decay * start[None, :, lower:lower + span] * c_out[:, :, None], a...  13.9 us
    all_to_all x1, starting transfers between devices, per_device(): lax.all_to_all(outgoing, 'exp', split_axis=0, concat_axis=0, tiled=True)  9.98 us
    all_to_all x1, starting transfers between devices, per_device(): lax.all_to_all(partial_out, 'exp', split_axis=0, concat_axis=0, tiled=True)  9.48 us
  transfers between devices with their start and end apart: 5, of which 4 were waited for; matrix products, arithmetic and copies ran while one was open for 9% of the time, Pallas kernels for 4%

profile of v8, /device:TPU:7, one launch (start us, length us, event | category | flops | bytes accessed | tf_op | source)
XLA Modules:
  0.0 453.3 jit_solution(13900474177724973438)
XLA Ops:
  6.5 1.6 copy-done
  8.1 4.8 %convert_multiply_fusion.1 = (f32[128,4096]{1,0:T(8,128)}, f32[128,4096]{1,0:T(8,128)}) fusion(bf16[1,128,4096]{2,1,0:T(8,128)(2,1)} %param.11, f32[4096]{0:T(1024)} %param.15, bf16[256,4096]{1,0:T(8,128)(2,1)S(1)} %copy-done, bf16[1,128,256]{2,1,0:T(8,128)(2,1)} %param.12), kind=kOutput, calls=%fused_computation.30 | convolution fusion | flops 273154048 | bytes 7421952 | tf_op jit(solution)/shard_map/dot_general | solution.py:86
  13.0 3.5 reduce_window_sum.26
  16.4 0.6 fusion.78
  17.1 2.8 fusion.79
  20.0 0.7 fusion.81
  21.0 1.1 fusion.76
  22.1 1.7 multiply_reduce_fusion.9
  24.0 5.6 %multiply_reduce_fusion.8 = (bf16[16,512]{1,0:T(8,128)(2,1)S(1)}, bf16[16,512]{1,0:T(8,128)(2,1)S(1)}, bf16[16,512]{1,0:T(8,128)(2,1)S(1)}, bf16[16,512]{1,0:T(8...) fusion(f32[128,512]{1,0:T(8,128)S(1)} %copy-done.7, f32[128,512]{1,0:T(8,128)S(1)} %get-tuple-element.58, ...), kind=kLoop, calls=%fused_computation.21 | loop fusion | flops 25116672 | bytes 3448832 | tf_op jit(solution)/shard_map/reduce_sum | solution.py:102
  29.6 0.8 maximum_bitcast_fusion
  30.5 0.2 all-gather.6.cloned.1.call-start
  30.8 1.3 broadcast_in_dim.11.b_ref
  32.1 1.3 broadcast_in_dim.13.c_ref
  33.4 0.7 broadcast_5_start_ref.2.start_ref
  34.2 17.3 %shard_map.109 = f32[128,4096]{1,0:T(8,128)} custom-call(f32[128,4096]{1,0:T(8,128)} %get-tuple-element.103.delta_ref, f32[128,4096]{1,0:T(8,128)} %get-tuple-element.102.driven_ref, f32[16,4096]{1,0:T(8,128)} %copy-done.4, f32[16,4096]{1,0:T(8,128)} %broadcast_5_start_ref.2.start_ref, f32[128,16,128]{2,1,0:T(8,128)} %broadcast_in_dim.11.b_ref, ...), custom_call_target="tpu_custom_call" | custom-call | flops 67108864 | bytes 6815744 | tf_op jit(solution)/shard_map/pallas_call | solution.py:65
  51.4 27.7 %all-gather.10.cloned.1.call-done = bf16[16,18,4096]{2,1,0:T(8,128)(2,1)} async-done(((bf16[1,18,4096]{2,1,0:T(8,128)(2,1)}), bf16[16,18,4096]{2,1,0:T(8,128)(2,1)}) %all-gather.10.cloned.1.call-update) | async-done | bytes 2359312 | tf_op jit(solution)/shard_map/all_gather | solution.py:20
  79.1 2.6 convert_element_type.71
  81.8 0.2 slice_add_fusion.14
  82.1 1.1 fusion.30
  83.4 0.1 eq.114
  83.5 0.1 eq.110
  83.7 0.6 reduce-window.6
  84.3 0.2 slice_reduce_fusion.4
  84.6 0.1 sub.143
  84.7 0.2 slice_reduce_fusion.2
  84.9 0.2 slice_reduce_fusion.3
  85.3 3.5 multiply_reduce_fusion.1
  88.9 10.5 %multiply_reduce_fusion = (f32[128,512]{1,0:T(8,128)S(1)}, f32[128,512]{1,0:T(8,128)S(1)}, f32[128,512]{1,0:T(8,128)S(1)}, f32[128,512]{1,0:T(8,128)S(1)}, f32[128,512]{1,0:T(8,128)S(1)}, /*index=5*/f32[128,512]{1,0:T(8,128)S(1)}) fusion(f32[16,512]{1,0:T(8,128)S(1)} %get-tuple-element.83, f32[128,512]{1,0:T(8,128)S(1)} %get-tuple-element.59, ...), kind=kLoop, calls=%fused_computation.13 | loop fusion | flops 24772608 | bytes 3547136 | tf_op jit(solution)/shard_map/reduce_sum | solution.py:113
  99.6 1.4 copy-done.2
  100.9 0.3 copy-done.5
  101.2 0.4 fusion.12
  101.6 1.5 convolution_convert_fusion.1
  103.2 5.6 %copy.56 = bf16[32,20,4096]{2,1,0:T(8,128)(2,1)} copy(bf16[32,20,4096]{2,0,1:T(8,128)(2,1)S(1)} %convolution_convert_fusion.1) | data formatting | bytes 10485760 | tf_op jit(solution)/shard_map/convert_element_type | solution.py:139
  108.7 10.0 %all-to-all-start = ((bf16[32,20,4096]{2,1,0:T(8,128)(2,1)}), bf16[32,20,4096]{2,1,0:T(8,128)(2,1)}, u32[]{:S(2)}, u32[]{:S(2)}) async-start(bf16[32,20,4096]{2,1,0:T(8,128)(2,1)} %copy.56), calls=%async_computation | async-start | bytes 12582912 | tf_op jit(solution)/shard_map/all_to_all | solution.py:140
  118.8 0.7 all-gather.8.cloned.1.call-update
  119.5 8.7 %all-gather.6.cloned.1.call-done = bf16[1,4096,640]{2,1,0:T(8,128)(2,1)} async-done(((bf16[1,256,640]{2,1,0:T(8,128)(2,1)}), bf16[1,4096,640]{2,1,0:T(8,128)(2,1)}) %all-gather.6.cloned.1.call-update) | async-done | bytes 5242896 | tf_op jit(solution)/shard_map/all_gather | solution.py:144
  128.1 135.3 %all-to-all-done = bf16[32,20,4096]{2,1,0:T(8,128)(2,1)} async-done(((bf16[32,20,4096]{2,1,0:T(8,128)(2,1)}), bf16[32,20,4096]{2,1,0:T(8,128)(2,1)}, u32[]{:S(2)}, u32[]{:S(2)}) %all-to-all-start) | async-done | bytes 5242912 | tf_op jit(solution)/shard_map/all_to_all | solution.py:140
  263.4 8.9 %multiply_convert_fusion = bf16[32,20,640]{2,1,0:T(8,128)(2,1)S(1)} fusion(bf16[32,20,4096]{2,1,0:T(8,128)(2,1)} %all-to-all-done, bf16[1,4096,640]{2,1,0:T(8,128)(2,1)} %all-gather.6.cloned.1.call-done), kind=kOutput, calls=%fused_computation.40 | convolution fusion | flops 3357491200 | bytes 11304960 | tf_op jit(solution)/shard_map/jsc,ch->jsh/dot_general | solution.py:141
  272.3 6.9 %convolution_convert_fusion = bf16[32,20,4096]{2,0,1:T(8,128)(2,1)S(1)} fusion(bf16[1,640,4096]{2,1,0:T(8,128)(2,1)} %all-gather.8.cloned.1.call-done, bf16[32,20,640]{2,1,0:T(8,128)(2,1)S(1)} %multiply_convert_fusion), kind=kOutput, calls=%fused_computation.1 | convolution fusion | flops 3358064640 | bytes 11304960 | tf_op jit(solution)/shard_map/jsh,hc->jsc/dot_general | solution.py:149
  279.2 5.6 %copy.58 = bf16[32,20,4096]{2,1,0:T(8,128)(2,1)} copy(bf16[32,20,4096]{2,0,1:T(8,128)(2,1)S(1)} %convolution_convert_fusion) | data formatting | bytes 10485760 | tf_op jit(solution)/shard_map/optimization_barrier | solution.py:148
  284.8 9.5 %all-to-all-start.1 = ((bf16[32,20,4096]{2,1,0:T(8,128)(2,1)}), bf16[32,20,4096]{2,1,0:T(8,128)(2,1)}, u32[]{:S(2)}, u32[]{:S(2)}) async-start(bf16[32,20,4096]{2,1,0:T(8,128)(2,1)} %copy.58), calls=%async_computation.1 | async-start | bytes 12582912 | tf_op jit(solution)/shard_map/all_to_all | solution.py:156
  294.4 0.1 reshape.448
  294.7 0.4 fusion.82
  295.0 2.0 gather_fusion
  297.2 0.2 fusion.75
  297.4 141.2 %all-to-all-done.1 = bf16[32,20,4096]{2,1,0:T(8,128)(2,1)} async-done(((bf16[32,20,4096]{2,1,0:T(8,128)(2,1)}), bf16[32,20,4096]{2,1,0:T(8,128)(2,1)}, u32[]{:S(2)}, u32[]{:S(2)}) %all-to-all-start.1) | async-done | bytes 5242912 | tf_op jit(solution)/shard_map/all_to_all | solution.py:156
  438.6 6.6 %fusion.8 = f32[2,128,4096]{2,1,0:T(8,128)S(1)} fusion(bf16[32,20,4096]{2,1,0:T(8,128)(2,1)} %all-to-all-done.1, pred[1,32,20,128]{3,1,2,0:T(32,128)(4,1)S(1)} %broadcast_and_fusion, pred[1,32,20,128]{3,1,2,0:T(32,128)(4,1)S(1)} %broadcast_and_fusion.1), kind=kOutput, calls=%fused_computation.11 | convolution fusion | flops 1344438272 | bytes 9601024 | tf_op jit(solution)/shard_map/kjst,jsc->ktc/dot_general | solution.py:158
  445.2 1.5 fusion.20
  (100 shorter events, 1.6 us)
Async XLA Ops:
  6.5 1.6 copy-start
  6.5 72.6 %all-gather.10.cloned.1.call-start = ((), (), s32[]{:S(2)}) async-start(), calls=%async_computation.4 | async-start | bytes 3342336 | tf_op jit(solution)/shard_map/all_gather | solution.py:20
  13.0 7.0 %copy-start.3 = (f32[16,4096]{1,0:T(8,128)S(1)}, f32[16,4096]{1,0:T(8,128)}, u32[]{:S(2)}) copy-start(f32[16,4096]{1,0:T(8,128)} %param.16) | copy-start | bytes 786436
  13.0 7.8 %copy-start.26 = (f32[1,128,32]{1,2,0:T(8,128)S(1)}, f32[1,128,32]{1,2,0:T(8,128)}, u32[]{:S(2)}) copy-start(f32[1,128,32]{1,2,0:T(8,128)} %param.13) | copy-start | bytes 49156
  20.0 3.9 copy-start.4
  20.7 3.1 copy-start.15
  20.8 1.3 copy-start.12
  20.8 1.3 copy-start.13
  20.9 1.3 copy-start.23
  20.9 1.3 copy-start.24
  20.9 3.0 copy-start.6
  20.9 3.0 copy-start.7
  20.9 3.0 copy-start.8
  20.9 3.0 copy-start.9
  20.9 3.0 copy-start.10
  20.9 3.0 copy-start.11
  20.9 3.0 copy-start.17
  20.9 3.0 copy-start.19
  21.0 3.0 copy-start.20
  21.0 3.0 copy-start.21
  21.0 3.0 copy-start.22
  30.5 97.7 %all-gather.6.cloned.1.call-start = ((), (), s32[]{:S(2)}) async-start(), calls=%async_computation.2 | async-start | bytes 5570560 | tf_op jit(solution)/shard_map/all_gather | solution.py:144
  81.8 1.4 copy-start.27
  83.2 5.6 %copy-start.16 = (f32[16,512]{1,0:T(8,128)S(1)}, f32[16,512]{1,0:T(8,128)}, u32[]{:S(2)}) copy-start(f32[16,512]{1,0:T(8,128)} %copy-done.15) | copy-start | bytes 98308
  83.2 5.6 %copy-start.18 = (f32[16,512]{1,0:T(8,128)S(1)}, f32[16,512]{1,0:T(8,128)}, u32[]{:S(2)}) copy-start(f32[16,512]{1,0:T(8,128)} %get-tuple-element.91) | copy-start | bytes 98308
  88.9 10.7 %copy-start.25 = (f32[4096]{0:T(1024)S(1)}, f32[4096]{0:T(1024)}, u32[]{:S(2)}) copy-start(f32[4096]{0:T(1024)} %param.17) | copy-start | bytes 49156
  99.3 1.6 copy-start.2
  99.4 1.8 copy-start.5
  108.7 154.7 %all-to-all-start = ((bf16[32,20,4096]{2,1,0:T(8,128)(2,1)}), bf16[32,20,4096]{2,1,0:T(8,128)(2,1)}, u32[]{:S(2)}, u32[]{:S(2)}) async-start(bf16[32,20,4096]{2,1,0:T(8,128)(2,1)} %copy.56), calls=%async_computation | async-start | bytes 12582912 | tf_op jit(solution)/shard_map/all_to_all | solution.py:140
  118.7 153.5 %all-gather.8.cloned.1.call-start = ((), (), s32[]{:S(2)}) async-start(), calls=%async_computation.3 | async-start | bytes 5570560 | tf_op jit(solution)/shard_map/all_gather | solution.py:152
  284.8 9.5 %copy-start.28 = (s32[1,128,2]{1,2,0:T(2,128)S(1)}, s32[1,128,2]{1,2,0:T(2,128)}, u32[]{:S(2)}) copy-start(s32[1,128,2]{1,2,0:T(2,128)} %param.19) | copy-start | bytes 3076
  284.8 9.9 %copy-start.14 = (bf16[16,4096]{1,0:T(8,128)(2,1)S(1)}, bf16[16,4096]{1,0:T(8,128)(2,1)}, u32[]{:S(2)}) copy-start(bf16[16,4096]{1,0:T(8,128)(2,1)} %param.18) | copy-start | bytes 393220
  284.8 153.8 %all-to-all-start.1 = ((bf16[32,20,4096]{2,1,0:T(8,128)(2,1)}), bf16[32,20,4096]{2,1,0:T(8,128)(2,1)}, u32[]{:S(2)}, u32[]{:S(2)}) async-start(bf16[32,20,4096]{2,1,0:T(8,128)(2,1)} %copy.58), calls=%async_computation.1 | async-start | bytes 12582912 | tf_op jit(solution)/shard_map/all_to_all | solution.py:156
  438.6 8.2 %copy-start.1 = (bf16[256,4096]{1,0:T(8,128)(2,1)S(1)}, bf16[256,4096]{1,0:T(8,128)(2,1)}, u32[]{:S(2)}) copy-start(bf16[256,4096]{1,0:T(8,128)(2,1)} %param.14) | copy-start | bytes 6291460
Sparse Core Ops, SparseCore 0:
  30.6 48.5 all-gather.9
  83.3 44.7 all-gather.5
  130.2 52.9 all-gather.7

commit v9 on v8

--- a/solution.py
+++ b/solution.py
@@ -18,12 +18,13 @@
     low = (total_delta - high.astype(jnp.float32)).astype(jnp.bfloat16)
     packed = jnp.concatenate([high[None], low[None], end_state.astype(jnp.bfloat16)], axis=0)
     every = lax.all_gather(packed, "seq").astype(jnp.float32)
-    state = jnp.zeros_like(end_state)
-    for k in range(count - 1):
-        total = every[k, 0] + every[k, 1]
-        folded = jnp.exp(a_neg * total[None, :]) * state + every[k, 2:]
-        state = jnp.where(k < me, folded, state)
-    return state
+
+    def fold(k, state):
+        packet = every[k]
+        folded = jnp.exp(a_neg * (packet[0] + packet[1])[None, :]) * state + packet[2:]
+        return jnp.where(k < me, folded, state)
+
+    return lax.fori_loop(0, count - 1, fold, jnp.zeros_like(end_state))
 
 
 def sweep_kernel(delta_ref, driven_ref, a_ref, start_ref, b_ref, c_ref, y_ref):
@@ -90,7 +91,7 @@
     b_in = b_c[0, :, :nstate]
     c_out = b_c[0, :, nstate:]
     cumulated = jnp.cumsum(delta, axis=0)
-    pieces = max(1, channels // 512)
+    pieces = max(1, channels // 2048)
     span = channels // pieces
     ends = []
     for lower in range(0, channels, span):

time: 454 us -> 484 us (1.066)
  other arithmetic: 33.8 us -> 67.8 us
  local copies, waits for them, and re-layouts: 26 us -> 21.1 us
    select_n x1 -> x15, other arithmetic: 1.14 us -> 17.9 us  [fold(): return jnp.where(k < me, folded, state)]
    add x2 -> x15, other arithmetic: 0.24 us -> 15.1 us  [fold(): packet[0] + packet[1]]
    reduce_sum x2 -> x1, other arithmetic: 13.9 us -> 11.8 us  [per_device(): jnp.sum(decay * start[None, :, lower:lower + span] * c_out[:, :, None], a...]
  transfers between devices with their start and end apart: 5 -> 5, of which waited for: 4 -> 4; matrix products, arithmetic and copies ran while one was open for 9% -> 8% of each run, Pallas kernels for 4% -> 4%
where the time goes in v9:
time: 484 us; the launch traced here: 482 us
  waiting for transfers between devices  313 us (65%)
  other arithmetic  67.8 us (14%)
  matrix products  29.1 us (6%)
  local copies, waits for them, and re-layouts  21.1 us (4%)
  starting transfers between devices  19.9 us (4%)
  Pallas kernels  17.2 us (4%)
  between operations  13.5 us (3%)
    all_to_all x1, waiting for transfers between devices, per_device(): lax.all_to_all(partial_out, 'exp', split_axis=0, concat_axis=0, tiled=True)  141 us
    all_to_all x1, waiting for transfers between devices, per_device(): lax.all_to_all(outgoing, 'exp', split_axis=0, concat_axis=0, tiled=True)  131 us
    all_gather x1, waiting for transfers between devices, carry_in(): every = lax.all_gather(packed, 'seq').astype(jnp.float32)  27.8 us
    select_n x15, other arithmetic, fold(): return jnp.where(k < me, folded, state)  17.9 us
    pallas_call x1, Pallas kernels, sweep(): pl.pallas_call(sweep_kernel, out_shape=jax.ShapeDtypeStruct((tokens_here,...  17.2 us
    add x15, other arithmetic, fold(): packet[0] + packet[1]  15.1 us
    all_gather x1, waiting for transfers between devices, per_device(): lax.all_gather(w_up, 'seq', axis=1, tiled=True)[0]  12.8 us
    reduce_sum x1, other arithmetic, per_device(): jnp.sum(decay * start[None, :, lower:lower + span] * c_out[:, :, None], a...  11.8 us
  transfers between devices with their start and end apart: 5, of which 4 were waited for; matrix products, arithmetic and copies ran while one was open for 8% of the time, Pallas kernels for 4%

profile of v9, /device:TPU:7, one launch (start us, length us, event | category | flops | bytes accessed | tf_op | source)
XLA Modules:
  0.0 482.3 jit_solution(12116572376975777273)
XLA Ops:
  6.5 1.6 copy-done
  8.1 4.8 convert_multiply_fusion.1
  12.9 3.4 reduce_window_sum.26
  16.4 1.3 copy-done.2
  17.9 2.7 fusion.48
  20.6 7.6 %multiply_reduce_fusion.3 = (bf16[16,2048]{1,0:T(8,128)(2,1)S(1)}, bf16[16,2048]{1,0:T(8,128)(2,1)S(1)}) fusion(f32[128,16]{1,0:T(8,128)S(1)} %copy.47, f32[128,2048]{1,0:T(8,128)S(1)} %get-tuple-element.164, f32[128,2048]{1,0:T(8,128)S(1)} %get-tuple-element.147, f32[16,2048]{1,0:T(8,128)S(1)} %get-tuple-element.157, f32[128,2048]{1,0:T(8,128)S(1)} %get-tuple-element.165, ...), kind=kLoop, calls=%fused_computation.8 | loop fusion | flops 33488896 | bytes 4595712 | tf_op jit(solution)/shard_map/reduce_sum | solution.py:103
  29.4 1.3 broadcast_in_dim.13.b_ref
  30.7 1.3 broadcast_in_dim.15.c_ref
  32.7 17.2 %shard_map.109 = f32[128,4096]{1,0:T(8,128)} custom-call(f32[128,4096]{1,0:T(8,128)} %get-tuple-element.163.delta_ref, f32[128,4096]{1,0:T(8,128)} %get-tuple-element.162.driven_ref, f32[16,4096]{1,0:T(8,128)S(1)} %exponential_negate_fusion.a_ref, f32[16,4096]{1,0:T(8,128)} %broadcast_5_start_ref.2.start_ref, f32[128,16,128]{2,1,0:T(8,128)} %broadcast_in_dim.13.b_ref, ...), custom_call_target="tpu_custom_call" | custom-call | flops 67108864 | bytes 6815744 | tf_op jit(solution)/shard_map/pallas_call | solution.py:66
  49.9 27.8 %all-gather.10.cloned.1.call-done = bf16[16,18,4096]{2,1,0:T(8,128)(2,1)} async-done(((bf16[1,18,4096]{2,1,0:T(8,128)(2,1)}), bf16[16,18,4096]{2,1,0:T(8,128)(2,1)}) %all-gather.10.cloned.1.call-update) | async-done | bytes 2359312 | tf_op jit(solution)/shard_map/all_gather | solution.py:20
  77.7 5.3 %convert_element_type.71 = f32[16,18,4096]{2,1,0:T(8,128)} convert(bf16[16,18,4096]{2,1,0:T(8,128)(2,1)} %all-gather.10.cloned.1.call-done) | non-fusion elementwise | flops 1179648 | bytes 7077888 | tf_op jit(solution)/shard_map/convert_element_type | solution.py:20
  83.1 33.4 %while.14 = (s32[]{:T(128)}, f32[16,4096]{1,0:T(8,128)S(1)}, s32[]{:T(128)}, f32[16,18,4096]{2,1,0:T(8,128)}, f32[16,4096]{1,0:T(8,128)S(1)}, /*index=5*/s32[]{:T(128)}, s32[]{:T(128)}, s32[]{}, s32[]{}) while((s32[]{:T(128)}, f32[16,4096]{1,0:T(8,128)S(1)}, s32[]{:T(128)}, f32[16,18,4096]{2,1,0:T(8,128)}, ...), condition=%wide.region_4.5_spmd.clone, body=%wide.region_3.4_spmd.clone.sunk | while | flops 331782 | bytes 1114265 | solution.py:27
  84.1 1.2 fusion.59
  85.3 1.0 dynamic-slice_add_fusion.2
  86.3 1.2 fusion.59
  87.5 1.0 dynamic-slice_add_fusion.2
  88.5 1.2 fusion.59
  89.7 1.0 dynamic-slice_add_fusion.2
  90.7 1.2 fusion.59
  92.0 1.0 dynamic-slice_add_fusion.2
  93.0 1.2 fusion.59
  94.2 1.0 dynamic-slice_add_fusion.2
  95.2 1.2 fusion.59
  96.4 1.0 dynamic-slice_add_fusion.2
  97.4 1.2 fusion.59
  98.6 1.0 dynamic-slice_add_fusion.2
  99.6 1.2 fusion.59
  101.9 1.2 fusion.59
  104.1 1.2 fusion.59
  106.3 1.2 fusion.59
  108.5 1.2 fusion.59
  110.8 1.2 fusion.59
  113.0 1.2 fusion.59
  115.2 1.2 fusion.59
  118.5 11.8 %multiply_reduce_fusion.1 = (f32[128,2048]{1,0:T(8,128)S(1)}, f32[128,2048]{1,0:T(8,128)S(1)}) fusion(f32[128,16]{1,0:T(8,128)S(1)} %copy.49, f32[16,2048]{1,0:T(8,128)S(1)} %get-tuple-element.155, f32[128,2048]{1,0:T(8,128)S(1)} %get-tuple-element.149, f32[16,2048]{1,0:T(8,128)S(1)} %get-tuple-element.157, f32[16,2048]{1,0:T(8,128)S(1)} %get-tuple-element.154, ...), kind=kLoop, calls=%fused_computation.6 | loop fusion | flops 33030144 | bytes 4726784 | tf_op jit(solution)/shard_map/reduce_sum | solution.py:114
  130.7 1.5 convolution_convert_fusion.1
  132.2 5.6 %copy.56 = bf16[32,20,4096]{2,1,0:T(8,128)(2,1)} copy(bf16[32,20,4096]{2,0,1:T(8,128)(2,1)S(1)} %convolution_convert_fusion.1) | data formatting | bytes 10485760 | tf_op jit(solution)/shard_map/convert_element_type | solution.py:140
  137.8 10.0 %all-to-all-start = ((bf16[32,20,4096]{2,1,0:T(8,128)(2,1)}), bf16[32,20,4096]{2,1,0:T(8,128)(2,1)}, u32[]{:S(2)}, u32[]{:S(2)}) async-start(bf16[32,20,4096]{2,1,0:T(8,128)(2,1)} %copy.56), calls=%async_computation | async-start | bytes 12582912 | tf_op jit(solution)/shard_map/all_to_all | solution.py:141
  148.5 12.8 %all-gather.6.cloned.1.call-done = bf16[1,4096,640]{2,1,0:T(8,128)(2,1)} async-done(((bf16[1,256,640]{2,1,0:T(8,128)(2,1)}), bf16[1,4096,640]{2,1,0:T(8,128)(2,1)}) %all-gather.6.cloned.1.call-update) | async-done | bytes 5242896 | tf_op jit(solution)/shard_map/all_gather | solution.py:145
  161.3 131.1 %all-to-all-done = bf16[32,20,4096]{2,1,0:T(8,128)(2,1)} async-done(((bf16[32,20,4096]{2,1,0:T(8,128)(2,1)}), bf16[32,20,4096]{2,1,0:T(8,128)(2,1)}, u32[]{:S(2)}, u32[]{:S(2)}) %all-to-all-start) | async-done | bytes 5242912 | tf_op jit(solution)/shard_map/all_to_all | solution.py:141
  292.4 8.9 %multiply_convert_fusion = bf16[32,20,640]{2,1,0:T(8,128)(2,1)S(1)} fusion(bf16[32,20,4096]{2,1,0:T(8,128)(2,1)} %all-to-all-done, bf16[1,4096,640]{2,1,0:T(8,128)(2,1)} %all-gather.6.cloned.1.call-done), kind=kOutput, calls=%fused_computation.33 | convolution fusion | flops 3357491200 | bytes 11304960 | tf_op jit(solution)/shard_map/jsc,ch->jsh/dot_general | solution.py:142
  301.3 6.9 %convolution_convert_fusion = bf16[32,20,4096]{2,0,1:T(8,128)(2,1)S(1)} fusion(bf16[1,640,4096]{2,1,0:T(8,128)(2,1)} %all-gather.8.cloned.1.call-done, bf16[32,20,640]{2,1,0:T(8,128)(2,1)S(1)} %multiply_convert_fusion), kind=kOutput, calls=%fused_computation.9 | convolution fusion | flops 3358064640 | bytes 11304960 | tf_op jit(solution)/shard_map/jsh,hc->jsc/dot_general | solution.py:150
  308.3 5.6 %copy.58 = bf16[32,20,4096]{2,1,0:T(8,128)(2,1)} copy(bf16[32,20,4096]{2,0,1:T(8,128)(2,1)S(1)} %convolution_convert_fusion) | data formatting | bytes 10485760 | tf_op jit(solution)/shard_map/optimization_barrier | solution.py:149
  313.8 9.5 %all-to-all-start.1 = ((bf16[32,20,4096]{2,1,0:T(8,128)(2,1)}), bf16[32,20,4096]{2,1,0:T(8,128)(2,1)}, u32[]{:S(2)}, u32[]{:S(2)}) async-start(bf16[32,20,4096]{2,1,0:T(8,128)(2,1)} %copy.58), calls=%async_computation.1 | async-start | bytes 12582912 | tf_op jit(solution)/shard_map/all_to_all | solution.py:157
  324.1 2.0 gather_fusion
  326.4 141.1 %all-to-all-done.1 = bf16[32,20,4096]{2,1,0:T(8,128)(2,1)} async-done(((bf16[32,20,4096]{2,1,0:T(8,128)(2,1)}), bf16[32,20,4096]{2,1,0:T(8,128)(2,1)}, u32[]{:S(2)}, u32[]{:S(2)}) %all-to-all-start.1) | async-done | bytes 5242912 | tf_op jit(solution)/shard_map/all_to_all | solution.py:157
  467.6 6.6 %fusion.10 = f32[2,128,4096]{2,1,0:T(8,128)S(1)} fusion(bf16[32,20,4096]{2,1,0:T(8,128)(2,1)} %all-to-all-done.1, pred[1,32,20,128]{3,1,2,0:T(32,128)(4,1)S(1)} %broadcast_and_fusion, pred[1,32,20,128]{3,1,2,0:T(32,128)(4,1)S(1)} %broadcast_and_fusion.1), kind=kOutput, calls=%fused_computation.19 | convolution fusion | flops 1344438272 | bytes 9601024 | tf_op jit(solution)/shard_map/kjst,jsc->ktc/dot_general | solution.py:159
  474.2 1.5 fusion.22
  (71 shorter events, 14.3 us)
Async XLA Ops:
  6.5 1.6 copy-start
  6.5 11.1 %copy-start.5 = (f32[16,4096]{1,0:T(8,128)S(1)}, f32[16,4096]{1,0:T(8,128)}, u32[]{:S(2)}) copy-start(f32[16,4096]{1,0:T(8,128)} %param.18) | copy-start | bytes 786436
  6.5 11.2 %copy-start.8 = (f32[1,128,32]{1,2,0:T(8,128)S(1)}, f32[1,128,32]{1,2,0:T(8,128)}, u32[]{:S(2)}) copy-start(f32[1,128,32]{1,2,0:T(8,128)} %param.15) | copy-start | bytes 49156
  6.5 71.2 %all-gather.10.cloned.1.call-start = ((), (), s32[]{:S(2)}) async-start(), calls=%async_computation.4 | async-start | bytes 3342336 | tf_op jit(solution)/shard_map/all_gather | solution.py:20
  16.3 1.3 copy-start.2
  29.1 132.3 %all-gather.6.cloned.1.call-start = ((), (), s32[]{:S(2)}) async-start(), calls=%async_computation.2 | async-start | bytes 5570560 | tf_op jit(solution)/shard_map/all_gather | solution.py:145
  83.1 33.4 %copy-start.9 = (s32[1,128,2]{1,2,0:T(2,128)S(1)}, s32[1,128,2]{1,2,0:T(2,128)}, u32[]{:S(2)}) copy-start(s32[1,128,2]{1,2,0:T(2,128)} %param.21) | copy-start | bytes 3076
  118.4 11.8 %copy-start.3 = (f32[128,4096]{1,0:T(8,128)S(1)}, f32[128,4096]{1,0:T(8,128)}, u32[]{:S(2)}) copy-start(f32[128,4096]{1,0:T(8,128)} %shard_map.109) | copy-start | bytes 6291460
  118.4 11.8 %copy-start.4 = (bf16[1,128,4096]{2,1,0:T(8,128)(2,1)S(1)}, bf16[1,128,4096]{2,1,0:T(8,128)(2,1)}, u32[]{:S(2)}) copy-start(bf16[1,128,4096]{2,1,0:T(8,128)(2,1)} %param.13) | copy-start | bytes 3145732
  118.5 11.8 %copy-start.7 = (f32[4096]{0:T(1024)S(1)}, f32[4096]{0:T(1024)}, u32[]{:S(2)}) copy-start(f32[4096]{0:T(1024)} %param.19) | copy-start | bytes 49156
  137.8 154.7 %all-to-all-start = ((bf16[32,20,4096]{2,1,0:T(8,128)(2,1)}), bf16[32,20,4096]{2,1,0:T(8,128)(2,1)}, u32[]{:S(2)}, u32[]{:S(2)}) async-start(bf16[32,20,4096]{2,1,0:T(8,128)(2,1)} %copy.56), calls=%async_computation | async-start | bytes 12582912 | tf_op jit(solution)/shard_map/all_to_all | solution.py:141
  147.8 153.5 %all-gather.8.cloned.1.call-start = ((), (), s32[]{:S(2)}) async-start(), calls=%async_computation.3 | async-start | bytes 5570560 | tf_op jit(solution)/shard_map/all_gather | solution.py:153
  313.8 9.9 %copy-start.6 = (bf16[16,4096]{1,0:T(8,128)(2,1)S(1)}, bf16[16,4096]{1,0:T(8,128)(2,1)}, u32[]{:S(2)}) copy-start(bf16[16,4096]{1,0:T(8,128)(2,1)} %param.20) | copy-start | bytes 393220
  313.8 153.7 %all-to-all-start.1 = ((bf16[32,20,4096]{2,1,0:T(8,128)(2,1)}), bf16[32,20,4096]{2,1,0:T(8,128)(2,1)}, u32[]{:S(2)}, u32[]{:S(2)}) async-start(bf16[32,20,4096]{2,1,0:T(8,128)(2,1)} %copy.58), calls=%async_computation.1 | async-start | bytes 12582912 | tf_op jit(solution)/shard_map/all_to_all | solution.py:157
  467.6 8.2 %copy-start.1 = (bf16[256,4096]{1,0:T(8,128)(2,1)S(1)}, bf16[256,4096]{1,0:T(8,128)(2,1)}, u32[]{:S(2)}) copy-start(bf16[256,4096]{1,0:T(8,128)(2,1)} %param.16) | copy-start | bytes 6291460
Sparse Core Ops, SparseCore 0:
  29.2 48.5 all-gather.9
  116.6 44.7 all-gather.5
  163.4 52.9 all-gather.7

commit v10 on v8

--- a/solution.py
+++ b/solution.py
@@ -108,9 +108,9 @@
     start, local, w_up, w_down = lax.optimization_barrier((start, local, w_up, w_down))
     carried = []
     for lower in range(0, channels, span):
-        decay = jnp.exp(a_neg[None, :, lower : lower + span] * cumulated[:, None, lower : lower + span])
+        decay = jnp.exp(a_neg[:, None, lower : lower + span] * cumulated[None, :, lower : lower + span])
         carried.append(
-            jnp.sum(decay * start[None, :, lower : lower + span] * c_out[:, :, None], axis=1)
+            jnp.sum(decay * start[:, None, lower : lower + span] * c_out.T[:, :, None], axis=0)
         )
     scanned = local + jnp.concatenate(carried, axis=1)
     mixer = (scanned + d_skip * xfloat).astype(jnp.bfloat16)

time: 454 us -> 451 us (level)
  other arithmetic: 33.8 us -> 29.2 us
  transfers between devices with their start and end apart: 5 -> 5, of which waited for: 4 -> 4; matrix products, arithmetic and copies ran while one was open for 9% -> 8% of each run, Pallas kernels for 4% -> 4%
where the time goes in v10:
time: 451 us; the launch traced here: 450 us
  waiting for transfers between devices  314 us (70%)
  other arithmetic  29.2 us (6%)
  matrix products  29.1 us (6%)
  local copies, waits for them, and re-layouts  26.8 us (6%)
  starting transfers between devices  20.4 us (5%)
  Pallas kernels  17.3 us (4%)
  between operations  13.9 us (3%)
    all_to_all x1, waiting for transfers between devices, per_device(): lax.all_to_all(partial_out, 'exp', split_axis=0, concat_axis=0, tiled=True)  141 us
    all_to_all x1, waiting for transfers between devices, per_device(): lax.all_to_all(outgoing, 'exp', split_axis=0, concat_axis=0, tiled=True)  131 us
    all_gather x1, waiting for transfers between devices, carry_in(): every = lax.all_gather(packed, 'seq').astype(jnp.float32)  27.7 us
    pallas_call x1, Pallas kernels, sweep(): pl.pallas_call(sweep_kernel, out_shape=jax.ShapeDtypeStruct((tokens_here,...  17.3 us
    all_gather x1, waiting for transfers between devices, per_device(): lax.all_gather(w_up, 'seq', axis=1, tiled=True)[0]  12.9 us
    all_to_all x1, starting transfers between devices, per_device(): lax.all_to_all(partial_out, 'exp', split_axis=0, concat_axis=0, tiled=True)  10.2 us
    all_to_all x1, starting transfers between devices, per_device(): lax.all_to_all(outgoing, 'exp', split_axis=0, concat_axis=0, tiled=True)  9.99 us
    reduce_sum x2, other arithmetic, per_device(): jnp.sum(decay * start[:, None, lower:lower + span] * c_out.T[:, :, None],...  9.39 us
  transfers between devices with their start and end apart: 5, of which 4 were waited for; matrix products, arithmetic and copies ran while one was open for 8% of the time, Pallas kernels for 4%

profile of v10, /device:TPU:7, one launch (start us, length us, event | category | flops | bytes accessed | tf_op | source)
XLA Modules:
  0.0 450.3 jit_solution(10195332568434326496)
XLA Ops:
  6.5 1.6 copy-done
  8.1 4.8 %convert_multiply_fusion.1 = (f32[128,4096]{1,0:T(8,128)}, f32[128,4096]{1,0:T(8,128)}) fusion(bf16[1,128,4096]{2,1,0:T(8,128)(2,1)} %param.11, f32[4096]{0:T(1024)} %param.15, bf16[256,4096]{1,0:T(8,128)(2,1)S(1)} %copy-done, bf16[1,128,256]{2,1,0:T(8,128)(2,1)} %param.12), kind=kOutput, calls=%fused_computation.30 | convolution fusion | flops 273154048 | bytes 7421952 | tf_op jit(solution)/shard_map/dot_general | solution.py:86
  13.0 3.5 reduce_window_sum.26
  16.4 0.6 fusion.78
  17.1 2.8 fusion.79
  20.0 0.7 fusion.81
  20.7 0.6 slice_bitcast_fusion.18
  21.6 1.1 fusion.76
  22.7 1.7 multiply_reduce_fusion.9
  24.6 5.6 %multiply_reduce_fusion.8 = (bf16[16,512]{1,0:T(8,128)(2,1)S(1)}, bf16[16,512]{1,0:T(8,128)(2,1)S(1)}, bf16[16,512]{1,0:T(8,128)(2,1)S(1)}, bf16[16,512]{1,0:T(8...) fusion(f32[128,512]{1,0:T(8,128)S(1)} %copy-done.7, f32[128,512]{1,0:T(8,128)S(1)} %get-tuple-element.58, ...), kind=kLoop, calls=%fused_computation.21 | loop fusion | flops 25116672 | bytes 3448832 | tf_op jit(solution)/shard_map/reduce_sum | solution.py:102
  30.2 0.8 maximum_bitcast_fusion
  31.0 0.2 all-gather.6.cloned.1.call-start
  31.4 1.3 broadcast_in_dim.11.b_ref
  32.7 1.3 broadcast_in_dim.13.c_ref
  34.0 0.7 broadcast_5_start_ref.2.start_ref
  34.8 17.3 %shard_map.109 = f32[128,4096]{1,0:T(8,128)} custom-call(f32[128,4096]{1,0:T(8,128)} %get-tuple-element.104.delta_ref, f32[128,4096]{1,0:T(8,128)} %get-tuple-element.103.driven_ref, f32[16,4096]{1,0:T(8,128)} %copy-done.4, f32[16,4096]{1,0:T(8,128)} %broadcast_5_start_ref.2.start_ref, f32[128,16,128]{2,1,0:T(8,128)} %broadcast_in_dim.11.b_ref, ...), custom_call_target="tpu_custom_call" | custom-call | flops 67108864 | bytes 6815744 | tf_op jit(solution)/shard_map/pallas_call | solution.py:65
  52.0 27.7 %all-gather.10.cloned.1.call-done = bf16[16,18,4096]{2,1,0:T(8,128)(2,1)} async-done(((bf16[1,18,4096]{2,1,0:T(8,128)(2,1)}), bf16[16,18,4096]{2,1,0:T(8,128)(2,1)}) %all-gather.10.cloned.1.call-update) | async-done | bytes 2359312 | tf_op jit(solution)/shard_map/all_gather | solution.py:20
  79.7 2.6 convert_element_type.71
  82.4 0.2 slice_add_fusion.14
  82.6 1.1 fusion.30
  84.0 0.1 eq.114
  84.1 0.1 eq.110
  84.2 0.6 reduce-window.6
  84.8 0.2 slice_reduce_fusion.4
  85.2 0.1 sub.143
  85.3 0.2 slice_reduce_fusion.2
  85.5 0.2 slice_reduce_fusion.3
  85.9 2.6 multiply_reduce_fusion.1
  88.6 6.8 %multiply_reduce_fusion = (f32[128,512]{1,0:T(8,128)S(1)}, f32[128,512]{1,0:T(8,128)S(1)}, f32[128,512]{1,0:T(8,128)S(1)}, f32[128,512]{1,0:T(8,128)S(1)}, f32[128,512]{1,0:T(8,128)S(1)}, /*index=5*/f32[128,512]{1,0:T(8,128)S(1)}) fusion(f32[16,512]{1,0:T(8,128)S(1)} %get-tuple-element.83, f32[128,512]{1,0:T(8,128)S(1)} %get-tuple-element.59, ...), kind=kLoop, calls=%fused_computation.13 | loop fusion | flops 24772608 | bytes 3547136 | tf_op jit(solution)/shard_map/reduce_sum | solution.py:113
  95.6 1.4 copy-done.2
  97.0 0.4 copy-done.5
  97.4 0.4 fusion.12
  97.9 1.5 convolution_convert_fusion.1
  99.4 5.6 %copy.51 = bf16[32,20,4096]{2,1,0:T(8,128)(2,1)} copy(bf16[32,20,4096]{2,0,1:T(8,128)(2,1)S(1)} %convolution_convert_fusion.1) | data formatting | bytes 10485760 | tf_op jit(solution)/shard_map/convert_element_type | solution.py:139
  105.0 10.0 %all-to-all-start = ((bf16[32,20,4096]{2,1,0:T(8,128)(2,1)}), bf16[32,20,4096]{2,1,0:T(8,128)(2,1)}, u32[]{:S(2)}, u32[]{:S(2)}) async-start(bf16[32,20,4096]{2,1,0:T(8,128)(2,1)} %copy.51), calls=%async_computation | async-start | bytes 12582912 | tf_op jit(solution)/shard_map/all_to_all | solution.py:140
  115.0 0.7 all-gather.8.cloned.1.call-update
  115.7 12.9 %all-gather.6.cloned.1.call-done = bf16[1,4096,640]{2,1,0:T(8,128)(2,1)} async-done(((bf16[1,256,640]{2,1,0:T(8,128)(2,1)}), bf16[1,4096,640]{2,1,0:T(8,128)(2,1)}) %all-gather.6.cloned.1.call-update) | async-done | bytes 5242896 | tf_op jit(solution)/shard_map/all_gather | solution.py:144
  128.6 131.1 %all-to-all-done = bf16[32,20,4096]{2,1,0:T(8,128)(2,1)} async-done(((bf16[32,20,4096]{2,1,0:T(8,128)(2,1)}), bf16[32,20,4096]{2,1,0:T(8,128)(2,1)}, u32[]{:S(2)}, u32[]{:S(2)}) %all-to-all-start) | async-done | bytes 5242912 | tf_op jit(solution)/shard_map/all_to_all | solution.py:140
  259.7 8.9 %multiply_convert_fusion = bf16[32,20,640]{2,1,0:T(8,128)(2,1)S(1)} fusion(bf16[32,20,4096]{2,1,0:T(8,128)(2,1)} %all-to-all-done, bf16[1,4096,640]{2,1,0:T(8,128)(2,1)} %all-gather.6.cloned.1.call-done), kind=kOutput, calls=%fused_computation.40 | convolution fusion | flops 3357491200 | bytes 11304960 | tf_op jit(solution)/shard_map/jsc,ch->jsh/dot_general | solution.py:141
  268.6 6.9 %convolution_convert_fusion = bf16[32,20,4096]{2,0,1:T(8,128)(2,1)S(1)} fusion(bf16[1,640,4096]{2,1,0:T(8,128)(2,1)} %all-gather.8.cloned.1.call-done, bf16[32,20,640]{2,1,0:T(8,128)(2,1)S(1)} %multiply_convert_fusion), kind=kOutput, calls=%fused_computation.1 | convolution fusion | flops 3358064640 | bytes 11304960 | tf_op jit(solution)/shard_map/jsh,hc->jsc/dot_general | solution.py:149
  275.5 5.6 %copy.53 = bf16[32,20,4096]{2,1,0:T(8,128)(2,1)} copy(bf16[32,20,4096]{2,0,1:T(8,128)(2,1)S(1)} %convolution_convert_fusion) | data formatting | bytes 10485760 | tf_op jit(solution)/shard_map/optimization_barrier | solution.py:148
  281.1 10.2 %all-to-all-start.1 = ((bf16[32,20,4096]{2,1,0:T(8,128)(2,1)}), bf16[32,20,4096]{2,1,0:T(8,128)(2,1)}, u32[]{:S(2)}, u32[]{:S(2)}) async-start(bf16[32,20,4096]{2,1,0:T(8,128)(2,1)} %copy.53), calls=%async_computation.1 | async-start | bytes 12582912 | tf_op jit(solution)/shard_map/all_to_all | solution.py:156
  291.7 0.4 fusion.82
  292.0 2.0 gather_fusion
  294.2 0.2 fusion.75
  294.4 141.2 %all-to-all-done.1 = bf16[32,20,4096]{2,1,0:T(8,128)(2,1)} async-done(((bf16[32,20,4096]{2,1,0:T(8,128)(2,1)}), bf16[32,20,4096]{2,1,0:T(8,128)(2,1)}, u32[]{:S(2)}, u32[]{:S(2)}) %all-to-all-start.1) | async-done | bytes 5242912 | tf_op jit(solution)/shard_map/all_to_all | solution.py:156
  435.6 6.6 %fusion.8 = f32[2,128,4096]{2,1,0:T(8,128)S(1)} fusion(bf16[32,20,4096]{2,1,0:T(8,128)(2,1)} %all-to-all-done.1, pred[1,32,20,128]{3,1,2,0:T(32,128)(4,1)S(1)} %broadcast_and_fusion, pred[1,32,20,128]{3,1,2,0:T(32,128)(4,1)S(1)} %broadcast_and_fusion.1), kind=kOutput, calls=%fused_computation.11 | convolution fusion | flops 1344438272 | bytes 9601024 | tf_op jit(solution)/shard_map/kjst,jsc->ktc/dot_general | solution.py:158
  442.2 1.5 fusion.20
  (98 shorter events, 1.7 us)
Async XLA Ops:
  6.5 1.6 copy-start
  6.5 73.2 %all-gather.10.cloned.1.call-start = ((), (), s32[]{:S(2)}) async-start(), calls=%async_computation.4 | async-start | bytes 3342336 | tf_op jit(solution)/shard_map/all_gather | solution.py:20
  13.0 7.0 %copy-start.3 = (f32[16,4096]{1,0:T(8,128)S(1)}, f32[16,4096]{1,0:T(8,128)}, u32[]{:S(2)}) copy-start(f32[16,4096]{1,0:T(8,128)} %param.16) | copy-start | bytes 786436
  13.0 7.8 %copy-start.25 = (f32[1,128,32]{1,2,0:T(8,128)S(1)}, f32[1,128,32]{1,2,0:T(8,128)}, u32[]{:S(2)}) copy-start(f32[1,128,32]{1,2,0:T(8,128)} %param.13) | copy-start | bytes 49156
  20.0 4.5 copy-start.4
  21.4 1.3 copy-start.12
  21.4 1.3 copy-start.13
  21.4 1.3 copy-start.22
  21.4 1.3 copy-start.23
  21.5 3.0 copy-start.6
  21.5 3.0 copy-start.7
  21.5 3.0 copy-start.8
  21.5 3.0 copy-start.9
  21.5 3.0 copy-start.10
  21.5 3.0 copy-start.11
  21.5 3.0 copy-start.15
  21.5 3.0 copy-start.17
  21.5 3.0 copy-start.19
  21.5 3.0 copy-start.20
  21.6 3.0 copy-start.21
  31.0 97.6 %all-gather.6.cloned.1.call-start = ((), (), s32[]{:S(2)}) async-start(), calls=%async_computation.2 | async-start | bytes 5570560 | tf_op jit(solution)/shard_map/all_gather | solution.py:144
  82.4 1.5 copy-start.27
  82.6 3.3 copy-start.26
  83.8 4.8 %copy-start.16 = (f32[16,512]{1,0:T(8,128)S(1)}, f32[16,512]{1,0:T(8,128)}, u32[]{:S(2)}) copy-start(f32[16,512]{1,0:T(8,128)} %get-tuple-element.91) | copy-start | bytes 98308
  83.8 4.8 %copy-start.18 = (f32[16,512]{1,0:T(8,128)S(1)}, f32[16,512]{1,0:T(8,128)}, u32[]{:S(2)}) copy-start(f32[16,512]{1,0:T(8,128)} %get-tuple-element.93) | copy-start | bytes 98308
  88.6 7.0 %copy-start.24 = (f32[4096]{0:T(1024)S(1)}, f32[4096]{0:T(1024)}, u32[]{:S(2)}) copy-start(f32[4096]{0:T(1024)} %param.17) | copy-start | bytes 49156
  95.4 1.6 copy-start.2
  95.4 2.0 copy-start.5
  105.0 154.7 %all-to-all-start = ((bf16[32,20,4096]{2,1,0:T(8,128)(2,1)}), bf16[32,20,4096]{2,1,0:T(8,128)(2,1)}, u32[]{:S(2)}, u32[]{:S(2)}) async-start(bf16[32,20,4096]{2,1,0:T(8,128)(2,1)} %copy.51), calls=%async_computation | async-start | bytes 12582912 | tf_op jit(solution)/shard_map/all_to_all | solution.py:140
  115.0 153.6 %all-gather.8.cloned.1.call-start = ((), (), s32[]{:S(2)}) async-start(), calls=%async_computation.3 | async-start | bytes 5570560 | tf_op jit(solution)/shard_map/all_gather | solution.py:152
  281.1 10.6 %copy-start.14 = (bf16[16,4096]{1,0:T(8,128)(2,1)S(1)}, bf16[16,4096]{1,0:T(8,128)(2,1)}, u32[]{:S(2)}) copy-start(bf16[16,4096]{1,0:T(8,128)(2,1)} %param.18) | copy-start | bytes 393220
  281.1 154.5 %all-to-all-start.1 = ((bf16[32,20,4096]{2,1,0:T(8,128)(2,1)}), bf16[32,20,4096]{2,1,0:T(8,128)(2,1)}, u32[]{:S(2)}, u32[]{:S(2)}) async-start(bf16[32,20,4096]{2,1,0:T(8,128)(2,1)} %copy.53), calls=%async_computation.1 | async-start | bytes 12582912 | tf_op jit(solution)/shard_map/all_to_all | solution.py:156
  435.6 8.2 %copy-start.1 = (bf16[256,4096]{1,0:T(8,128)(2,1)S(1)}, bf16[256,4096]{1,0:T(8,128)(2,1)}, u32[]{:S(2)}) copy-start(bf16[256,4096]{1,0:T(8,128)(2,1)} %param.14) | copy-start | bytes 6291460
Sparse Core Ops, SparseCore 0:
  31.2 48.5 all-gather.9
  83.9 44.6 all-gather.5
  130.6 53.0 all-gather.7

commit v11 on v10

--- a/solution.py
+++ b/solution.py
@@ -89,7 +89,9 @@
     driven = delta * xfloat
     b_in = b_c[0, :, :nstate]
     c_out = b_c[0, :, nstate:]
-    cumulated = jnp.cumsum(delta, axis=0)
+    order = jnp.arange(tokens_here, dtype=jnp.int32)
+    lower_ones = (order[:, None] >= order[None, :]).astype(jnp.float32)
+    cumulated = jnp.dot(lower_ones, delta, precision=lax.Precision.HIGHEST)
     pieces = max(1, channels // 512)
     span = channels // pieces
     ends = []

time: 451 us -> 443 us (0.982)
  no operation moved by 1% of the time
where the time goes in v11:
time: 443 us
  waiting for transfers between devices  313 us (71%)
  matrix products  28.3 us (6%)
  local copies, waits for them, and re-layouts  25.1 us (6%)
  other arithmetic  25 us (6%)
  starting transfers between devices  19.7 us (4%)
  Pallas kernels  17.3 us (4%)
  between operations  14 us (3%)
    all_to_all x1, waiting for transfers between devices, per_device(): lax.all_to_all(partial_out, 'exp', split_axis=0, concat_axis=0, tiled=True)  141 us
    all_to_all x1, waiting for transfers between devices, per_device(): lax.all_to_all(outgoing, 'exp', split_axis=0, concat_axis=0, tiled=True)  130 us
    all_gather x1, waiting for transfers between devices, carry_in(): every = lax.all_gather(packed, 'seq').astype(jnp.float32)  27.7 us
    pallas_call x1, Pallas kernels, sweep(): pl.pallas_call(sweep_kernel, out_shape=jax.ShapeDtypeStruct((tokens_here,...  17.3 us
    all_gather x1, waiting for transfers between devices, per_device(): lax.all_gather(w_up, 'seq', axis=1, tiled=True)[0]  13.9 us
    all_to_all x1, starting transfers between devices, per_device(): lax.all_to_all(outgoing, 'exp', split_axis=0, concat_axis=0, tiled=True)  9.98 us
    all_to_all x1, starting transfers between devices, per_device(): lax.all_to_all(partial_out, 'exp', split_axis=0, concat_axis=0, tiled=True)  9.48 us
  transfers between devices with their start and end apart: 5, of which 4 were waited for; matrix products, arithmetic and copies ran while one was open for 8% of the time, Pallas kernels for 4%

profile of v11, /device:TPU:7, one launch (start us, length us, event | category | flops | bytes accessed | tf_op | source)
XLA Modules:
  0.0 442.8 jit_solution(11650839191858296321)
XLA Ops:
  6.5 1.6 copy-done
  8.1 2.8 convert_multiply_fusion.1
  11.0 1.2 fusion.68
  12.1 0.6 fusion.79
  12.8 1.3 fusion.80
  14.2 0.7 fusion.82
  14.9 0.6 slice_bitcast_fusion.18
  15.8 1.1 fusion.77
  16.9 1.7 multiply_reduce_fusion.9
  18.8 5.6 %multiply_reduce_fusion.8 = (bf16[16,512]{1,0:T(8,128)(2,1)S(1)}, bf16[16,512]{1,0:T(8,128)(2,1)S(1)}, bf16[16,512]{1,0:T(8,128)(2,1)S(1)}, bf16[16,512]{1,0:T(8...) fusion(f32[128,512]{1,0:T(8,128)S(1)} %copy-done.9, f32[128,512]{1,0:T(8,128)S(1)} %get-tuple-element.58, ...), kind=kLoop, calls=%fused_computation.21 | loop fusion | flops 25116672 | bytes 3448832 | tf_op jit(solution)/shard_map/reduce_sum | solution.py:104
  24.4 0.8 maximum_bitcast_fusion
  25.2 0.2 all-gather.6.cloned.1.call-start
  25.6 1.3 broadcast_in_dim.11.b_ref
  26.9 1.3 broadcast_in_dim.13.c_ref
  28.2 0.7 broadcast_5_start_ref.2.start_ref
  29.0 17.3 %shard_map.109 = f32[128,4096]{1,0:T(8,128)} custom-call(f32[128,4096]{1,0:T(8,128)} %copy-done.4, f32[128,4096]{1,0:T(8,128)} %copy-done.3, f32[16,4096]{1,0:T(8,128)} %copy-done.6, f32[16,4096]{1,0:T(8,128)} %broadcast_5_start_ref.2.start_ref, f32[128,16,128]{2,1,0:T(8,128)} %broadcast_in_dim.11.b_ref, f32[128,16,128]{2,1,0:T(8,128)} %broadcast_in_dim.13.c_ref), custom_call_target="tpu_custom_call" | custom-call | flops 67108864 | bytes 6815744 | tf_op jit(solution)/shard_map/pallas_call | solution.py:65
  46.2 27.7 %all-gather.10.cloned.1.call-done = bf16[16,18,4096]{2,1,0:T(8,128)(2,1)} async-done(((bf16[1,18,4096]{2,1,0:T(8,128)(2,1)}), bf16[16,18,4096]{2,1,0:T(8,128)(2,1)}) %all-gather.10.cloned.1.call-update) | async-done | bytes 2359312 | tf_op jit(solution)/shard_map/all_gather | solution.py:20
  73.9 2.6 convert_element_type.72
  76.6 0.1 slice_add_fusion.14
  76.8 1.1 fusion.30
  78.2 0.1 eq.114
  78.3 0.1 eq.110
  78.5 0.6 reduce-window.6
  79.0 0.2 slice_reduce_fusion.4
  79.4 0.1 sub.143
  79.5 0.2 slice_reduce_fusion.2
  79.7 0.2 slice_reduce_fusion.3
  80.1 2.7 multiply_reduce_fusion.1
  82.9 6.0 %multiply_reduce_fusion = (f32[128,512]{1,0:T(8,128)S(1)}, f32[128,512]{1,0:T(8,128)S(1)}, f32[128,512]{1,0:T(8,128)S(1)}, f32[128,512]{1,0:T(8,128)S(1)}, f32[128,512]{1,0:T(8,128)S(1)}, /*index=5*/f32[128,512]{1,0:T(8,128)S(1)}) fusion(f32[16,512]{1,0:T(8,128)S(1)} %get-tuple-element.83, f32[128,512]{1,0:T(8,128)S(1)} %get-tuple-element.59, ...), kind=kLoop, calls=%fused_computation.13 | loop fusion | flops 24772608 | bytes 3547136 | tf_op jit(solution)/shard_map/reduce_sum | solution.py:115
  89.1 1.4 copy-done.2
  90.5 0.3 copy-done.7
  90.7 0.4 fusion.12
  91.2 1.5 convolution_convert_fusion.1
  92.7 5.6 %copy.51 = bf16[32,20,4096]{2,1,0:T(8,128)(2,1)} copy(bf16[32,20,4096]{2,0,1:T(8,128)(2,1)S(1)} %convolution_convert_fusion.1) | data formatting | bytes 10485760 | tf_op jit(solution)/shard_map/convert_element_type | solution.py:141
  98.3 10.0 %all-to-all-start = ((bf16[32,20,4096]{2,1,0:T(8,128)(2,1)}), bf16[32,20,4096]{2,1,0:T(8,128)(2,1)}, u32[]{:S(2)}, u32[]{:S(2)}) async-start(bf16[32,20,4096]{2,1,0:T(8,128)(2,1)} %copy.51), calls=%async_computation | async-start | bytes 12582912 | tf_op jit(solution)/shard_map/all_to_all | solution.py:142
  108.3 0.7 all-gather.8.cloned.1.call-update
  109.0 13.9 %all-gather.6.cloned.1.call-done = bf16[1,4096,640]{2,1,0:T(8,128)(2,1)} async-done(((bf16[1,256,640]{2,1,0:T(8,128)(2,1)}), bf16[1,4096,640]{2,1,0:T(8,128)(2,1)}) %all-gather.6.cloned.1.call-update) | async-done | bytes 5242896 | tf_op jit(solution)/shard_map/all_gather | solution.py:146
  122.9 130.0 %all-to-all-done = bf16[32,20,4096]{2,1,0:T(8,128)(2,1)} async-done(((bf16[32,20,4096]{2,1,0:T(8,128)(2,1)}), bf16[32,20,4096]{2,1,0:T(8,128)(2,1)}, u32[]{:S(2)}, u32[]{:S(2)}) %all-to-all-start) | async-done | bytes 5242912 | tf_op jit(solution)/shard_map/all_to_all | solution.py:142
  252.9 8.9 %multiply_convert_fusion = bf16[32,20,640]{2,1,0:T(8,128)(2,1)S(1)} fusion(bf16[32,20,4096]{2,1,0:T(8,128)(2,1)} %all-to-all-done, bf16[1,4096,640]{2,1,0:T(8,128)(2,1)} %all-gather.6.cloned.1.call-done), kind=kOutput, calls=%fused_computation.40 | convolution fusion | flops 3357491200 | bytes 11304960 | tf_op jit(solution)/shard_map/jsc,ch->jsh/dot_general | solution.py:143
  261.8 6.9 %convolution_convert_fusion = bf16[32,20,4096]{2,0,1:T(8,128)(2,1)S(1)} fusion(bf16[1,640,4096]{2,1,0:T(8,128)(2,1)} %all-gather.8.cloned.1.call-done, bf16[32,20,640]{2,1,0:T(8,128)(2,1)S(1)} %multiply_convert_fusion), kind=kOutput, calls=%fused_computation.1 | convolution fusion | flops 3358064640 | bytes 11304960 | tf_op jit(solution)/shard_map/jsh,hc->jsc/dot_general | solution.py:151
  268.7 5.6 %copy.53 = bf16[32,20,4096]{2,1,0:T(8,128)(2,1)} copy(bf16[32,20,4096]{2,0,1:T(8,128)(2,1)S(1)} %convolution_convert_fusion) | data formatting | bytes 10485760 | tf_op jit(solution)/shard_map/optimization_barrier | solution.py:150
  274.3 9.5 %all-to-all-start.1 = ((bf16[32,20,4096]{2,1,0:T(8,128)(2,1)}), bf16[32,20,4096]{2,1,0:T(8,128)(2,1)}, u32[]{:S(2)}, u32[]{:S(2)}) async-start(bf16[32,20,4096]{2,1,0:T(8,128)(2,1)} %copy.53), calls=%async_computation.1 | async-start | bytes 12582912 | tf_op jit(solution)/shard_map/all_to_all | solution.py:158
  284.2 0.4 fusion.83
  284.6 2.0 gather_fusion
  286.7 0.2 fusion.76
  286.9 141.1 %all-to-all-done.1 = bf16[32,20,4096]{2,1,0:T(8,128)(2,1)} async-done(((bf16[32,20,4096]{2,1,0:T(8,128)(2,1)}), bf16[32,20,4096]{2,1,0:T(8,128)(2,1)}, u32[]{:S(2)}, u32[]{:S(2)}) %all-to-all-start.1) | async-done | bytes 5242912 | tf_op jit(solution)/shard_map/all_to_all | solution.py:158
  428.0 6.6 %fusion.8 = f32[2,128,4096]{2,1,0:T(8,128)S(1)} fusion(bf16[32,20,4096]{2,1,0:T(8,128)(2,1)} %all-to-all-done.1, pred[1,32,20,128]{3,1,2,0:T(32,128)(4,1)S(1)} %broadcast_and_fusion, pred[1,32,20,128]{3,1,2,0:T(32,128)(4,1)S(1)} %broadcast_and_fusion.1), kind=kOutput, calls=%fused_computation.11 | convolution fusion | flops 1344438272 | bytes 9601024 | tf_op jit(solution)/shard_map/kjst,jsc->ktc/dot_general | solution.py:160
  434.7 1.5 fusion.20
  (108 shorter events, 1.8 us)
Async XLA Ops:
  6.5 1.6 copy-start
  6.5 67.4 %all-gather.10.cloned.1.call-start = ((), (), s32[]{:S(2)}) async-start(), calls=%async_computation.4 | async-start | bytes 3342336 | tf_op jit(solution)/shard_map/all_gather | solution.py:20
  10.9 3.2 copy-start.3
  10.9 3.2 copy-start.4
  10.9 3.2 copy-start.5
  11.0 4.0 copy-start.30
  14.2 4.5 %copy-start.6 = (f32[16,4096]{1,0:T(8,128)}, f32[16,4096]{1,0:T(8,128)S(1)}, u32[]{:S(2)}) copy-start(f32[16,4096]{1,0:T(8,128)S(1)} %exponential_negate_fusion.a_ref) | copy-start | bytes 786436
  15.6 1.3 copy-start.14
  15.6 1.3 copy-start.15
  15.6 1.3 copy-start.27
  15.6 1.3 copy-start.28
  15.7 3.0 copy-start.8
  15.7 3.0 copy-start.9
  15.7 3.0 copy-start.10
  15.7 3.0 copy-start.11
  15.7 3.0 copy-start.12
  15.7 3.0 copy-start.13
  15.7 3.0 copy-start.17
  15.7 3.0 copy-start.19
  15.7 3.0 copy-start.21
  15.8 3.0 copy-start.23
  15.8 3.0 copy-start.25
  25.2 97.6 %all-gather.6.cloned.1.call-start = ((), (), s32[]{:S(2)}) async-start(), calls=%async_computation.2 | async-start | bytes 5570560 | tf_op jit(solution)/shard_map/all_gather | solution.py:146
  76.6 1.4 copy-start.32
  76.8 3.3 copy-start.31
  78.0 4.8 %copy-start.18 = (f32[16,512]{1,0:T(8,128)S(1)}, f32[16,512]{1,0:T(8,128)}, u32[]{:S(2)}) copy-start(f32[16,512]{1,0:T(8,128)} %get-tuple-element.91) | copy-start | bytes 98308
  78.0 4.8 %copy-start.20 = (f32[16,512]{1,0:T(8,128)S(1)}, f32[16,512]{1,0:T(8,128)}, u32[]{:S(2)}) copy-start(f32[16,512]{1,0:T(8,128)} %get-tuple-element.93) | copy-start | bytes 98308
  78.0 4.8 %copy-start.22 = (f32[16,512]{1,0:T(8,128)S(1)}, f32[16,512]{1,0:T(8,128)}, u32[]{:S(2)}) copy-start(f32[16,512]{1,0:T(8,128)} %get-tuple-element.94) | copy-start | bytes 98308
  78.0 4.8 %copy-start.24 = (f32[16,512]{1,0:T(8,128)S(1)}, f32[16,512]{1,0:T(8,128)}, u32[]{:S(2)}) copy-start(f32[16,512]{1,0:T(8,128)} %get-tuple-element.95) | copy-start | bytes 98308
  78.0 4.8 %copy-start.26 = (f32[16,512]{1,0:T(8,128)S(1)}, f32[16,512]{1,0:T(8,128)}, u32[]{:S(2)}) copy-start(f32[16,512]{1,0:T(8,128)} %get-tuple-element.96) | copy-start | bytes 98308
  82.9 6.2 %copy-start.29 = (f32[4096]{0:T(1024)S(1)}, f32[4096]{0:T(1024)}, u32[]{:S(2)}) copy-start(f32[4096]{0:T(1024)} %param.17) | copy-start | bytes 49156
  88.9 1.6 copy-start.2
  88.9 1.8 copy-start.7
  98.3 154.7 %all-to-all-start = ((bf16[32,20,4096]{2,1,0:T(8,128)(2,1)}), bf16[32,20,4096]{2,1,0:T(8,128)(2,1)}, u32[]{:S(2)}, u32[]{:S(2)}) async-start(bf16[32,20,4096]{2,1,0:T(8,128)(2,1)} %copy.51), calls=%async_computation | async-start | bytes 12582912 | tf_op jit(solution)/shard_map/all_to_all | solution.py:142
  108.2 153.5 %all-gather.8.cloned.1.call-start = ((), (), s32[]{:S(2)}) async-start(), calls=%async_computation.3 | async-start | bytes 5570560 | tf_op jit(solution)/shard_map/all_gather | solution.py:154
  274.3 9.9 %copy-start.16 = (bf16[16,4096]{1,0:T(8,128)(2,1)S(1)}, bf16[16,4096]{1,0:T(8,128)(2,1)}, u32[]{:S(2)}) copy-start(bf16[16,4096]{1,0:T(8,128)(2,1)} %param.18) | copy-start | bytes 393220
  274.3 153.7 %all-to-all-start.1 = ((bf16[32,20,4096]{2,1,0:T(8,128)(2,1)}), bf16[32,20,4096]{2,1,0:T(8,128)(2,1)}, u32[]{:S(2)}, u32[]{:S(2)}) async-start(bf16[32,20,4096]{2,1,0:T(8,128)(2,1)} %copy.53), calls=%async_computation.1 | async-start | bytes 12582912 | tf_op jit(solution)/shard_map/all_to_all | solution.py:158
  428.0 8.2 %copy-start.1 = (bf16[256,4096]{1,0:T(8,128)(2,1)S(1)}, bf16[256,4096]{1,0:T(8,128)(2,1)}, u32[]{:S(2)}) copy-start(bf16[256,4096]{1,0:T(8,128)(2,1)} %param.14) | copy-start | bytes 6291460
Sparse Core Ops, SparseCore 0:
  25.4 48.5 all-gather.9
  78.1 44.7 all-gather.5
  124.9 52.9 all-gather.7
